TPU v7x, 256 devices: a whole 4x4x8 slice. The times are simulated.
256 devices in a mesh: leaf: 4 (over y), row: 8 (over z), col: 8 (over x, core).
Axes of the slice: x: 4, y: 4, z: 8, core: 2. Of those that a mesh axis runs over, the one named last changes fastest.
Arguments:
- rhs: float32 [4, 4, 8, 256, 256], P('leaf', None, 'row'), may hold values from -6 to 6
- rhs_top: float32 [2, 8, 256, 256], P(None, 'row'), may hold values from -6 to 6
- factor: bfloat16 [4, 4, 8, 4, 8, 256, 256], P('leaf', None, 'row', None, 'col'), may hold values from -0.125 to 0.125
- factor_inv: bfloat16 [4, 2, 4, 8, 256, 256], P('leaf', None, None, 'row')
- lower_bridge: bfloat16 [4, 2, 8, 4, 8, 256, 256], P('leaf', None, 'row', None, 'col'), may hold values from -0.0625 to 0.0625
- upper_bridge: bfloat16 [4, 4, 8, 2, 8, 256, 256], P('leaf', None, 'row', None, 'col'), may hold values from -0.1875 to 0.1875
- top_factor: bfloat16 [2, 8, 2, 8, 256, 256], P(None, 'row', None, 'col'), may hold values from -0.1875 to 0.1875
- top_inv: bfloat16 [2, 2, 8, 256, 256], P(None, None, 'row')
- widths: int32 [4, 4, 8], P('leaf', None, 'row'), may hold values from 128 to 256, as said below
- pattern: int32 [4, 4, 8, 4, 8], P('leaf', None, 'row', None, 'col'), may hold values 0 or 1
- lower_links: int32 [4, 2, 8, 4, 8], P('leaf', None, 'row', None, 'col'), may hold values 0 or 1
- upper_links: int32 [4, 4, 8, 2, 8], P('leaf', None, 'row', None, 'col'), may hold values 0 or 1
- top_pattern: int32 [2, 8, 2, 8], P(None, 'row', None, 'col'), may hold values 0 or 1
Outputs:
- solution: float32 [4, 4, 8, 256, 256], P('leaf', None, 'row', None, 'col')
- solution_top: float32 [2, 8, 256, 256], P(None, 'row', None, 'col')
Inputs may be any that keep to these rules, and one draw needn't show every extreme that they name: widths of supernodes; the largest is 256 in every subtree.
All inputs are finite; a program needn't handle non-finite values. No bound on the sum of `pattern` or of `lower_links` or of `upper_links` or of `top_pattern` on one device may be relied on, other than what follows from the above.
Results may differ from a plain program's by a relative error of at most 0.02.
Values may be sent and summed in bfloat16 or wider, within the bound.
No kernel may reach another device: no remote copies, remote signals or barrier semaphores. Data moves between devices by JAX's collectives and lax.ppermute only.
A program may use at most 64 MiB of HBM per device.

v0:
```python
import jax
import jax.numpy as jnp
from jax import lax
from jax.sharding import PartitionSpec as P

GRID = ("row", "col")


def masked(blocks, marks):
    return blocks * marks.astype(jnp.bfloat16)[..., None, None]


def ring_distance(a, b, size):
    d = abs(a - b) % size
    return min(d, size - d)


def to_columns(x, n):
    pairs = []
    for c in range(n):
        targets = sorted(range(n), key=lambda r: (-ring_distance(r, c, n), r))
        sources = sorted(range(n), key=lambda s: (ring_distance(s // 2, c // 2, n // 2), s % 2 != c % 2, s))
        pairs += [(c * n + s, r * n + c) for r, s in zip(targets, sources)]
    return lax.ppermute(x, GRID, pairs)


def tree_sum(parts):
    while len(parts) > 1:
        parts = [parts[i] + parts[i + 1] for i in range(0, len(parts), 2)]
    return parts[0]


def group_sum(x, axis, n, step=1):
    got = [x] + [lax.ppermute(x, axis, [(i, i ^ (step * k)) for i in range(n)]) for k in range(1, n // step)]
    return tree_sum(got)


def column_total(x, n, leaves=0):
    core = lax.axis_index("col") % 2
    half = x.shape[-1] // 2
    keep_half = lax.dynamic_slice_in_dim(x, core * half, half, x.ndim - 1)
    give_half = lax.dynamic_slice_in_dim(x, (1 - core) * half, half, x.ndim - 1)
    mine = keep_half + lax.ppermute(give_half, "col", [(i, i ^ 1) for i in range(n)])
    mine = group_sum(mine, "col", n, 2)
    if leaves:
        mine = group_sum(mine, "leaf", leaves)
    return mine


def join_halves(mine, n):
    core = lax.axis_index("col") % 2
    other = lax.ppermute(mine, "col", [(i, i ^ 1) for i in range(n)])
    first = jnp.where(core == 0, mine, other)
    second = jnp.where(core == 0, other, mine)
    return jnp.concatenate([first, second], mine.ndim - 1)


def own_half(x, ncol):
    chunk = x.shape[-1] // ncol
    lead = x.shape[:-1]
    x = x.reshape(lead + (ncol // 2, 2, chunk))
    x = jnp.moveaxis(x, -2, -3).reshape(lead + (x.shape[-1] * ncol,))
    half = x.shape[-1] // 2
    return lax.dynamic_slice_in_dim(x, (lax.axis_index("col") % 2) * half, half, x.ndim - 1)


def products(blocks, segments):
    return jnp.einsum(
        "jbk,jkr->br", jnp.stack(blocks, 0), jnp.stack(segments, 0), preferred_element_type=jnp.float32
    )


def shards(
    rhs,
    rhs_top,
    factor,
    factor_inv,
    lower_bridge,
    upper_bridge,
    top_factor,
    top_inv,
    widths,
    pattern,
    lower_links,
    upper_links,
    top_pattern,
):
    f32 = jnp.float32
    bf16 = jnp.bfloat16
    n = lax.axis_size("row")
    ncol = lax.axis_size("col")
    leaves = lax.axis_size("leaf")
    levels = factor.shape[1]
    tops = top_factor.shape[0]
    block = factor.shape[5]
    sides = rhs.shape[4]
    share = sides // ncol

    fm = masked(factor[0, :, 0, :, 0], pattern[0, :, 0, :, 0])
    lm = masked(lower_bridge[0, :, 0, :, 0], lower_links[0, :, 0, :, 0])
    um = masked(upper_bridge[0, :, 0, :, 0], upper_links[0, :, 0, :, 0])
    tm = masked(top_factor[:, 0, :, 0], top_pattern[:, 0, :, 0])
    marks = lax.broadcasted_iota(jnp.int32, (levels, block, 1), 1)
    keep = (marks < widths[0, :, 0][:, None, None]).astype(f32)
    own_rhs = own_half(rhs[0, :, 0], ncol)
    inv = factor_inv[0, :, :, 0]
    top_rhs = own_half(rhs_top[:, 0], ncol)
    tinv = top_inv[:, :, 0]

    ys = []
    segs = []
    for level in range(levels):
        if level == 0:
            resid = own_rhs[0].astype(bf16)
        else:
            part = products([fm[level, j] for j in range(level)], segs)
            resid = (own_rhs[level] - column_total(part, ncol)).astype(bf16)
        solved = keep[level] * jnp.dot(inv[0, level], resid, preferred_element_type=f32)
        ys.append(solved)
        segs.append(to_columns(join_halves(solved.astype(bf16), ncol), n))

    coupling = jnp.stack([products([lm[t, j] for j in range(levels)], segs) for t in range(tops)], 0)
    coupling = column_total(coupling, ncol, leaves)

    yts = []
    tsegs = []
    for top in range(tops):
        summed = coupling[top]
        if top > 0:
            part = products([tm[top, j] for j in range(top)], tsegs)
            summed = summed + column_total(part, ncol)
        resid = (top_rhs[top] - summed).astype(bf16)
        solved = jnp.dot(tinv[0, top], resid, preferred_element_type=f32)
        yts.append(solved)
        tsegs.append(to_columns(join_halves(solved.astype(bf16), ncol), n))

    zts = [None] * tops
    tback = [None] * tops
    for top in reversed(range(tops)):
        if top == tops - 1:
            resid = yts[top].astype(bf16)
        else:
            part = products([tm[top, j] for j in range(top + 1, tops)], tback[top + 1 :])
            resid = (yts[top] - column_total(part, ncol)).astype(bf16)
        solved = jnp.dot(tinv[1, top], resid, preferred_element_type=f32)
        zts[top] = solved
        tback[top] = to_columns(join_halves(solved.astype(bf16), ncol), n)

    zs = [None] * levels
    back = [None] * levels
    for level in reversed(range(levels)):
        blocks = [um[level, t] for t in range(tops)] + [fm[level, j] for j in range(level + 1, levels)]
        part = products(blocks, tback + back[level + 1 :])
        resid = (ys[level] - column_total(part, ncol)).astype(bf16)
        solved = keep[level] * jnp.dot(inv[1, level], resid, preferred_element_type=f32)
        zs[level] = solved
        if level > 0:
            back[level] = to_columns(join_halves(solved.astype(bf16), ncol), n)

    start = (lax.axis_index("col") // 2) * share
    result = lax.dynamic_slice_in_dim(jnp.stack(zs, 0), start, share, 2)
    result_top = lax.dynamic_slice_in_dim(jnp.stack(zts, 0), start, share, 2)
    return (result[None, :, None], result_top[:, None])


def solution(mesh):
    assert mesh.shape["row"] == mesh.shape["col"]
    placed = (
        P("leaf", None, "row", None, None),
        P(None, "row", None, None),
        P("leaf", None, "row", None, "col", None, None),
        P("leaf", None, None, "row", None, None),
        P("leaf", None, "row", None, "col", None, None),
        P("leaf", None, "row", None, "col", None, None),
        P(None, "row", None, "col", None, None),
        P(None, None, "row", None, None),
        P("leaf", None, "row"),
        P("leaf", None, "row", None, "col"),
        P("leaf", None, "row", None, "col"),
        P("leaf", None, "row", None, "col"),
        P(None, "row", None, "col"),
    )
    return jax.shard_map(
        shards,
        mesh=mesh,
        in_specs=placed,
        out_specs=(P("leaf", None, "row", None, "col"), P(None, "row", None, "col")),
        check_vma=False,
    )
```

profile of v0, /device:TPU:96, one launch (start us, length us, event | category | flops | bytes accessed | tf_op | source)
XLA Modules:
  0.0 322.7 jit_solution(15236341274094312995)
XLA Ops:
  6.0 4.4 %collective-permute-start.1 = (bf16[256,256]{0,1:T(8,128)(2,1)S(1)}, bf16[256,256]{0,1:T(8,128)(2,1)S(1)}, u32[]{:S(2)}, u32[]{:S(2)}) collective-permute-start(bf16[256,256]{0,1:T(8,128)(2,1)S(1)} %pad_maximum_fusion.1), channel_id=1, source_target_pairs={{0,32},{1,24},{2,40},{6,16},{3,48},{7,8},{4,56},{5,0},{9,41},{8,33... | collective-permute-start | bytes 393224 | tf_op jit(solution)/shard_map/ppermute | solution.py:24
  12.2 6.2 %collective-permute-done.1 = bf16[256,256]{0,1:T(8,128)(2,1)S(1)} collective-permute-done((bf16[256,256]{0,1:T(8,128)(2,1)S(1)}, bf16[256,256]{0,1:T(8,128)(2,1)S(1)}, u32[]{:S(2)}, u32[]{:S(2)}) %collective-permute-start.1) | collective-permute-done | bytes 131104 | tf_op jit(solution)/shard_map/ppermute | solution.py:24
  20.1 7.5 %collective-permute-start.4 = (f32[256,128]{1,0:T(8,128)S(1)}, f32[256,128]{1,0:T(8,128)S(1)}, u32[]{:S(2)}, u32[]{:S(2)}) collective-permute-start(f32[256,128]{1,0:T(8,128)S(1)} %dynamic-slice_add_fusion.8), channel_id=1, source_target_pairs={{0,4},{1,5},{2,6},{3,7},{4,0},{5,1},{6,2},{7,3},{8,12},{9,13},{10,... | collective-permute-start | bytes 393224 | tf_op jit(solution)/shard_map/ppermute | solution.py:34
  28.5 5.6 %collective-permute-done.4 = f32[256,128]{1,0:T(8,128)S(1)} collective-permute-done((f32[256,128]{1,0:T(8,128)S(1)}, f32[256,128]{1,0:T(8,128)S(1)}, u32[]{:S(2)}, u32[]{:S(2)}) %collective-permute-start.4) | collective-permute-done | bytes 131104 | tf_op jit(solution)/shard_map/ppermute | solution.py:34
  34.1 2.2 collective-permute-done.5
  39.8 6.4 %collective-permute-done.7 = bf16[256,256]{0,1:T(8,128)(2,1)S(1)} collective-permute-done((bf16[256,256]{0,1:T(8,128)(2,1)S(1)}, bf16[256,256]{0,1:T(8,128)(2,1)S(1)}, u32[]{:S(2)}, u32[]{:S(2)}) %collective-permute-start.7) | collective-permute-done | bytes 131104 | tf_op jit(solution)/shard_map/ppermute | solution.py:24
  50.5 4.0 %collective-permute-start.11 = (f32[256,128]{1,0:T(8,128)S(1)}, f32[256,128]{1,0:T(8,128)S(1)}, u32[]{:S(2)}, u32[]{:S(2)}) collective-permute-start(f32[256,128]{1,0:T(8,128)S(1)} %dynamic-slice_add_fusion.7), channel_id=1, source_target_pairs={{0,6},{1,7},{2,4},{3,5},{4,2},{5,3},{6,0},{7,1},{8,14},{9,15},{10,... | collective-permute-start | bytes 393224 | tf_op jit(solution)/shard_map/ppermute | solution.py:34
  57.6 2.9 collective-permute-done.11
  65.7 6.9 %collective-permute-done.13 = bf16[256,256]{0,1:T(8,128)(2,1)S(1)} collective-permute-done((bf16[256,256]{0,1:T(8,128)(2,1)S(1)}, bf16[256,256]{0,1:T(8,128)(2,1)S(1)}, u32[]{:S(2)}, u32[]{:S(2)}) %collective-permute-start.13) | collective-permute-done | bytes 131104 | tf_op jit(solution)/shard_map/ppermute | solution.py:24
  74.1 3.4 %collective-permute-start.14 = (f32[256,128]{1,0:T(8,128)S(1)}, f32[256,128]{1,0:T(8,128)S(1)}, u32[]{:S(2)}, u32[]{:S(2)}) collective-permute-start(f32[256,128]{1,0:T(8,128)S(1)} %constant_dynamic-slice_fusion.7), channel_id=1, source_target_pairs={{0,1},{1,0},{2,3},{3,2},{4,5},{5,4},{6,7},{7,6},{8,9},{9,8},{10,11... | collective-permute-start | bytes 393224 | tf_op jit(solution)/shard_map/ppermute | solution.py:43
  78.6 5.6 %collective-permute-start.16 = (f32[256,128]{1,0:T(8,128)S(1)}, f32[256,128]{1,0:T(8,128)}, u32[]{:S(2)}, u32[]{:S(2)}) collective-permute-start(f32[256,128]{1,0:T(8,128)S(1)} %dynamic-slice_add_fusion.6), channel_id=1, source_target_pairs={{0,4},{1,5},{2,6},{3,7},{4,0},{5,1},{6,2},{7,3},{8,12},{9,13},{10,... | collective-permute-start | bytes 393224 | tf_op jit(solution)/shard_map/ppermute | solution.py:34
  85.9 4.6 %collective-permute-done.16 = f32[256,128]{1,0:T(8,128)} collective-permute-done((f32[256,128]{1,0:T(8,128)S(1)}, f32[256,128]{1,0:T(8,128)}, u32[]{:S(2)}, u32[]{:S(2)}) %collective-permute-start.16) | collective-permute-done | bytes 131104 | tf_op jit(solution)/shard_map/ppermute | solution.py:34
  90.5 2.3 collective-permute-done.17
  96.3 7.5 %collective-permute-done.19 = bf16[256,256]{0,1:T(8,128)(2,1)S(1)} collective-permute-done((bf16[256,256]{0,1:T(8,128)(2,1)S(1)}, bf16[256,256]{0,1:T(8,128)(2,1)S(1)}, u32[]{:S(2)}, u32[]{:S(2)}) %collective-permute-start.19) | collective-permute-done | bytes 131104 | tf_op jit(solution)/shard_map/ppermute | solution.py:24
  107.9 4.6 %collective-permute-start.22 = (f32[2,256,128]{2,1,0:T(8,128)S(1)}, f32[2,256,128]{2,1,0:T(8,128)S(1)}, u32[]{:S(2)}, u32[]{:S(2)}) collective-permute-start(f32[2,256,128]{2,1,0:T(8,128)S(1)} %fusion.56), channel_id=1, source_target_pairs={{0,4},{1,5},{2,6},{3,7},{4,0},{5,1},{6,2},{7,3},{8,12},{9,13},{10,... | collective-permute-start | bytes 786440 | tf_op jit(solution)/shard_map/ppermute | solution.py:34
  112.6 4.5 %collective-permute-done.21 = f32[2,256,128]{2,1,0:T(8,128)S(1)} collective-permute-done((f32[2,256,128]{2,1,0:T(8,128)S(1)}, f32[2,256,128]{2,1,0:T(8,128)S(1)}, u32[]{:S(2)}, u32[]{:S(2)}) %collective-permute-start.21) | collective-permute-done | bytes 262176 | tf_op jit(solution)/shard_map/ppermute | solution.py:34
  117.0 7.4 %collective-permute-done.22 = f32[2,256,128]{2,1,0:T(8,128)S(1)} collective-permute-done((f32[2,256,128]{2,1,0:T(8,128)S(1)}, f32[2,256,128]{2,1,0:T(8,128)S(1)}, u32[]{:S(2)}, u32[]{:S(2)}) %collective-permute-start.22) | collective-permute-done | bytes 262176 | tf_op jit(solution)/shard_map/ppermute | solution.py:34
  124.5 2.6 collective-permute-done.23
  128.8 2.9 collective-permute-start.25
  133.0 3.6 %collective-permute-done.24 = f32[2,256,128]{2,1,0:T(8,128)} collective-permute-done((f32[2,256,128]{2,1,0:T(8,128)S(1)}, f32[2,256,128]{2,1,0:T(8,128)}, u32[]{:S(2)}, u32[]{:S(2)}) %collective-permute-start.24) | collective-permute-done | bytes 262176 | tf_op jit(solution)/shard_map/ppermute | solution.py:34
  136.5 5.9 %collective-permute-done.25 = f32[2,256,128]{2,1,0:T(8,128)} collective-permute-done((f32[2,256,128]{2,1,0:T(8,128)S(1)}, f32[2,256,128]{2,1,0:T(8,128)}, u32[]{:S(2)}, u32[]{:S(2)}) %collective-permute-start.25) | collective-permute-done | bytes 262176 | tf_op jit(solution)/shard_map/ppermute | solution.py:34
  142.4 2.6 collective-permute-done.26
  150.5 6.4 %collective-permute-done.28 = bf16[256,256]{0,1:T(8,128)(2,1)S(1)} collective-permute-done((bf16[256,256]{0,1:T(8,128)(2,1)S(1)}, bf16[256,256]{0,1:T(8,128)(2,1)S(1)}, u32[]{:S(2)}, u32[]{:S(2)}) %collective-permute-start.28) | collective-permute-done | bytes 131104 | tf_op jit(solution)/shard_map/ppermute | solution.py:24
  157.1 3.1 collective-permute-start.29
  161.3 4.9 %collective-permute-start.31 = (f32[256,128]{1,0:T(8,128)S(1)}, f32[256,128]{1,0:T(8,128)S(1)}, u32[]{:S(2)}, u32[]{:S(2)}) collective-permute-start(f32[256,128]{1,0:T(8,128)S(1)} %dynamic-slice_add_fusion.5), channel_id=1, source_target_pairs={{0,4},{1,5},{2,6},{3,7},{4,0},{5,1},{6,2},{7,3},{8,12},{9,13},{10,... | collective-permute-start | bytes 393224 | tf_op jit(solution)/shard_map/ppermute | solution.py:34
  167.6 4.9 %collective-permute-done.31 = f32[256,128]{1,0:T(8,128)S(1)} collective-permute-done((f32[256,128]{1,0:T(8,128)S(1)}, f32[256,128]{1,0:T(8,128)S(1)}, u32[]{:S(2)}, u32[]{:S(2)}) %collective-permute-start.31) | collective-permute-done | bytes 131104 | tf_op jit(solution)/shard_map/ppermute | solution.py:34
  177.8 9.0 %collective-permute-start.34 = (bf16[256,256]{0,1:T(8,128)(2,1)S(1)}, bf16[256,256]{0,1:T(8,128)(2,1)S(1)}, u32[]{:S(2)}, u32[]{:S(2)}) collective-permute-start(bf16[256,256]{0,1:T(8,128)(2,1)S(1)} %pad_maximum_fusion.6), channel_id=1, source_target_pairs={{0,32},{1,24},{2,40},{6,16},{3,48},{7,8},{4,56},{5,0},{9,41},{8,33... | collective-permute-start | bytes 393224 | tf_op jit(solution)/shard_map/ppermute | solution.py:24
  186.9 7.5 %collective-permute-done.34 = bf16[256,256]{0,1:T(8,128)(2,1)S(1)} collective-permute-done((bf16[256,256]{0,1:T(8,128)(2,1)S(1)}, bf16[256,256]{0,1:T(8,128)(2,1)S(1)}, u32[]{:S(2)}, u32[]{:S(2)}) %collective-permute-start.34) | collective-permute-done | bytes 131104 | tf_op jit(solution)/shard_map/ppermute | solution.py:24
  195.3 2.6 collective-permute-start.35
  199.0 4.2 %collective-permute-start.37 = (f32[256,128]{0,1:T(8,128)S(1)}, f32[256,128]{0,1:T(8,128)}, u32[]{:S(2)}, u32[]{:S(2)}) collective-permute-start(f32[256,128]{0,1:T(8,128)S(1)} %dynamic-slice_add_fusion.4), channel_id=1, source_target_pairs={{0,4},{1,5},{2,6},{3,7},{4,0},{5,1},{6,2},{7,3},{8,12},{9,13},{10,... | collective-permute-start | bytes 393224 | tf_op jit(solution)/shard_map/ppermute | solution.py:34
  206.3 3.5 %collective-permute-done.37 = f32[256,128]{0,1:T(8,128)} collective-permute-done((f32[256,128]{0,1:T(8,128)S(1)}, f32[256,128]{0,1:T(8,128)}, u32[]{:S(2)}, u32[]{:S(2)}) %collective-permute-start.37) | collective-permute-done | bytes 131104 | tf_op jit(solution)/shard_map/ppermute | solution.py:34
  209.8 2.2 collective-permute-done.38
  215.5 7.5 %collective-permute-done.40 = bf16[256,256]{0,1:T(8,128)(2,1)S(1)} collective-permute-done((bf16[256,256]{0,1:T(8,128)(2,1)S(1)}, bf16[256,256]{0,1:T(8,128)(2,1)S(1)}, u32[]{:S(2)}, u32[]{:S(2)}) %collective-permute-start.40) | collective-permute-done | bytes 131104 | tf_op jit(solution)/shard_map/ppermute | solution.py:24
  223.3 2.9 collective-permute-start.41
  227.3 4.7 %collective-permute-start.43 = (f32[256,128]{0,1:T(8,128)S(1)}, f32[256,128]{0,1:T(8,128)S(1)}, u32[]{:S(2)}, u32[]{:S(2)}) collective-permute-start(f32[256,128]{0,1:T(8,128)S(1)} %dynamic-slice_add_fusion.3), channel_id=1, source_target_pairs={{0,4},{1,5},{2,6},{3,7},{4,0},{5,1},{6,2},{7,3},{8,12},{9,13},{10,... | collective-permute-start | bytes 393224 | tf_op jit(solution)/shard_map/ppermute | solution.py:34
  233.7 4.8 %collective-permute-done.43 = f32[256,128]{0,1:T(8,128)S(1)} collective-permute-done((f32[256,128]{0,1:T(8,128)S(1)}, f32[256,128]{0,1:T(8,128)S(1)}, u32[]{:S(2)}, u32[]{:S(2)}) %collective-permute-start.43) | collective-permute-done | bytes 131104 | tf_op jit(solution)/shard_map/ppermute | solution.py:34
  242.9 7.5 %collective-permute-done.46 = bf16[256,256]{0,1:T(8,128)(2,1)S(1)} collective-permute-done((bf16[256,256]{0,1:T(8,128)(2,1)S(1)}, bf16[256,256]{0,1:T(8,128)(2,1)S(1)}, u32[]{:S(2)}, u32[]{:S(2)}) %collective-permute-start.46) | collective-permute-done | bytes 131104 | tf_op jit(solution)/shard_map/ppermute | solution.py:24
  250.8 2.7 collective-permute-start.47
  254.6 4.2 %collective-permute-start.49 = (f32[256,128]{0,1:T(8,128)S(1)}, f32[256,128]{0,1:T(8,128)S(1)}, u32[]{:S(2)}, u32[]{:S(2)}) collective-permute-start(f32[256,128]{0,1:T(8,128)S(1)} %dynamic-slice_add_fusion.2), channel_id=1, source_target_pairs={{0,4},{1,5},{2,6},{3,7},{4,0},{5,1},{6,2},{7,3},{8,12},{9,13},{10,... | collective-permute-start | bytes 393224 | tf_op jit(solution)/shard_map/ppermute | solution.py:34
  261.0 4.2 %collective-permute-done.49 = f32[256,128]{0,1:T(8,128)S(1)} collective-permute-done((f32[256,128]{0,1:T(8,128)S(1)}, f32[256,128]{0,1:T(8,128)S(1)}, u32[]{:S(2)}, u32[]{:S(2)}) %collective-permute-start.49) | collective-permute-done | bytes 131104 | tf_op jit(solution)/shard_map/ppermute | solution.py:34
  269.9 7.5 %collective-permute-done.52 = bf16[256,256]{0,1:T(8,128)(2,1)S(1)} collective-permute-done((bf16[256,256]{0,1:T(8,128)(2,1)S(1)}, bf16[256,256]{0,1:T(8,128)(2,1)S(1)}, u32[]{:S(2)}, u32[]{:S(2)}) %collective-permute-start.52) | collective-permute-done | bytes 131104 | tf_op jit(solution)/shard_map/ppermute | solution.py:24
  277.9 3.3 %collective-permute-start.53 = (f32[256,128]{0,1:T(8,128)S(1)}, f32[256,128]{0,1:T(8,128)S(1)}, u32[]{:S(2)}, u32[]{:S(2)}) collective-permute-start(f32[256,128]{0,1:T(8,128)S(1)} %constant_dynamic-slice_fusion.2), channel_id=1, source_target_pairs={{0,1},{1,0},{2,3},{3,2},{4,5},{5,4},{6,7},{7,6},{8,9},{9,8},{10,11... | collective-permute-start | bytes 393224 | tf_op jit(solution)/shard_map/ppermute | solution.py:43
  282.2 4.3 %collective-permute-start.55 = (f32[256,128]{0,1:T(8,128)S(1)}, f32[256,128]{0,1:T(8,128)S(1)}, u32[]{:S(2)}, u32[]{:S(2)}) collective-permute-start(f32[256,128]{0,1:T(8,128)S(1)} %dynamic-slice_add_fusion.1), channel_id=1, source_target_pairs={{0,4},{1,5},{2,6},{3,7},{4,0},{5,1},{6,2},{7,3},{8,12},{9,13},{10,... | collective-permute-start | bytes 393224 | tf_op jit(solution)/shard_map/ppermute | solution.py:34
  288.6 4.4 %collective-permute-done.55 = f32[256,128]{0,1:T(8,128)S(1)} collective-permute-done((f32[256,128]{0,1:T(8,128)S(1)}, f32[256,128]{0,1:T(8,128)S(1)}, u32[]{:S(2)}, u32[]{:S(2)}) %collective-permute-start.55) | collective-permute-done | bytes 131104 | tf_op jit(solution)/shard_map/ppermute | solution.py:34
  297.0 7.5 %collective-permute-done.58 = bf16[256,256]{0,1:T(8,128)(2,1)S(1)} collective-permute-done((bf16[256,256]{0,1:T(8,128)(2,1)S(1)}, bf16[256,256]{0,1:T(8,128)(2,1)S(1)}, u32[]{:S(2)}, u32[]{:S(2)}) %collective-permute-start.58) | collective-permute-done | bytes 131104 | tf_op jit(solution)/shard_map/ppermute | solution.py:24
  304.9 2.9 collective-permute-start.59
  308.9 4.0 %collective-permute-start.61 = (f32[256,128]{0,1:T(8,128)S(1)}, f32[256,128]{0,1:T(8,128)S(1)}, u32[]{:S(2)}, u32[]{:S(2)}) collective-permute-start(f32[256,128]{0,1:T(8,128)S(1)} %dynamic-slice_add_fusion), channel_id=1, source_target_pairs={{0,4},{1,5},{2,6},{3,7},{4,0},{5,1},{6,2},{7,3},{8,12},{9,13},{10,... | collective-permute-start | bytes 393224 | tf_op jit(solution)/shard_map/ppermute | solution.py:34
  315.3 4.1 %collective-permute-done.61 = f32[256,128]{0,1:T(8,128)S(1)} collective-permute-done((f32[256,128]{0,1:T(8,128)S(1)}, f32[256,128]{0,1:T(8,128)S(1)}, u32[]{:S(2)}, u32[]{:S(2)}) %collective-permute-start.61) | collective-permute-done | bytes 131104 | tf_op jit(solution)/shard_map/ppermute | solution.py:34
  (235 shorter events, 92.3 us)
Async XLA Ops:
  6.0 12.3 %collective-permute-start.1 = (bf16[256,256]{0,1:T(8,128)(2,1)S(1)}, bf16[256,256]{0,1:T(8,128)(2,1)S(1)}, u32[]{:S(2)}, u32[]{:S(2)}) collective-permute-start(bf16[256,256]{0,1:T(8,128)(2,1)S(1)} %pad_maximum_fusion.1), channel_id=1, source_target_pairs={{0,32},{1,24},{2,40},{6,16},{3,48},{7,8},{4,56},{5,0},{9,41},{8,33... | collective-permute-start | bytes 393224 | tf_op jit(solution)/shard_map/ppermute | solution.py:24
  20.0 8.4 %collective-permute-start.3 = (f32[256,128]{1,0:T(8,128)S(1)}, f32[256,128]{1,0:T(8,128)S(1)}, u32[]{:S(2)}, u32[]{:S(2)}) collective-permute-start(f32[256,128]{1,0:T(8,128)S(1)} %dynamic-slice_add_fusion.8), channel_id=1, source_target_pairs={{0,2},{1,3},{2,0},{3,1},{4,6},{5,7},{6,4},{7,5},{8,10},{9,11},{10,... | collective-permute-start | bytes 393224 | tf_op jit(solution)/shard_map/ppermute | solution.py:34
  20.1 14.0 %collective-permute-start.4 = (f32[256,128]{1,0:T(8,128)S(1)}, f32[256,128]{1,0:T(8,128)S(1)}, u32[]{:S(2)}, u32[]{:S(2)}) collective-permute-start(f32[256,128]{1,0:T(8,128)S(1)} %dynamic-slice_add_fusion.8), channel_id=1, source_target_pairs={{0,4},{1,5},{2,6},{3,7},{4,0},{5,1},{6,2},{7,3},{8,12},{9,13},{10,... | collective-permute-start | bytes 393224 | tf_op jit(solution)/shard_map/ppermute | solution.py:34
  27.7 8.7 %collective-permute-start.5 = (f32[256,128]{1,0:T(8,128)S(1)}, f32[256,128]{1,0:T(8,128)S(1)}, u32[]{:S(2)}, u32[]{:S(2)}) collective-permute-start(f32[256,128]{1,0:T(8,128)S(1)} %dynamic-slice_add_fusion.8), channel_id=1, source_target_pairs={{0,6},{1,7},{2,4},{3,5},{4,2},{5,3},{6,0},{7,1},{8,14},{9,15},{10,... | collective-permute-start | bytes 393224 | tf_op jit(solution)/shard_map/ppermute | solution.py:34
  38.8 7.3 %collective-permute-start.7 = (bf16[256,256]{0,1:T(8,128)(2,1)S(1)}, bf16[256,256]{0,1:T(8,128)(2,1)S(1)}, u32[]{:S(2)}, u32[]{:S(2)}) collective-permute-start(bf16[256,256]{0,1:T(8,128)(2,1)S(1)} %pad_maximum_fusion.2), channel_id=1, source_target_pairs={{0,32},{1,24},{2,40},{6,16},{3,48},{7,8},{4,56},{5,0},{9,41},{8,33... | collective-permute-start | bytes 393224 | tf_op jit(solution)/shard_map/ppermute | solution.py:24
  50.1 7.5 %collective-permute-start.10 = (f32[256,128]{1,0:T(8,128)S(1)}, f32[256,128]{1,0:T(8,128)S(1)}, u32[]{:S(2)}, u32[]{:S(2)}) collective-permute-start(f32[256,128]{1,0:T(8,128)S(1)} %dynamic-slice_add_fusion.7), channel_id=1, source_target_pairs={{0,4},{1,5},{2,6},{3,7},{4,0},{5,1},{6,2},{7,3},{8,12},{9,13},{10,... | collective-permute-start | bytes 393224 | tf_op jit(solution)/shard_map/ppermute | solution.py:34
  50.5 9.9 %collective-permute-start.11 = (f32[256,128]{1,0:T(8,128)S(1)}, f32[256,128]{1,0:T(8,128)S(1)}, u32[]{:S(2)}, u32[]{:S(2)}) collective-permute-start(f32[256,128]{1,0:T(8,128)S(1)} %dynamic-slice_add_fusion.7), channel_id=1, source_target_pairs={{0,6},{1,7},{2,4},{3,5},{4,2},{5,3},{6,0},{7,1},{8,14},{9,15},{10,... | collective-permute-start | bytes 393224 | tf_op jit(solution)/shard_map/ppermute | solution.py:34
  54.6 7.1 %collective-permute-start.9 = (f32[256,128]{1,0:T(8,128)S(1)}, f32[256,128]{1,0:T(8,128)S(1)}, u32[]{:S(2)}, u32[]{:S(2)}) collective-permute-start(f32[256,128]{1,0:T(8,128)S(1)} %dynamic-slice_add_fusion.7), channel_id=1, source_target_pairs={{0,2},{1,3},{2,0},{3,1},{4,6},{5,7},{6,4},{7,5},{8,10},{9,11},{10,... | collective-permute-start | bytes 393224 | tf_op jit(solution)/shard_map/ppermute | solution.py:34
  64.8 7.8 %collective-permute-start.13 = (bf16[256,256]{0,1:T(8,128)(2,1)S(1)}, bf16[256,256]{0,1:T(8,128)(2,1)S(1)}, u32[]{:S(2)}, u32[]{:S(2)}) collective-permute-start(bf16[256,256]{0,1:T(8,128)(2,1)S(1)} %pad_maximum_fusion.3), channel_id=1, source_target_pairs={{0,32},{1,24},{2,40},{6,16},{3,48},{7,8},{4,56},{5,0},{9,41},{8,33... | collective-permute-start | bytes 393224 | tf_op jit(solution)/shard_map/ppermute | solution.py:24
  74.1 4.4 %collective-permute-start.14 = (f32[256,128]{1,0:T(8,128)S(1)}, f32[256,128]{1,0:T(8,128)S(1)}, u32[]{:S(2)}, u32[]{:S(2)}) collective-permute-start(f32[256,128]{1,0:T(8,128)S(1)} %constant_dynamic-slice_fusion.7), channel_id=1, source_target_pairs={{0,1},{1,0},{2,3},{3,2},{4,5},{5,4},{6,7},{7,6},{8,9},{9,8},{10,11... | collective-permute-start | bytes 393224 | tf_op jit(solution)/shard_map/ppermute | solution.py:43
  78.5 7.4 %collective-permute-start.15 = (f32[256,128]{1,0:T(8,128)S(1)}, f32[256,128]{1,0:T(8,128)}, u32[]{:S(2)}, u32[]{:S(2)}) collective-permute-start(f32[256,128]{1,0:T(8,128)S(1)} %dynamic-slice_add_fusion.6), channel_id=1, source_target_pairs={{0,2},{1,3},{2,0},{3,1},{4,6},{5,7},{6,4},{7,5},{8,10},{9,11},{10,... | collective-permute-start | bytes 393224 | tf_op jit(solution)/shard_map/ppermute | solution.py:34
  78.6 11.9 %collective-permute-start.16 = (f32[256,128]{1,0:T(8,128)S(1)}, f32[256,128]{1,0:T(8,128)}, u32[]{:S(2)}, u32[]{:S(2)}) collective-permute-start(f32[256,128]{1,0:T(8,128)S(1)} %dynamic-slice_add_fusion.6), channel_id=1, source_target_pairs={{0,4},{1,5},{2,6},{3,7},{4,0},{5,1},{6,2},{7,3},{8,12},{9,13},{10,... | collective-permute-start | bytes 393224 | tf_op jit(solution)/shard_map/ppermute | solution.py:34
  84.2 8.7 %collective-permute-start.17 = (f32[256,128]{1,0:T(8,128)S(1)}, f32[256,128]{1,0:T(8,128)}, u32[]{:S(2)}, u32[]{:S(2)}) collective-permute-start(f32[256,128]{1,0:T(8,128)S(1)} %dynamic-slice_add_fusion.6), channel_id=1, source_target_pairs={{0,6},{1,7},{2,4},{3,5},{4,2},{5,3},{6,0},{7,1},{8,14},{9,15},{10,... | collective-permute-start | bytes 393224 | tf_op jit(solution)/shard_map/ppermute | solution.py:34
  96.1 7.6 %collective-permute-start.19 = (bf16[256,256]{0,1:T(8,128)(2,1)S(1)}, bf16[256,256]{0,1:T(8,128)(2,1)S(1)}, u32[]{:S(2)}, u32[]{:S(2)}) collective-permute-start(bf16[256,256]{0,1:T(8,128)(2,1)S(1)} %pad_maximum_fusion.4), channel_id=1, source_target_pairs={{0,32},{1,24},{2,40},{6,16},{3,48},{7,8},{4,56},{5,0},{9,41},{8,33... | collective-permute-start | bytes 393224 | tf_op jit(solution)/shard_map/ppermute | solution.py:24
  107.8 9.3 %collective-permute-start.21 = (f32[2,256,128]{2,1,0:T(8,128)S(1)}, f32[2,256,128]{2,1,0:T(8,128)S(1)}, u32[]{:S(2)}, u32[]{:S(2)}) collective-permute-start(f32[2,256,128]{2,1,0:T(8,128)S(1)} %fusion.56), channel_id=1, source_target_pairs={{0,2},{1,3},{2,0},{3,1},{4,6},{5,7},{6,4},{7,5},{8,10},{9,11},{10,... | collective-permute-start | bytes 786440 | tf_op jit(solution)/shard_map/ppermute | solution.py:34
  107.9 16.6 %collective-permute-start.22 = (f32[2,256,128]{2,1,0:T(8,128)S(1)}, f32[2,256,128]{2,1,0:T(8,128)S(1)}, u32[]{:S(2)}, u32[]{:S(2)}) collective-permute-start(f32[2,256,128]{2,1,0:T(8,128)S(1)} %fusion.56), channel_id=1, source_target_pairs={{0,4},{1,5},{2,6},{3,7},{4,0},{5,1},{6,2},{7,3},{8,12},{9,13},{10,... | collective-permute-start | bytes 786440 | tf_op jit(solution)/shard_map/ppermute | solution.py:34
  112.4 14.6 %collective-permute-start.23 = (f32[2,256,128]{2,1,0:T(8,128)S(1)}, f32[2,256,128]{2,1,0:T(8,128)S(1)}, u32[]{:S(2)}, u32[]{:S(2)}) collective-permute-start(f32[2,256,128]{2,1,0:T(8,128)S(1)} %fusion.56), channel_id=1, source_target_pairs={{0,6},{1,7},{2,4},{3,5},{4,2},{5,3},{6,0},{7,1},{8,14},{9,15},{10,... | collective-permute-start | bytes 786440 | tf_op jit(solution)/shard_map/ppermute | solution.py:34
  127.1 9.4 %collective-permute-start.24 = (f32[2,256,128]{2,1,0:T(8,128)S(1)}, f32[2,256,128]{2,1,0:T(8,128)}, u32[]{:S(2)}, u32[]{:S(2)}) collective-permute-start(f32[2,256,128]{2,1,0:T(8,128)S(1)} %add_add_fusion.1), channel_id=1, source_target_pairs={{0,64},{64,0},{128,192},{192,128},{1,65},{65,1},{129,193},{193,129... | collective-permute-start | bytes 786440 | tf_op jit(solution)/shard_map/ppermute | solution.py:34
  128.8 13.6 %collective-permute-start.25 = (f32[2,256,128]{2,1,0:T(8,128)S(1)}, f32[2,256,128]{2,1,0:T(8,128)}, u32[]{:S(2)}, u32[]{:S(2)}) collective-permute-start(f32[2,256,128]{2,1,0:T(8,128)S(1)} %add_add_fusion.1), channel_id=1, source_target_pairs={{0,128},{64,192},{128,0},{192,64},{1,129},{65,193},{129,1},{193,65... | collective-permute-start | bytes 786440 | tf_op jit(solution)/shard_map/ppermute | solution.py:34
  131.7 13.3 %collective-permute-start.26 = (f32[2,256,128]{2,1,0:T(8,128)S(1)}, f32[2,256,128]{2,1,0:T(8,128)}, u32[]{:S(2)}, u32[]{:S(2)}) collective-permute-start(f32[2,256,128]{2,1,0:T(8,128)S(1)} %add_add_fusion.1), channel_id=1, source_target_pairs={{0,192},{64,128},{128,64},{192,0},{1,193},{65,129},{129,65},{193,1... | collective-permute-start | bytes 786440 | tf_op jit(solution)/shard_map/ppermute | solution.py:34
  149.2 7.6 %collective-permute-start.28 = (bf16[256,256]{0,1:T(8,128)(2,1)S(1)}, bf16[256,256]{0,1:T(8,128)(2,1)S(1)}, u32[]{:S(2)}, u32[]{:S(2)}) collective-permute-start(bf16[256,256]{0,1:T(8,128)(2,1)S(1)} %pad_maximum_fusion.5), channel_id=1, source_target_pairs={{0,32},{1,24},{2,40},{6,16},{3,48},{7,8},{4,56},{5,0},{9,41},{8,33... | collective-permute-start | bytes 393224 | tf_op jit(solution)/shard_map/ppermute | solution.py:24
  157.1 4.1 %collective-permute-start.29 = (f32[256,128]{1,0:T(8,128)S(1)}, f32[256,128]{1,0:T(8,128)S(1)}, u32[]{:S(2)}, u32[]{:S(2)}) collective-permute-start(f32[256,128]{1,0:T(8,128)S(1)} %constant_dynamic-slice_fusion.6), channel_id=1, source_target_pairs={{0,1},{1,0},{2,3},{3,2},{4,5},{5,4},{6,7},{7,6},{8,9},{9,8},{10,11... | collective-permute-start | bytes 393224 | tf_op jit(solution)/shard_map/ppermute | solution.py:43
  161.2 6.5 %collective-permute-start.30 = (f32[256,128]{1,0:T(8,128)S(1)}, f32[256,128]{1,0:T(8,128)S(1)}, u32[]{:S(2)}, u32[]{:S(2)}) collective-permute-start(f32[256,128]{1,0:T(8,128)S(1)} %dynamic-slice_add_fusion.5), channel_id=1, source_target_pairs={{0,2},{1,3},{2,0},{3,1},{4,6},{5,7},{6,4},{7,5},{8,10},{9,11},{10,... | collective-permute-start | bytes 393224 | tf_op jit(solution)/shard_map/ppermute | solution.py:34
  161.3 11.3 %collective-permute-start.31 = (f32[256,128]{1,0:T(8,128)S(1)}, f32[256,128]{1,0:T(8,128)S(1)}, u32[]{:S(2)}, u32[]{:S(2)}) collective-permute-start(f32[256,128]{1,0:T(8,128)S(1)} %dynamic-slice_add_fusion.5), channel_id=1, source_target_pairs={{0,4},{1,5},{2,6},{3,7},{4,0},{5,1},{6,2},{7,3},{8,12},{9,13},{10,... | collective-permute-start | bytes 393224 | tf_op jit(solution)/shard_map/ppermute | solution.py:34
  166.1 8.8 %collective-permute-start.32 = (f32[256,128]{1,0:T(8,128)S(1)}, f32[256,128]{1,0:T(8,128)}, u32[]{:S(2)}, u32[]{:S(2)}) collective-permute-start(f32[256,128]{1,0:T(8,128)S(1)} %dynamic-slice_add_fusion.5), channel_id=1, source_target_pairs={{0,6},{1,7},{2,4},{3,5},{4,2},{5,3},{6,0},{7,1},{8,14},{9,15},{10,... | collective-permute-start | bytes 393224 | tf_op jit(solution)/shard_map/ppermute | solution.py:34
  177.8 16.6 %collective-permute-start.34 = (bf16[256,256]{0,1:T(8,128)(2,1)S(1)}, bf16[256,256]{0,1:T(8,128)(2,1)S(1)}, u32[]{:S(2)}, u32[]{:S(2)}) collective-permute-start(bf16[256,256]{0,1:T(8,128)(2,1)S(1)} %pad_maximum_fusion.6), channel_id=1, source_target_pairs={{0,32},{1,24},{2,40},{6,16},{3,48},{7,8},{4,56},{5,0},{9,41},{8,33... | collective-permute-start | bytes 393224 | tf_op jit(solution)/shard_map/ppermute | solution.py:24
  198.9 7.4 %collective-permute-start.36 = (f32[256,128]{0,1:T(8,128)S(1)}, f32[256,128]{0,1:T(8,128)}, u32[]{:S(2)}, u32[]{:S(2)}) collective-permute-start(f32[256,128]{0,1:T(8,128)S(1)} %dynamic-slice_add_fusion.4), channel_id=1, source_target_pairs={{0,2},{1,3},{2,0},{3,1},{4,6},{5,7},{6,4},{7,5},{8,10},{9,11},{10,... | collective-permute-start | bytes 393224 | tf_op jit(solution)/shard_map/ppermute | solution.py:34
  199.0 10.8 %collective-permute-start.37 = (f32[256,128]{0,1:T(8,128)S(1)}, f32[256,128]{0,1:T(8,128)}, u32[]{:S(2)}, u32[]{:S(2)}) collective-permute-start(f32[256,128]{0,1:T(8,128)S(1)} %dynamic-slice_add_fusion.4), channel_id=1, source_target_pairs={{0,4},{1,5},{2,6},{3,7},{4,0},{5,1},{6,2},{7,3},{8,12},{9,13},{10,... | collective-permute-start | bytes 393224 | tf_op jit(solution)/shard_map/ppermute | solution.py:34
  203.3 8.8 %collective-permute-start.38 = (f32[256,128]{0,1:T(8,128)S(1)}, f32[256,128]{0,1:T(8,128)}, u32[]{:S(2)}, u32[]{:S(2)}) collective-permute-start(f32[256,128]{0,1:T(8,128)S(1)} %dynamic-slice_add_fusion.4), channel_id=1, source_target_pairs={{0,6},{1,7},{2,4},{3,5},{4,2},{5,3},{6,0},{7,1},{8,14},{9,15},{10,... | collective-permute-start | bytes 393224 | tf_op jit(solution)/shard_map/ppermute | solution.py:34
  215.3 7.6 %collective-permute-start.40 = (bf16[256,256]{0,1:T(8,128)(2,1)S(1)}, bf16[256,256]{0,1:T(8,128)(2,1)S(1)}, u32[]{:S(2)}, u32[]{:S(2)}) collective-permute-start(bf16[256,256]{0,1:T(8,128)(2,1)S(1)} %pad_maximum_fusion.7), channel_id=1, source_target_pairs={{0,32},{1,24},{2,40},{6,16},{3,48},{7,8},{4,56},{5,0},{9,41},{8,33... | collective-permute-start | bytes 393224 | tf_op jit(solution)/shard_map/ppermute | solution.py:24
  223.3 3.9 %collective-permute-start.41 = (f32[256,128]{0,1:T(8,128)S(1)}, f32[256,128]{0,1:T(8,128)S(1)}, u32[]{:S(2)}, u32[]{:S(2)}) collective-permute-start(f32[256,128]{0,1:T(8,128)S(1)} %constant_dynamic-slice_fusion.4), channel_id=1, source_target_pairs={{0,1},{1,0},{2,3},{3,2},{4,5},{5,4},{6,7},{7,6},{8,9},{9,8},{10,11... | collective-permute-start | bytes 393224 | tf_op jit(solution)/shard_map/ppermute | solution.py:43
  227.2 6.5 %collective-permute-start.42 = (f32[256,128]{0,1:T(8,128)S(1)}, f32[256,128]{0,1:T(8,128)S(1)}, u32[]{:S(2)}, u32[]{:S(2)}) collective-permute-start(f32[256,128]{0,1:T(8,128)S(1)} %dynamic-slice_add_fusion.3), channel_id=1, source_target_pairs={{0,2},{1,3},{2,0},{3,1},{4,6},{5,7},{6,4},{7,5},{8,10},{9,11},{10,... | collective-permute-start | bytes 393224 | tf_op jit(solution)/shard_map/ppermute | solution.py:34
  227.3 11.1 %collective-permute-start.43 = (f32[256,128]{0,1:T(8,128)S(1)}, f32[256,128]{0,1:T(8,128)S(1)}, u32[]{:S(2)}, u32[]{:S(2)}) collective-permute-start(f32[256,128]{0,1:T(8,128)S(1)} %dynamic-slice_add_fusion.3), channel_id=1, source_target_pairs={{0,4},{1,5},{2,6},{3,7},{4,0},{5,1},{6,2},{7,3},{8,12},{9,13},{10,... | collective-permute-start | bytes 393224 | tf_op jit(solution)/shard_map/ppermute | solution.py:34
  232.0 8.7 %collective-permute-start.44 = (f32[256,128]{0,1:T(8,128)S(1)}, f32[256,128]{0,1:T(8,128)S(1)}, u32[]{:S(2)}, u32[]{:S(2)}) collective-permute-start(f32[256,128]{0,1:T(8,128)S(1)} %dynamic-slice_add_fusion.3), channel_id=1, source_target_pairs={{0,6},{1,7},{2,4},{3,5},{4,2},{5,3},{6,0},{7,1},{8,14},{9,15},{10,... | collective-permute-start | bytes 393224 | tf_op jit(solution)/shard_map/ppermute | solution.py:34
  242.8 7.6 %collective-permute-start.46 = (bf16[256,256]{0,1:T(8,128)(2,1)S(1)}, bf16[256,256]{0,1:T(8,128)(2,1)S(1)}, u32[]{:S(2)}, u32[]{:S(2)}) collective-permute-start(bf16[256,256]{0,1:T(8,128)(2,1)S(1)} %pad_maximum_fusion.8), channel_id=1, source_target_pairs={{0,32},{1,24},{2,40},{6,16},{3,48},{7,8},{4,56},{5,0},{9,41},{8,33... | collective-permute-start | bytes 393224 | tf_op jit(solution)/shard_map/ppermute | solution.py:24
  254.5 6.5 %collective-permute-start.48 = (f32[256,128]{0,1:T(8,128)S(1)}, f32[256,128]{0,1:T(8,128)S(1)}, u32[]{:S(2)}, u32[]{:S(2)}) collective-permute-start(f32[256,128]{0,1:T(8,128)S(1)} %dynamic-slice_add_fusion.2), channel_id=1, source_target_pairs={{0,2},{1,3},{2,0},{3,1},{4,6},{5,7},{6,4},{7,5},{8,10},{9,11},{10,... | collective-permute-start | bytes 393224 | tf_op jit(solution)/shard_map/ppermute | solution.py:34
  254.6 10.6 %collective-permute-start.49 = (f32[256,128]{0,1:T(8,128)S(1)}, f32[256,128]{0,1:T(8,128)S(1)}, u32[]{:S(2)}, u32[]{:S(2)}) collective-permute-start(f32[256,128]{0,1:T(8,128)S(1)} %dynamic-slice_add_fusion.2), channel_id=1, source_target_pairs={{0,4},{1,5},{2,6},{3,7},{4,0},{5,1},{6,2},{7,3},{8,12},{9,13},{10,... | collective-permute-start | bytes 393224 | tf_op jit(solution)/shard_map/ppermute | solution.py:34
  258.8 8.7 %collective-permute-start.50 = (f32[256,128]{0,1:T(8,128)S(1)}, f32[256,128]{0,1:T(8,128)S(1)}, u32[]{:S(2)}, u32[]{:S(2)}) collective-permute-start(f32[256,128]{0,1:T(8,128)S(1)} %dynamic-slice_add_fusion.2), channel_id=1, source_target_pairs={{0,6},{1,7},{2,4},{3,5},{4,2},{5,3},{6,0},{7,1},{8,14},{9,15},{10,... | collective-permute-start | bytes 393224 | tf_op jit(solution)/shard_map/ppermute | solution.py:34
  269.6 7.9 %collective-permute-start.52 = (bf16[256,256]{0,1:T(8,128)(2,1)S(1)}, bf16[256,256]{0,1:T(8,128)(2,1)S(1)}, u32[]{:S(2)}, u32[]{:S(2)}) collective-permute-start(bf16[256,256]{0,1:T(8,128)(2,1)S(1)} %pad_maximum_fusion.9), channel_id=1, source_target_pairs={{0,32},{1,24},{2,40},{6,16},{3,48},{7,8},{4,56},{5,0},{9,41},{8,33... | collective-permute-start | bytes 393224 | tf_op jit(solution)/shard_map/ppermute | solution.py:24
  277.9 4.2 %collective-permute-start.53 = (f32[256,128]{0,1:T(8,128)S(1)}, f32[256,128]{0,1:T(8,128)S(1)}, u32[]{:S(2)}, u32[]{:S(2)}) collective-permute-start(f32[256,128]{0,1:T(8,128)S(1)} %constant_dynamic-slice_fusion.2), channel_id=1, source_target_pairs={{0,1},{1,0},{2,3},{3,2},{4,5},{5,4},{6,7},{7,6},{8,9},{9,8},{10,11... | collective-permute-start | bytes 393224 | tf_op jit(solution)/shard_map/ppermute | solution.py:43
  282.1 6.5 %collective-permute-start.54 = (f32[256,128]{0,1:T(8,128)S(1)}, f32[256,128]{0,1:T(8,128)S(1)}, u32[]{:S(2)}, u32[]{:S(2)}) collective-permute-start(f32[256,128]{0,1:T(8,128)S(1)} %dynamic-slice_add_fusion.1), channel_id=1, source_target_pairs={{0,2},{1,3},{2,0},{3,1},{4,6},{5,7},{6,4},{7,5},{8,10},{9,11},{10,... | collective-permute-start | bytes 393224 | tf_op jit(solution)/shard_map/ppermute | solution.py:34
  282.2 10.8 %collective-permute-start.55 = (f32[256,128]{0,1:T(8,128)S(1)}, f32[256,128]{0,1:T(8,128)S(1)}, u32[]{:S(2)}, u32[]{:S(2)}) collective-permute-start(f32[256,128]{0,1:T(8,128)S(1)} %dynamic-slice_add_fusion.1), channel_id=1, source_target_pairs={{0,4},{1,5},{2,6},{3,7},{4,0},{5,1},{6,2},{7,3},{8,12},{9,13},{10,... | collective-permute-start | bytes 393224 | tf_op jit(solution)/shard_map/ppermute | solution.py:34
  286.6 8.7 %collective-permute-start.56 = (f32[256,128]{0,1:T(8,128)S(1)}, f32[256,128]{0,1:T(8,128)S(1)}, u32[]{:S(2)}, u32[]{:S(2)}) collective-permute-start(f32[256,128]{0,1:T(8,128)S(1)} %dynamic-slice_add_fusion.1), channel_id=1, source_target_pairs={{0,6},{1,7},{2,4},{3,5},{4,2},{5,3},{6,0},{7,1},{8,14},{9,15},{10,... | collective-permute-start | bytes 393224 | tf_op jit(solution)/shard_map/ppermute | solution.py:34
  296.8 7.7 %collective-permute-start.58 = (bf16[256,256]{0,1:T(8,128)(2,1)S(1)}, bf16[256,256]{0,1:T(8,128)(2,1)S(1)}, u32[]{:S(2)}, u32[]{:S(2)}) collective-permute-start(bf16[256,256]{0,1:T(8,128)(2,1)S(1)} %pad_maximum_fusion.10), channel_id=1, source_target_pairs={{0,32},{1,24},{2,40},{6,16},{3,48},{7,8},{4,56},{5,0},{9,41},{8,33... | collective-permute-start | bytes 393224 | tf_op jit(solution)/shard_map/ppermute | solution.py:24
  304.9 3.9 %collective-permute-start.59 = (f32[256,128]{0,1:T(8,128)S(1)}, f32[256,128]{0,1:T(8,128)S(1)}, u32[]{:S(2)}, u32[]{:S(2)}) collective-permute-start(f32[256,128]{0,1:T(8,128)S(1)} %constant_dynamic-slice_fusion.1), channel_id=1, source_target_pairs={{0,1},{1,0},{2,3},{3,2},{4,5},{5,4},{6,7},{7,6},{8,9},{9,8},{10,11... | collective-permute-start | bytes 393224 | tf_op jit(solution)/shard_map/ppermute | solution.py:43
  308.8 6.5 %collective-permute-start.60 = (f32[256,128]{0,1:T(8,128)S(1)}, f32[256,128]{0,1:T(8,128)S(1)}, u32[]{:S(2)}, u32[]{:S(2)}) collective-permute-start(f32[256,128]{0,1:T(8,128)S(1)} %dynamic-slice_add_fusion), channel_id=1, source_target_pairs={{0,2},{1,3},{2,0},{3,1},{4,6},{5,7},{6,4},{7,5},{8,10},{9,11},{10,... | collective-permute-start | bytes 393224 | tf_op jit(solution)/shard_map/ppermute | solution.py:34
  308.9 10.4 %collective-permute-start.61 = (f32[256,128]{0,1:T(8,128)S(1)}, f32[256,128]{0,1:T(8,128)S(1)}, u32[]{:S(2)}, u32[]{:S(2)}) collective-permute-start(f32[256,128]{0,1:T(8,128)S(1)} %dynamic-slice_add_fusion), channel_id=1, source_target_pairs={{0,4},{1,5},{2,6},{3,7},{4,0},{5,1},{6,2},{7,3},{8,12},{9,13},{10,... | collective-permute-start | bytes 393224 | tf_op jit(solution)/shard_map/ppermute | solution.py:34
  312.9 8.7 %collective-permute-start.62 = (f32[256,128]{0,1:T(8,128)S(1)}, f32[256,128]{0,1:T(8,128)S(1)}, u32[]{:S(2)}, u32[]{:S(2)}) collective-permute-start(f32[256,128]{0,1:T(8,128)S(1)} %dynamic-slice_add_fusion), channel_id=1, source_target_pairs={{0,6},{1,7},{2,4},{3,5},{4,2},{5,3},{6,0},{7,1},{8,14},{9,15},{10,... | collective-permute-start | bytes 393224 | tf_op jit(solution)/shard_map/ppermute | solution.py:34
  (40 other events, 434.1 us)
where the time goes:
time: 327 us; the launch traced here: 323 us
  waiting for transfers between devices  185 us (57%)
  starting transfers between devices  97.1 us (30%)
  matrix products  19.2 us (6%)
  local copies, waits for them, and re-layouts  10 us (3%)
  other arithmetic  9.61 us (3%)
    ppermute x33, waiting for transfers between devices, group_sum(): lax.ppermute(x, axis, [(i, i ^ step * k) for i in range(n)])  92.9 us
    ppermute x10, waiting for transfers between devices, to_columns(): return lax.ppermute(x, GRID, pairs)  70.9 us
    ppermute x33, starting transfers between devices, group_sum(): lax.ppermute(x, axis, [(i, i ^ step * k) for i in range(n)])  57 us
    ppermute x10, starting transfers between devices, column_total(): lax.ppermute(give_half, 'col', [(i, i ^ 1) for i in range(n)])  24.7 us
    ppermute x10, starting transfers between devices, to_columns(): return lax.ppermute(x, GRID, pairs)  15.2 us
    ppermute x10, waiting for transfers between devices, join_halves(): other = lax.ppermute(mine, 'col', [(i, i ^ 1) for i in range(n)])  10.7 us
    ppermute x10, waiting for transfers between devices, column_total(): lax.ppermute(give_half, 'col', [(i, i ^ 1) for i in range(n)])  10.4 us
    dot_general x4, matrix products, shards(): jnp.dot(inv[0, level], resid, preferred_element_type=f32)  6.61 us
  transfers between devices with their start and end apart: 63, of which 60 were waited for; matrix products, arithmetic and copies ran while one was open for 4% of the time, Pallas kernels for 0%

commit v1 on v0

--- a/solution.py
+++ b/solution.py
@@ -22,6 +22,25 @@
         sources = sorted(range(n), key=lambda s: (ring_distance(s // 2, c // 2, n // 2), s % 2 != c % 2, s))
         pairs += [(c * n + s, r * n + c) for r, s in zip(targets, sources)]
     return lax.ppermute(x, GRID, pairs)
+
+
+def halves_to_columns(mine, n):
+    r_me = lax.axis_index("row")
+    c_me = lax.axis_index("col")
+    got = []
+    for h in range(2):
+        first = [[False] * n for _ in range(n)]
+        rounds = [[], []]
+        for c in range(n):
+            targets = sorted(range(n), key=lambda r: (-ring_distance(r, c, n), r))
+            sources = sorted(range(h, n, 2), key=lambda s: (ring_distance(s // 2, c // 2, n // 2), s))
+            for i, r in enumerate(targets):
+                rounds[i // len(sources)].append((c * n + sources[i % len(sources)], r * n + c))
+                first[r][c] = i < len(sources)
+        sent = [lax.ppermute(mine, GRID, pairs) for pairs in rounds]
+        pick = jnp.asarray(first)[r_me, c_me]
+        got.append(jnp.where(pick, sent[0], sent[1]))
+    return jnp.concatenate(got, mine.ndim - 1)
 
 
 def tree_sum(parts):
@@ -117,7 +136,7 @@
             resid = (own_rhs[level] - column_total(part, ncol)).astype(bf16)
         solved = keep[level] * jnp.dot(inv[0, level], resid, preferred_element_type=f32)
         ys.append(solved)
-        segs.append(to_columns(join_halves(solved.astype(bf16), ncol), n))
+        segs.append(halves_to_columns(solved.astype(bf16), n))
 
     coupling = jnp.stack([products([lm[t, j] for j in range(levels)], segs) for t in range(tops)], 0)
     coupling = column_total(coupling, ncol, leaves)
@@ -132,7 +151,7 @@
         resid = (top_rhs[top] - summed).astype(bf16)
         solved = jnp.dot(tinv[0, top], resid, preferred_element_type=f32)
         yts.append(solved)
-        tsegs.append(to_columns(join_halves(solved.astype(bf16), ncol), n))
+        tsegs.append(halves_to_columns(solved.astype(bf16), n))
 
     zts = [None] * tops
     tback = [None] * tops
@@ -144,7 +163,7 @@
             resid = (yts[top] - column_total(part, ncol)).astype(bf16)
         solved = jnp.dot(tinv[1, top], resid, preferred_element_type=f32)
         zts[top] = solved
-        tback[top] = to_columns(join_halves(solved.astype(bf16), ncol), n)
+        tback[top] = halves_to_columns(solved.astype(bf16), n)
 
     zs = [None] * levels
     back = [None] * levels
@@ -155,7 +174,7 @@
         solved = keep[level] * jnp.dot(inv[1, level], resid, preferred_element_type=f32)
         zs[level] = solved
         if level > 0:
-            back[level] = to_columns(join_halves(solved.astype(bf16), ncol), n)
+            back[level] = halves_to_columns(solved.astype(bf16), n)
 
     start = (lax.axis_index("col") // 2) * share
     result = lax.dynamic_slice_in_dim(jnp.stack(zs, 0), start, share, 2)

time: 327 us -> 380 us (1.16)
  the two profiles are of different devices: /device:TPU:96 before, /device:TPU:1 now
where the time goes in v1:
time: 380 us; the launch traced here: 378 us
  starting transfers between devices  186 us (49%)
  waiting for transfers between devices  146 us (38%)
  other arithmetic  18.9 us (5%)
  matrix products  17.3 us (5%)
  local copies, waits for them, and re-layouts  7.94 us (2%)
    ppermute x40, starting transfers between devices, halves_to_columns(): sent = [lax.ppermute(mine, GRID, pairs) for pairs in rounds]  139 us
    ppermute x33, waiting for transfers between devices, group_sum(): lax.ppermute(x, axis, [(i, i ^ step * k) for i in range(n)])  96.8 us
    ppermute x33, starting transfers between devices, group_sum(): lax.ppermute(x, axis, [(i, i ^ step * k) for i in range(n)])  45 us
    ppermute x40, waiting for transfers between devices, halves_to_columns(): sent = [lax.ppermute(mine, GRID, pairs) for pairs in rounds]  38.1 us
    select_n x20, other arithmetic, halves_to_columns(): got.append(jnp.where(pick, sent[0], sent[1]))  11 us
    ppermute x10, waiting for transfers between devices, column_total(): lax.ppermute(give_half, 'col', [(i, i ^ 1) for i in range(n)])  10.8 us
  transfers between devices with their start and end apart: 83, of which 50 were waited for; matrix products, arithmetic and copies ran while one was open for 4% of the time, Pallas kernels for 0%

profile of v1, /device:TPU:1, one launch (start us, length us, event | category | flops | bytes accessed | tf_op | source)
XLA Modules:
  0.0 378.4 jit_solution(15815599558825771701)
XLA Ops:
  4.7 10.2 %collective-permute-start.2 = (bf16[256,128]{0,1:T(8,128)(2,1)S(1)}, bf16[256,128]{0,1:T(8,128)(2,1)S(1)}, u32[]{:S(2)}, u32[]{:S(2)}) collective-permute-start(bf16[256,128]{0,1:T(8,128)(2,1)S(1)} %get-tuple-element.33), channel_id=1, source_target_pairs={{1,32},{3,24},{7,40},{5,16},{9,41},{11,33},{15,49},{13,25},{19,50}... | collective-permute-start | bytes 196616 | tf_op jit(solution)/shard_map/ppermute | solution.py:40
  21.8 4.4 %collective-permute-done.1 = bf16[256,128]{0,1:T(8,128)(2,1)S(1)} collective-permute-done((bf16[256,128]{0,1:T(8,128)(2,1)S(1)}, bf16[256,128]{0,1:T(8,128)(2,1)S(1)}, u32[]{:S(2)}, u32[]{:S(2)}) %collective-permute-start.1) | collective-permute-done | bytes 65568 | tf_op jit(solution)/shard_map/ppermute | solution.py:40
  33.5 4.7 %collective-permute-done.6 = f32[256,128]{1,0:T(8,128)S(1)} collective-permute-done((f32[256,128]{1,0:T(8,128)S(1)}, f32[256,128]{1,0:T(8,128)S(1)}, u32[]{:S(2)}, u32[]{:S(2)}) %collective-permute-start.6) | collective-permute-done | bytes 131104 | tf_op jit(solution)/shard_map/ppermute | solution.py:53
  38.2 2.5 collective-permute-done.7
  43.8 10.4 %collective-permute-start.10 = (bf16[256,128]{0,1:T(8,128)(2,1)S(1)}, bf16[256,128]{0,1:T(8,128)(2,1)S(1)}, u32[]{:S(2)}, u32[]{:S(2)}) collective-permute-start(bf16[256,128]{0,1:T(8,128)(2,1)S(1)} %get-tuple-element.35), channel_id=1, source_target_pairs={{1,32},{3,24},{7,40},{5,16},{9,41},{11,33},{15,49},{13,25},{19,50}... | collective-permute-start | bytes 196616 | tf_op jit(solution)/shard_map/ppermute | solution.py:40
  56.8 3.8 collective-permute-done.11
  64.3 3.2 collective-permute-start.14
  67.7 5.9 %collective-permute-done.14 = f32[256,128]{1,0:T(8,128)S(1)} collective-permute-done((f32[256,128]{1,0:T(8,128)S(1)}, f32[256,128]{1,0:T(8,128)S(1)}, u32[]{:S(2)}, u32[]{:S(2)}) %collective-permute-start.14) | collective-permute-done | bytes 131104 | tf_op jit(solution)/shard_map/ppermute | solution.py:53
  73.6 2.5 collective-permute-done.15
  80.0 9.7 %collective-permute-start.18 = (bf16[256,128]{0,1:T(8,128)(2,1)S(1)}, bf16[256,128]{0,1:T(8,128)(2,1)S(1)}, u32[]{:S(2)}, u32[]{:S(2)}) collective-permute-start(bf16[256,128]{0,1:T(8,128)(2,1)S(1)} %get-tuple-element.37), channel_id=1, source_target_pairs={{1,32},{3,24},{7,40},{5,16},{9,41},{11,33},{15,49},{13,25},{19,50}... | collective-permute-start | bytes 196616 | tf_op jit(solution)/shard_map/ppermute | solution.py:40
  92.2 3.7 collective-permute-done.19
  99.3 3.5 collective-permute-start.22
  104.3 4.6 %collective-permute-done.22 = f32[256,128]{1,0:T(8,128)} collective-permute-done((f32[256,128]{1,0:T(8,128)S(1)}, f32[256,128]{1,0:T(8,128)}, u32[]{:S(2)}, u32[]{:S(2)}) %collective-permute-start.22) | collective-permute-done | bytes 131104 | tf_op jit(solution)/shard_map/ppermute | solution.py:53
  109.0 2.5 collective-permute-done.23
  115.5 9.7 %collective-permute-start.26 = (bf16[256,128]{0,1:T(8,128)(2,1)S(1)}, bf16[256,128]{0,1:T(8,128)(2,1)S(1)}, u32[]{:S(2)}, u32[]{:S(2)}) collective-permute-start(bf16[256,128]{0,1:T(8,128)(2,1)S(1)} %get-tuple-element.39), channel_id=1, source_target_pairs={{1,32},{3,24},{7,40},{5,16},{9,41},{11,33},{15,49},{13,25},{19,50}... | collective-permute-start | bytes 196616 | tf_op jit(solution)/shard_map/ppermute | solution.py:40
  127.7 4.0 %collective-permute-done.27 = bf16[256,128]{0,1:T(8,128)(2,1)S(1)} collective-permute-done((bf16[256,128]{0,1:T(8,128)(2,1)S(1)}, bf16[256,128]{0,1:T(8,128)(2,1)S(1)}, u32[]{:S(2)}, u32[]{:S(2)}) %collective-permute-start.27) | collective-permute-done | bytes 65568 | tf_op jit(solution)/shard_map/ppermute | solution.py:40
  134.9 3.9 %collective-permute-start.30 = (f32[2,256,128]{2,1,0:T(8,128)S(1)}, f32[2,256,128]{2,1,0:T(8,128)S(1)}, u32[]{:S(2)}, u32[]{:S(2)}) collective-permute-start(f32[2,256,128]{2,1,0:T(8,128)S(1)} %fusion.56), channel_id=1, source_target_pairs={{0,4},{1,5},{2,6},{3,7},{4,0},{5,1},{6,2},{7,3},{8,12},{9,13},{10,... | collective-permute-start | bytes 786440 | tf_op jit(solution)/shard_map/ppermute | solution.py:53
  138.8 3.8 collective-permute-done.29
  142.6 7.9 %collective-permute-done.30 = f32[2,256,128]{2,1,0:T(8,128)S(1)} collective-permute-done((f32[2,256,128]{2,1,0:T(8,128)S(1)}, f32[2,256,128]{2,1,0:T(8,128)S(1)}, u32[]{:S(2)}, u32[]{:S(2)}) %collective-permute-start.30) | collective-permute-done | bytes 262176 | tf_op jit(solution)/shard_map/ppermute | solution.py:53
  154.1 2.6 collective-permute-start.33
  159.0 8.1 %collective-permute-done.33 = f32[2,256,128]{2,1,0:T(8,128)} collective-permute-done((f32[2,256,128]{2,1,0:T(8,128)S(1)}, f32[2,256,128]{2,1,0:T(8,128)}, u32[]{:S(2)}, u32[]{:S(2)}) %collective-permute-start.33) | collective-permute-done | bytes 262176 | tf_op jit(solution)/shard_map/ppermute | solution.py:53
  167.1 3.1 collective-permute-done.34
  174.5 10.8 %collective-permute-start.37 = (bf16[256,128]{0,1:T(8,128)(2,1)S(1)}, bf16[256,128]{0,1:T(8,128)(2,1)S(1)}, u32[]{:S(2)}, u32[]{:S(2)}) collective-permute-start(bf16[256,128]{0,1:T(8,128)(2,1)S(1)} %get-tuple-element.41), channel_id=1, source_target_pairs={{1,32},{3,24},{7,40},{5,16},{9,41},{11,33},{15,49},{13,25},{19,50}... | collective-permute-start | bytes 196616 | tf_op jit(solution)/shard_map/ppermute | solution.py:40
  187.9 3.4 collective-permute-done.38
  193.6 2.7 collective-permute-start.41
  198.5 3.9 %collective-permute-done.41 = f32[256,128]{1,0:T(8,128)} collective-permute-done((f32[256,128]{1,0:T(8,128)S(1)}, f32[256,128]{1,0:T(8,128)}, u32[]{:S(2)}, u32[]{:S(2)}) %collective-permute-start.41) | collective-permute-done | bytes 131104 | tf_op jit(solution)/shard_map/ppermute | solution.py:53
  202.4 2.6 collective-permute-done.42
  209.9 10.7 %collective-permute-start.45 = (bf16[256,128]{0,1:T(8,128)(2,1)}, bf16[256,128]{0,1:T(8,128)(2,1)S(1)}, u32[]{:S(2)}, u32[]{:S(2)}) collective-permute-start(bf16[256,128]{0,1:T(8,128)(2,1)} %get-tuple-element.43), channel_id=1, source_target_pairs={{1,32},{3,24},{7,40},{5,16},{9,41},{11,33},{15,49},{13,25},{19,50}... | collective-permute-start | bytes 196616 | tf_op jit(solution)/shard_map/ppermute | solution.py:40
  223.2 3.9 %collective-permute-done.46 = bf16[256,128]{0,1:T(8,128)(2,1)S(1)} collective-permute-done((bf16[256,128]{0,1:T(8,128)(2,1)}, bf16[256,128]{0,1:T(8,128)(2,1)S(1)}, u32[]{:S(2)}, u32[]{:S(2)}) %collective-permute-start.46) | collective-permute-done | bytes 65568 | tf_op jit(solution)/shard_map/ppermute | solution.py:40
  230.0 4.2 %collective-permute-start.49 = (f32[256,128]{0,1:T(8,128)S(1)}, f32[256,128]{0,1:T(8,128)S(1)}, u32[]{:S(2)}, u32[]{:S(2)}) collective-permute-start(f32[256,128]{0,1:T(8,128)S(1)} %dynamic-slice_add_fusion.4), channel_id=1, source_target_pairs={{0,4},{1,5},{2,6},{3,7},{4,0},{5,1},{6,2},{7,3},{8,12},{9,13},{10,... | collective-permute-start | bytes 393224 | tf_op jit(solution)/shard_map/ppermute | solution.py:53
  235.0 5.6 %collective-permute-done.49 = f32[256,128]{0,1:T(8,128)S(1)} collective-permute-done((f32[256,128]{0,1:T(8,128)S(1)}, f32[256,128]{0,1:T(8,128)S(1)}, u32[]{:S(2)}, u32[]{:S(2)}) %collective-permute-start.49) | collective-permute-done | bytes 131104 | tf_op jit(solution)/shard_map/ppermute | solution.py:53
  240.6 2.5 collective-permute-done.50
  247.0 9.3 %collective-permute-start.53 = (bf16[256,128]{0,1:T(8,128)(2,1)S(1)}, bf16[256,128]{0,1:T(8,128)(2,1)S(1)}, u32[]{:S(2)}, u32[]{:S(2)}) collective-permute-start(bf16[256,128]{0,1:T(8,128)(2,1)S(1)} %get-tuple-element.45), channel_id=1, source_target_pairs={{1,32},{3,24},{7,40},{5,16},{9,41},{11,33},{15,49},{13,25},{19,50}... | collective-permute-start | bytes 196616 | tf_op jit(solution)/shard_map/ppermute | solution.py:40
  258.9 3.4 collective-permute-done.54
  264.7 3.2 collective-permute-start.57
  269.6 4.4 %collective-permute-done.57 = f32[256,128]{0,1:T(8,128)S(1)} collective-permute-done((f32[256,128]{0,1:T(8,128)S(1)}, f32[256,128]{0,1:T(8,128)S(1)}, u32[]{:S(2)}, u32[]{:S(2)}) %collective-permute-start.57) | collective-permute-done | bytes 131104 | tf_op jit(solution)/shard_map/ppermute | solution.py:53
  278.9 9.7 %collective-permute-start.61 = (bf16[256,128]{0,1:T(8,128)(2,1)S(1)}, bf16[256,128]{0,1:T(8,128)(2,1)S(1)}, u32[]{:S(2)}, u32[]{:S(2)}) collective-permute-start(bf16[256,128]{0,1:T(8,128)(2,1)S(1)} %get-tuple-element.47), channel_id=1, source_target_pairs={{1,32},{3,24},{7,40},{5,16},{9,41},{11,33},{15,49},{13,25},{19,50}... | collective-permute-start | bytes 196616 | tf_op jit(solution)/shard_map/ppermute | solution.py:40
  291.1 3.7 collective-permute-done.62
  297.6 4.3 %collective-permute-start.65 = (f32[256,128]{0,1:T(8,128)S(1)}, f32[256,128]{0,1:T(8,128)S(1)}, u32[]{:S(2)}, u32[]{:S(2)}) collective-permute-start(f32[256,128]{0,1:T(8,128)S(1)} %dynamic-slice_add_fusion.2), channel_id=1, source_target_pairs={{0,4},{1,5},{2,6},{3,7},{4,0},{5,1},{6,2},{7,3},{8,12},{9,13},{10,... | collective-permute-start | bytes 393224 | tf_op jit(solution)/shard_map/ppermute | solution.py:53
  302.3 5.6 %collective-permute-done.65 = f32[256,128]{0,1:T(8,128)S(1)} collective-permute-done((f32[256,128]{0,1:T(8,128)S(1)}, f32[256,128]{0,1:T(8,128)S(1)}, u32[]{:S(2)}, u32[]{:S(2)}) %collective-permute-start.65) | collective-permute-done | bytes 131104 | tf_op jit(solution)/shard_map/ppermute | solution.py:53
  313.3 9.7 %collective-permute-start.69 = (bf16[256,128]{0,1:T(8,128)(2,1)S(1)}, bf16[256,128]{0,1:T(8,128)(2,1)S(1)}, u32[]{:S(2)}, u32[]{:S(2)}) collective-permute-start(bf16[256,128]{0,1:T(8,128)(2,1)S(1)} %get-tuple-element.49), channel_id=1, source_target_pairs={{1,32},{3,24},{7,40},{5,16},{9,41},{11,33},{15,49},{13,25},{19,50}... | collective-permute-start | bytes 196616 | tf_op jit(solution)/shard_map/ppermute | solution.py:40
  325.5 4.0 %collective-permute-done.70 = bf16[256,128]{0,1:T(8,128)(2,1)S(1)} collective-permute-done((bf16[256,128]{0,1:T(8,128)(2,1)S(1)}, bf16[256,128]{0,1:T(8,128)(2,1)S(1)}, u32[]{:S(2)}, u32[]{:S(2)}) %collective-permute-start.70) | collective-permute-done | bytes 65568 | tf_op jit(solution)/shard_map/ppermute | solution.py:40
  332.0 3.8 %collective-permute-start.73 = (f32[256,128]{0,1:T(8,128)S(1)}, f32[256,128]{0,1:T(8,128)S(1)}, u32[]{:S(2)}, u32[]{:S(2)}) collective-permute-start(f32[256,128]{0,1:T(8,128)S(1)} %dynamic-slice_add_fusion.1), channel_id=1, source_target_pairs={{0,4},{1,5},{2,6},{3,7},{4,0},{5,1},{6,2},{7,3},{8,12},{9,13},{10,... | collective-permute-start | bytes 393224 | tf_op jit(solution)/shard_map/ppermute | solution.py:53
  336.9 5.0 %collective-permute-done.73 = f32[256,128]{0,1:T(8,128)S(1)} collective-permute-done((f32[256,128]{0,1:T(8,128)S(1)}, f32[256,128]{0,1:T(8,128)S(1)}, u32[]{:S(2)}, u32[]{:S(2)}) %collective-permute-start.73) | collective-permute-done | bytes 131104 | tf_op jit(solution)/shard_map/ppermute | solution.py:53
  346.8 9.7 %collective-permute-start.77 = (bf16[256,128]{0,1:T(8,128)(2,1)S(1)}, bf16[256,128]{0,1:T(8,128)(2,1)S(1)}, u32[]{:S(2)}, u32[]{:S(2)}) collective-permute-start(bf16[256,128]{0,1:T(8,128)(2,1)S(1)} %get-tuple-element.51), channel_id=1, source_target_pairs={{1,32},{3,24},{7,40},{5,16},{9,41},{11,33},{15,49},{13,25},{19,50}... | collective-permute-start | bytes 196616 | tf_op jit(solution)/shard_map/ppermute | solution.py:40
  359.0 3.7 collective-permute-done.78
  365.3 3.5 collective-permute-start.81
  370.2 4.7 %collective-permute-done.81 = f32[256,128]{0,1:T(8,128)S(1)} collective-permute-done((f32[256,128]{0,1:T(8,128)S(1)}, f32[256,128]{0,1:T(8,128)S(1)}, u32[]{:S(2)}, u32[]{:S(2)}) %collective-permute-start.81) | collective-permute-done | bytes 131104 | tf_op jit(solution)/shard_map/ppermute | solution.py:53
  (280 shorter events, 123.1 us)
Async XLA Ops:
  4.7 16.5 %collective-permute-start.2 = (bf16[256,128]{0,1:T(8,128)(2,1)S(1)}, bf16[256,128]{0,1:T(8,128)(2,1)S(1)}, u32[]{:S(2)}, u32[]{:S(2)}) collective-permute-start(bf16[256,128]{0,1:T(8,128)(2,1)S(1)} %get-tuple-element.33), channel_id=1, source_target_pairs={{1,32},{3,24},{7,40},{5,16},{9,41},{11,33},{15,49},{13,25},{19,50}... | collective-permute-start | bytes 196616 | tf_op jit(solution)/shard_map/ppermute | solution.py:40
  17.5 8.7 %collective-permute-start.1 = (bf16[256,128]{0,1:T(8,128)(2,1)S(1)}, bf16[256,128]{0,1:T(8,128)(2,1)S(1)}, u32[]{:S(2)}, u32[]{:S(2)}) collective-permute-start(bf16[256,128]{0,1:T(8,128)(2,1)S(1)} %get-tuple-element.33), channel_id=1, source_target_pairs={{0,48},{2,8},{6,56},{4,0},{8,57},{10,1},{14,17},{12,9},{18,34},{16... | collective-permute-start | bytes 196616 | tf_op jit(solution)/shard_map/ppermute | solution.py:40
  31.9 8.8 %collective-permute-start.7 = (f32[256,128]{1,0:T(8,128)S(1)}, f32[256,128]{1,0:T(8,128)S(1)}, u32[]{:S(2)}, u32[]{:S(2)}) collective-permute-start(f32[256,128]{1,0:T(8,128)S(1)} %dynamic-slice_add_fusion.8), channel_id=1, source_target_pairs={{0,6},{1,7},{2,4},{3,5},{4,2},{5,3},{6,0},{7,1},{8,14},{9,15},{10,... | collective-permute-start | bytes 393224 | tf_op jit(solution)/shard_map/ppermute | solution.py:53
  41.8 14.3 %collective-permute-start.8 = (bf16[256,128]{0,1:T(8,128)(2,1)S(1)}, bf16[256,128]{0,1:T(8,128)(2,1)S(1)}, u32[]{:S(2)}, u32[]{:S(2)}) collective-permute-start(bf16[256,128]{0,1:T(8,128)(2,1)S(1)} %get-tuple-element.35), channel_id=1, source_target_pairs={{0,32},{2,24},{6,40},{4,16},{8,41},{10,33},{14,49},{12,25},{18,50}... | collective-permute-start | bytes 196616 | tf_op jit(solution)/shard_map/ppermute | solution.py:40
  42.5 13.7 %collective-permute-start.9 = (bf16[256,128]{0,1:T(8,128)(2,1)S(1)}, bf16[256,128]{0,1:T(8,128)(2,1)S(1)}, u32[]{:S(2)}, u32[]{:S(2)}) collective-permute-start(bf16[256,128]{0,1:T(8,128)(2,1)S(1)} %get-tuple-element.35), channel_id=1, source_target_pairs={{0,48},{2,8},{6,56},{4,0},{8,57},{10,1},{14,17},{12,9},{18,34},{16... | collective-permute-start | bytes 196616 | tf_op jit(solution)/shard_map/ppermute | solution.py:40
  43.8 12.9 %collective-permute-start.10 = (bf16[256,128]{0,1:T(8,128)(2,1)S(1)}, bf16[256,128]{0,1:T(8,128)(2,1)S(1)}, u32[]{:S(2)}, u32[]{:S(2)}) collective-permute-start(bf16[256,128]{0,1:T(8,128)(2,1)S(1)} %get-tuple-element.35), channel_id=1, source_target_pairs={{1,32},{3,24},{7,40},{5,16},{9,41},{11,33},{15,49},{13,25},{19,50}... | collective-permute-start | bytes 196616 | tf_op jit(solution)/shard_map/ppermute | solution.py:40
  64.3 9.3 %collective-permute-start.14 = (f32[256,128]{1,0:T(8,128)S(1)}, f32[256,128]{1,0:T(8,128)S(1)}, u32[]{:S(2)}, u32[]{:S(2)}) collective-permute-start(f32[256,128]{1,0:T(8,128)S(1)} %dynamic-slice_add_fusion.7), channel_id=1, source_target_pairs={{0,4},{1,5},{2,6},{3,7},{4,0},{5,1},{6,2},{7,3},{8,12},{9,13},{10,... | collective-permute-start | bytes 393224 | tf_op jit(solution)/shard_map/ppermute | solution.py:53
  67.5 8.6 %collective-permute-start.15 = (f32[256,128]{1,0:T(8,128)S(1)}, f32[256,128]{1,0:T(8,128)S(1)}, u32[]{:S(2)}, u32[]{:S(2)}) collective-permute-start(f32[256,128]{1,0:T(8,128)S(1)} %dynamic-slice_add_fusion.7), channel_id=1, source_target_pairs={{0,6},{1,7},{2,4},{3,5},{4,2},{5,3},{6,0},{7,1},{8,14},{9,15},{10,... | collective-permute-start | bytes 393224 | tf_op jit(solution)/shard_map/ppermute | solution.py:53
  78.0 13.6 %collective-permute-start.16 = (bf16[256,128]{0,1:T(8,128)(2,1)S(1)}, bf16[256,128]{0,1:T(8,128)(2,1)S(1)}, u32[]{:S(2)}, u32[]{:S(2)}) collective-permute-start(bf16[256,128]{0,1:T(8,128)(2,1)S(1)} %get-tuple-element.37), channel_id=1, source_target_pairs={{0,32},{2,24},{6,40},{4,16},{8,41},{10,33},{14,49},{12,25},{18,50}... | collective-permute-start | bytes 196616 | tf_op jit(solution)/shard_map/ppermute | solution.py:40
  78.7 12.9 %collective-permute-start.17 = (bf16[256,128]{0,1:T(8,128)(2,1)S(1)}, bf16[256,128]{0,1:T(8,128)(2,1)S(1)}, u32[]{:S(2)}, u32[]{:S(2)}) collective-permute-start(bf16[256,128]{0,1:T(8,128)(2,1)S(1)} %get-tuple-element.37), channel_id=1, source_target_pairs={{0,48},{2,8},{6,56},{4,0},{8,57},{10,1},{14,17},{12,9},{18,34},{16... | collective-permute-start | bytes 196616 | tf_op jit(solution)/shard_map/ppermute | solution.py:40
  80.0 12.2 %collective-permute-start.18 = (bf16[256,128]{0,1:T(8,128)(2,1)S(1)}, bf16[256,128]{0,1:T(8,128)(2,1)S(1)}, u32[]{:S(2)}, u32[]{:S(2)}) collective-permute-start(bf16[256,128]{0,1:T(8,128)(2,1)S(1)} %get-tuple-element.37), channel_id=1, source_target_pairs={{1,32},{3,24},{7,40},{5,16},{9,41},{11,33},{15,49},{13,25},{19,50}... | collective-permute-start | bytes 196616 | tf_op jit(solution)/shard_map/ppermute | solution.py:40
  99.3 9.7 %collective-permute-start.22 = (f32[256,128]{1,0:T(8,128)S(1)}, f32[256,128]{1,0:T(8,128)}, u32[]{:S(2)}, u32[]{:S(2)}) collective-permute-start(f32[256,128]{1,0:T(8,128)S(1)} %dynamic-slice_add_fusion.6), channel_id=1, source_target_pairs={{0,4},{1,5},{2,6},{3,7},{4,0},{5,1},{6,2},{7,3},{8,12},{9,13},{10,... | collective-permute-start | bytes 393224 | tf_op jit(solution)/shard_map/ppermute | solution.py:53
  102.8 8.7 %collective-permute-start.23 = (f32[256,128]{1,0:T(8,128)S(1)}, f32[256,128]{1,0:T(8,128)}, u32[]{:S(2)}, u32[]{:S(2)}) collective-permute-start(f32[256,128]{1,0:T(8,128)S(1)} %dynamic-slice_add_fusion.6), channel_id=1, source_target_pairs={{0,6},{1,7},{2,4},{3,5},{4,2},{5,3},{6,0},{7,1},{8,14},{9,15},{10,... | collective-permute-start | bytes 393224 | tf_op jit(solution)/shard_map/ppermute | solution.py:53
  113.5 13.7 %collective-permute-start.24 = (bf16[256,128]{0,1:T(8,128)(2,1)S(1)}, bf16[256,128]{0,1:T(8,128)(2,1)S(1)}, u32[]{:S(2)}, u32[]{:S(2)}) collective-permute-start(bf16[256,128]{0,1:T(8,128)(2,1)S(1)} %get-tuple-element.39), channel_id=1, source_target_pairs={{0,32},{2,24},{6,40},{4,16},{8,41},{10,33},{14,49},{12,25},{18,50}... | collective-permute-start | bytes 196616 | tf_op jit(solution)/shard_map/ppermute | solution.py:40
  114.1 13.0 %collective-permute-start.25 = (bf16[256,128]{0,1:T(8,128)(2,1)S(1)}, bf16[256,128]{0,1:T(8,128)(2,1)S(1)}, u32[]{:S(2)}, u32[]{:S(2)}) collective-permute-start(bf16[256,128]{0,1:T(8,128)(2,1)S(1)} %get-tuple-element.39), channel_id=1, source_target_pairs={{0,48},{2,8},{6,56},{4,0},{8,57},{10,1},{14,17},{12,9},{18,34},{16... | collective-permute-start | bytes 196616 | tf_op jit(solution)/shard_map/ppermute | solution.py:40
  115.5 12.2 %collective-permute-start.26 = (bf16[256,128]{0,1:T(8,128)(2,1)S(1)}, bf16[256,128]{0,1:T(8,128)(2,1)S(1)}, u32[]{:S(2)}, u32[]{:S(2)}) collective-permute-start(bf16[256,128]{0,1:T(8,128)(2,1)S(1)} %get-tuple-element.39), channel_id=1, source_target_pairs={{1,32},{3,24},{7,40},{5,16},{9,41},{11,33},{15,49},{13,25},{19,50}... | collective-permute-start | bytes 196616 | tf_op jit(solution)/shard_map/ppermute | solution.py:40
  134.9 15.6 %collective-permute-start.30 = (f32[2,256,128]{2,1,0:T(8,128)S(1)}, f32[2,256,128]{2,1,0:T(8,128)S(1)}, u32[]{:S(2)}, u32[]{:S(2)}) collective-permute-start(f32[2,256,128]{2,1,0:T(8,128)S(1)} %fusion.56), channel_id=1, source_target_pairs={{0,4},{1,5},{2,6},{3,7},{4,0},{5,1},{6,2},{7,3},{8,12},{9,13},{10,... | collective-permute-start | bytes 786440 | tf_op jit(solution)/shard_map/ppermute | solution.py:53
  138.8 13.8 %collective-permute-start.31 = (f32[2,256,128]{2,1,0:T(8,128)S(1)}, f32[2,256,128]{2,1,0:T(8,128)S(1)}, u32[]{:S(2)}, u32[]{:S(2)}) collective-permute-start(f32[2,256,128]{2,1,0:T(8,128)S(1)} %fusion.56), channel_id=1, source_target_pairs={{0,6},{1,7},{2,4},{3,5},{4,2},{5,3},{6,0},{7,1},{8,14},{9,15},{10,... | collective-permute-start | bytes 786440 | tf_op jit(solution)/shard_map/ppermute | solution.py:53
  154.1 13.0 %collective-permute-start.33 = (f32[2,256,128]{2,1,0:T(8,128)S(1)}, f32[2,256,128]{2,1,0:T(8,128)}, u32[]{:S(2)}, u32[]{:S(2)}) collective-permute-start(f32[2,256,128]{2,1,0:T(8,128)S(1)} %add_add_fusion.1), channel_id=1, source_target_pairs={{0,128},{64,192},{128,0},{192,64},{1,129},{65,193},{129,1},{193,65... | collective-permute-start | bytes 786440 | tf_op jit(solution)/shard_map/ppermute | solution.py:53
  156.7 13.5 %collective-permute-start.34 = (f32[2,256,128]{2,1,0:T(8,128)S(1)}, f32[2,256,128]{2,1,0:T(8,128)}, u32[]{:S(2)}, u32[]{:S(2)}) collective-permute-start(f32[2,256,128]{2,1,0:T(8,128)S(1)} %add_add_fusion.1), channel_id=1, source_target_pairs={{0,192},{64,128},{128,64},{192,0},{1,193},{65,129},{129,65},{193,1... | collective-permute-start | bytes 786440 | tf_op jit(solution)/shard_map/ppermute | solution.py:53
  172.5 14.8 %collective-permute-start.35 = (bf16[256,128]{0,1:T(8,128)(2,1)S(1)}, bf16[256,128]{0,1:T(8,128)(2,1)S(1)}, u32[]{:S(2)}, u32[]{:S(2)}) collective-permute-start(bf16[256,128]{0,1:T(8,128)(2,1)S(1)} %get-tuple-element.41), channel_id=1, source_target_pairs={{0,32},{2,24},{6,40},{4,16},{8,41},{10,33},{14,49},{12,25},{18,50}... | collective-permute-start | bytes 196616 | tf_op jit(solution)/shard_map/ppermute | solution.py:40
  173.1 14.2 %collective-permute-start.36 = (bf16[256,128]{0,1:T(8,128)(2,1)S(1)}, bf16[256,128]{0,1:T(8,128)(2,1)S(1)}, u32[]{:S(2)}, u32[]{:S(2)}) collective-permute-start(bf16[256,128]{0,1:T(8,128)(2,1)S(1)} %get-tuple-element.41), channel_id=1, source_target_pairs={{0,48},{2,8},{6,56},{4,0},{8,57},{10,1},{14,17},{12,9},{18,34},{16... | collective-permute-start | bytes 196616 | tf_op jit(solution)/shard_map/ppermute | solution.py:40
  174.5 13.3 %collective-permute-start.37 = (bf16[256,128]{0,1:T(8,128)(2,1)S(1)}, bf16[256,128]{0,1:T(8,128)(2,1)S(1)}, u32[]{:S(2)}, u32[]{:S(2)}) collective-permute-start(bf16[256,128]{0,1:T(8,128)(2,1)S(1)} %get-tuple-element.41), channel_id=1, source_target_pairs={{1,32},{3,24},{7,40},{5,16},{9,41},{11,33},{15,49},{13,25},{19,50}... | collective-permute-start | bytes 196616 | tf_op jit(solution)/shard_map/ppermute | solution.py:40
  193.6 8.8 %collective-permute-start.41 = (f32[256,128]{1,0:T(8,128)S(1)}, f32[256,128]{1,0:T(8,128)}, u32[]{:S(2)}, u32[]{:S(2)}) collective-permute-start(f32[256,128]{1,0:T(8,128)S(1)} %dynamic-slice_add_fusion.5), channel_id=1, source_target_pairs={{0,4},{1,5},{2,6},{3,7},{4,0},{5,1},{6,2},{7,3},{8,12},{9,13},{10,... | collective-permute-start | bytes 393224 | tf_op jit(solution)/shard_map/ppermute | solution.py:53
  196.3 8.7 %collective-permute-start.42 = (f32[256,128]{1,0:T(8,128)S(1)}, f32[256,128]{1,0:T(8,128)}, u32[]{:S(2)}, u32[]{:S(2)}) collective-permute-start(f32[256,128]{1,0:T(8,128)S(1)} %dynamic-slice_add_fusion.5), channel_id=1, source_target_pairs={{0,6},{1,7},{2,4},{3,5},{4,2},{5,3},{6,0},{7,1},{8,14},{9,15},{10,... | collective-permute-start | bytes 393224 | tf_op jit(solution)/shard_map/ppermute | solution.py:53
  207.2 15.4 %collective-permute-start.43 = (bf16[256,128]{0,1:T(8,128)(2,1)}, bf16[256,128]{0,1:T(8,128)(2,1)S(1)}, u32[]{:S(2)}, u32[]{:S(2)}) collective-permute-start(bf16[256,128]{0,1:T(8,128)(2,1)} %get-tuple-element.43), channel_id=1, source_target_pairs={{0,32},{2,24},{6,40},{4,16},{8,41},{10,33},{14,49},{12,25},{18,50}... | collective-permute-start | bytes 196616 | tf_op jit(solution)/shard_map/ppermute | solution.py:40
  207.8 14.8 %collective-permute-start.44 = (bf16[256,128]{0,1:T(8,128)(2,1)}, bf16[256,128]{0,1:T(8,128)(2,1)S(1)}, u32[]{:S(2)}, u32[]{:S(2)}) collective-permute-start(bf16[256,128]{0,1:T(8,128)(2,1)} %get-tuple-element.43), channel_id=1, source_target_pairs={{0,48},{2,8},{6,56},{4,0},{8,57},{10,1},{14,17},{12,9},{18,34},{16... | collective-permute-start | bytes 196616 | tf_op jit(solution)/shard_map/ppermute | solution.py:40
  209.9 13.3 %collective-permute-start.45 = (bf16[256,128]{0,1:T(8,128)(2,1)}, bf16[256,128]{0,1:T(8,128)(2,1)S(1)}, u32[]{:S(2)}, u32[]{:S(2)}) collective-permute-start(bf16[256,128]{0,1:T(8,128)(2,1)} %get-tuple-element.43), channel_id=1, source_target_pairs={{1,32},{3,24},{7,40},{5,16},{9,41},{11,33},{15,49},{13,25},{19,50}... | collective-permute-start | bytes 196616 | tf_op jit(solution)/shard_map/ppermute | solution.py:40
  230.0 10.6 %collective-permute-start.49 = (f32[256,128]{0,1:T(8,128)S(1)}, f32[256,128]{0,1:T(8,128)S(1)}, u32[]{:S(2)}, u32[]{:S(2)}) collective-permute-start(f32[256,128]{0,1:T(8,128)S(1)} %dynamic-slice_add_fusion.4), channel_id=1, source_target_pairs={{0,4},{1,5},{2,6},{3,7},{4,0},{5,1},{6,2},{7,3},{8,12},{9,13},{10,... | collective-permute-start | bytes 393224 | tf_op jit(solution)/shard_map/ppermute | solution.py:53
  234.2 9.0 %collective-permute-start.50 = (f32[256,128]{0,1:T(8,128)S(1)}, f32[256,128]{0,1:T(8,128)S(1)}, u32[]{:S(2)}, u32[]{:S(2)}) collective-permute-start(f32[256,128]{0,1:T(8,128)S(1)} %dynamic-slice_add_fusion.4), channel_id=1, source_target_pairs={{0,6},{1,7},{2,4},{3,5},{4,2},{5,3},{6,0},{7,1},{8,14},{9,15},{10,... | collective-permute-start | bytes 393224 | tf_op jit(solution)/shard_map/ppermute | solution.py:53
  244.9 13.4 %collective-permute-start.51 = (bf16[256,128]{0,1:T(8,128)(2,1)S(1)}, bf16[256,128]{0,1:T(8,128)(2,1)S(1)}, u32[]{:S(2)}, u32[]{:S(2)}) collective-permute-start(bf16[256,128]{0,1:T(8,128)(2,1)S(1)} %get-tuple-element.45), channel_id=1, source_target_pairs={{0,32},{2,24},{6,40},{4,16},{8,41},{10,33},{14,49},{12,25},{18,50}... | collective-permute-start | bytes 196616 | tf_op jit(solution)/shard_map/ppermute | solution.py:40
  245.7 12.6 %collective-permute-start.52 = (bf16[256,128]{0,1:T(8,128)(2,1)S(1)}, bf16[256,128]{0,1:T(8,128)(2,1)S(1)}, u32[]{:S(2)}, u32[]{:S(2)}) collective-permute-start(bf16[256,128]{0,1:T(8,128)(2,1)S(1)} %get-tuple-element.45), channel_id=1, source_target_pairs={{0,48},{2,8},{6,56},{4,0},{8,57},{10,1},{14,17},{12,9},{18,34},{16... | collective-permute-start | bytes 196616 | tf_op jit(solution)/shard_map/ppermute | solution.py:40
  247.0 11.9 %collective-permute-start.53 = (bf16[256,128]{0,1:T(8,128)(2,1)S(1)}, bf16[256,128]{0,1:T(8,128)(2,1)S(1)}, u32[]{:S(2)}, u32[]{:S(2)}) collective-permute-start(bf16[256,128]{0,1:T(8,128)(2,1)S(1)} %get-tuple-element.45), channel_id=1, source_target_pairs={{1,32},{3,24},{7,40},{5,16},{9,41},{11,33},{15,49},{13,25},{19,50}... | collective-permute-start | bytes 196616 | tf_op jit(solution)/shard_map/ppermute | solution.py:40
  264.7 9.3 %collective-permute-start.57 = (f32[256,128]{0,1:T(8,128)S(1)}, f32[256,128]{0,1:T(8,128)S(1)}, u32[]{:S(2)}, u32[]{:S(2)}) collective-permute-start(f32[256,128]{0,1:T(8,128)S(1)} %dynamic-slice_add_fusion.3), channel_id=1, source_target_pairs={{0,4},{1,5},{2,6},{3,7},{4,0},{5,1},{6,2},{7,3},{8,12},{9,13},{10,... | collective-permute-start | bytes 393224 | tf_op jit(solution)/shard_map/ppermute | solution.py:53
  276.8 13.7 %collective-permute-start.59 = (bf16[256,128]{0,1:T(8,128)(2,1)S(1)}, bf16[256,128]{0,1:T(8,128)(2,1)S(1)}, u32[]{:S(2)}, u32[]{:S(2)}) collective-permute-start(bf16[256,128]{0,1:T(8,128)(2,1)S(1)} %get-tuple-element.47), channel_id=1, source_target_pairs={{0,32},{2,24},{6,40},{4,16},{8,41},{10,33},{14,49},{12,25},{18,50}... | collective-permute-start | bytes 196616 | tf_op jit(solution)/shard_map/ppermute | solution.py:40
  277.6 12.9 %collective-permute-start.60 = (bf16[256,128]{0,1:T(8,128)(2,1)S(1)}, bf16[256,128]{0,1:T(8,128)(2,1)S(1)}, u32[]{:S(2)}, u32[]{:S(2)}) collective-permute-start(bf16[256,128]{0,1:T(8,128)(2,1)S(1)} %get-tuple-element.47), channel_id=1, source_target_pairs={{0,48},{2,8},{6,56},{4,0},{8,57},{10,1},{14,17},{12,9},{18,34},{16... | collective-permute-start | bytes 196616 | tf_op jit(solution)/shard_map/ppermute | solution.py:40
  278.9 12.2 %collective-permute-start.61 = (bf16[256,128]{0,1:T(8,128)(2,1)S(1)}, bf16[256,128]{0,1:T(8,128)(2,1)S(1)}, u32[]{:S(2)}, u32[]{:S(2)}) collective-permute-start(bf16[256,128]{0,1:T(8,128)(2,1)S(1)} %get-tuple-element.47), channel_id=1, source_target_pairs={{1,32},{3,24},{7,40},{5,16},{9,41},{11,33},{15,49},{13,25},{19,50}... | collective-permute-start | bytes 196616 | tf_op jit(solution)/shard_map/ppermute | solution.py:40
  297.6 10.4 %collective-permute-start.65 = (f32[256,128]{0,1:T(8,128)S(1)}, f32[256,128]{0,1:T(8,128)S(1)}, u32[]{:S(2)}, u32[]{:S(2)}) collective-permute-start(f32[256,128]{0,1:T(8,128)S(1)} %dynamic-slice_add_fusion.2), channel_id=1, source_target_pairs={{0,4},{1,5},{2,6},{3,7},{4,0},{5,1},{6,2},{7,3},{8,12},{9,13},{10,... | collective-permute-start | bytes 393224 | tf_op jit(solution)/shard_map/ppermute | solution.py:53
  301.8 8.6 %collective-permute-start.66 = (f32[256,128]{0,1:T(8,128)S(1)}, f32[256,128]{0,1:T(8,128)S(1)}, u32[]{:S(2)}, u32[]{:S(2)}) collective-permute-start(f32[256,128]{0,1:T(8,128)S(1)} %dynamic-slice_add_fusion.2), channel_id=1, source_target_pairs={{0,6},{1,7},{2,4},{3,5},{4,2},{5,3},{6,0},{7,1},{8,14},{9,15},{10,... | collective-permute-start | bytes 393224 | tf_op jit(solution)/shard_map/ppermute | solution.py:53
  311.3 13.6 %collective-permute-start.67 = (bf16[256,128]{0,1:T(8,128)(2,1)S(1)}, bf16[256,128]{0,1:T(8,128)(2,1)S(1)}, u32[]{:S(2)}, u32[]{:S(2)}) collective-permute-start(bf16[256,128]{0,1:T(8,128)(2,1)S(1)} %get-tuple-element.49), channel_id=1, source_target_pairs={{0,32},{2,24},{6,40},{4,16},{8,41},{10,33},{14,49},{12,25},{18,50}... | collective-permute-start | bytes 196616 | tf_op jit(solution)/shard_map/ppermute | solution.py:40
  312.0 13.0 %collective-permute-start.68 = (bf16[256,128]{0,1:T(8,128)(2,1)S(1)}, bf16[256,128]{0,1:T(8,128)(2,1)S(1)}, u32[]{:S(2)}, u32[]{:S(2)}) collective-permute-start(bf16[256,128]{0,1:T(8,128)(2,1)S(1)} %get-tuple-element.49), channel_id=1, source_target_pairs={{0,48},{2,8},{6,56},{4,0},{8,57},{10,1},{14,17},{12,9},{18,34},{16... | collective-permute-start | bytes 196616 | tf_op jit(solution)/shard_map/ppermute | solution.py:40
  313.3 12.2 %collective-permute-start.69 = (bf16[256,128]{0,1:T(8,128)(2,1)S(1)}, bf16[256,128]{0,1:T(8,128)(2,1)S(1)}, u32[]{:S(2)}, u32[]{:S(2)}) collective-permute-start(bf16[256,128]{0,1:T(8,128)(2,1)S(1)} %get-tuple-element.49), channel_id=1, source_target_pairs={{1,32},{3,24},{7,40},{5,16},{9,41},{11,33},{15,49},{13,25},{19,50}... | collective-permute-start | bytes 196616 | tf_op jit(solution)/shard_map/ppermute | solution.py:40
  332.0 9.9 %collective-permute-start.73 = (f32[256,128]{0,1:T(8,128)S(1)}, f32[256,128]{0,1:T(8,128)S(1)}, u32[]{:S(2)}, u32[]{:S(2)}) collective-permute-start(f32[256,128]{0,1:T(8,128)S(1)} %dynamic-slice_add_fusion.1), channel_id=1, source_target_pairs={{0,4},{1,5},{2,6},{3,7},{4,0},{5,1},{6,2},{7,3},{8,12},{9,13},{10,... | collective-permute-start | bytes 393224 | tf_op jit(solution)/shard_map/ppermute | solution.py:53
  335.8 8.6 %collective-permute-start.74 = (f32[256,128]{0,1:T(8,128)S(1)}, f32[256,128]{0,1:T(8,128)S(1)}, u32[]{:S(2)}, u32[]{:S(2)}) collective-permute-start(f32[256,128]{0,1:T(8,128)S(1)} %dynamic-slice_add_fusion.1), channel_id=1, source_target_pairs={{0,6},{1,7},{2,4},{3,5},{4,2},{5,3},{6,0},{7,1},{8,14},{9,15},{10,... | collective-permute-start | bytes 393224 | tf_op jit(solution)/shard_map/ppermute | solution.py:53
  344.7 13.8 %collective-permute-start.75 = (bf16[256,128]{0,1:T(8,128)(2,1)S(1)}, bf16[256,128]{0,1:T(8,128)(2,1)S(1)}, u32[]{:S(2)}, u32[]{:S(2)}) collective-permute-start(bf16[256,128]{0,1:T(8,128)(2,1)S(1)} %get-tuple-element.51), channel_id=1, source_target_pairs={{0,32},{2,24},{6,40},{4,16},{8,41},{10,33},{14,49},{12,25},{18,50}... | collective-permute-start | bytes 196616 | tf_op jit(solution)/shard_map/ppermute | solution.py:40
  345.5 13.0 %collective-permute-start.76 = (bf16[256,128]{0,1:T(8,128)(2,1)S(1)}, bf16[256,128]{0,1:T(8,128)(2,1)S(1)}, u32[]{:S(2)}, u32[]{:S(2)}) collective-permute-start(bf16[256,128]{0,1:T(8,128)(2,1)S(1)} %get-tuple-element.51), channel_id=1, source_target_pairs={{0,48},{2,8},{6,56},{4,0},{8,57},{10,1},{14,17},{12,9},{18,34},{16... | collective-permute-start | bytes 196616 | tf_op jit(solution)/shard_map/ppermute | solution.py:40
  346.8 12.2 %collective-permute-start.77 = (bf16[256,128]{0,1:T(8,128)(2,1)S(1)}, bf16[256,128]{0,1:T(8,128)(2,1)S(1)}, u32[]{:S(2)}, u32[]{:S(2)}) collective-permute-start(bf16[256,128]{0,1:T(8,128)(2,1)S(1)} %get-tuple-element.51), channel_id=1, source_target_pairs={{1,32},{3,24},{7,40},{5,16},{9,41},{11,33},{15,49},{13,25},{19,50}... | collective-permute-start | bytes 196616 | tf_op jit(solution)/shard_map/ppermute | solution.py:40
  365.3 9.6 %collective-permute-start.81 = (f32[256,128]{0,1:T(8,128)S(1)}, f32[256,128]{0,1:T(8,128)S(1)}, u32[]{:S(2)}, u32[]{:S(2)}) collective-permute-start(f32[256,128]{0,1:T(8,128)S(1)} %dynamic-slice_add_fusion), channel_id=1, source_target_pairs={{0,4},{1,5},{2,6},{3,7},{4,0},{5,1},{6,2},{7,3},{8,12},{9,13},{10,... | collective-permute-start | bytes 393224 | tf_op jit(solution)/shard_map/ppermute | solution.py:53
  (58 other events, 742.4 us)

commit v2 on v0

--- a/solution.py
+++ b/solution.py
@@ -119,8 +119,7 @@
         ys.append(solved)
         segs.append(to_columns(join_halves(solved.astype(bf16), ncol), n))
 
-    coupling = jnp.stack([products([lm[t, j] for j in range(levels)], segs) for t in range(tops)], 0)
-    coupling = column_total(coupling, ncol, leaves)
+    coupling = [column_total(products([lm[t, j] for j in range(levels)], segs), ncol, leaves) for t in range(tops)]
 
     yts = []
     tsegs = []

time: 327 us -> 324 us (level)
  waiting for transfers between devices: 185 us -> 162 us
  starting transfers between devices: 97.1 us -> 110 us
  local copies, waits for them, and re-layouts: 10 us -> 13.6 us
    ppermute x33 -> x39, starting transfers between devices: 57 us -> 82.5 us  [group_sum(): lax.ppermute(x, axis, [(i, i ^ step * k) for i in range(n)])]
    ppermute x33 -> x39, waiting for transfers between devices: 92.9 us -> 78.1 us  [group_sum(): lax.ppermute(x, axis, [(i, i ^ step * k) for i in range(n)])]
    ppermute x10, starting transfers between devices: 15.2 us -> 6.23 us  [to_columns(): return lax.ppermute(x, GRID, pairs)]
    ppermute x10, waiting for transfers between devices: 70.9 us -> 63.9 us  [to_columns(): return lax.ppermute(x, GRID, pairs)]
    ppermute x10 -> x11, starting transfers between devices: 24.7 us -> 20.7 us  [column_total(): lax.ppermute(give_half, 'col', [(i, i ^ 1) for i in range(n)])]
    unnamed x69 -> x75, local copies, waits for them, and re-layouts: 5.96 us -> 7.92 us
    ppermute x10 -> x11, waiting for transfers between devices: 10.4 us -> 8.53 us  [column_total(): lax.ppermute(give_half, 'col', [(i, i ^ 1) for i in range(n)])]
  transfers between devices with their start and end apart: 63 -> 70, of which waited for: 60 -> 57; matrix products, arithmetic and copies ran while one was open for 4% -> 6% of each run, Pallas kernels for 0% -> 0%
where the time goes in v2:
time: 324 us; the launch traced here: 319 us
  waiting for transfers between devices  162 us (50%)
  starting transfers between devices  110 us (34%)
  matrix products  19.6 us (6%)
  local copies, waits for them, and re-layouts  13.6 us (4%)
  other arithmetic  12.8 us (4%)
    ppermute x39, starting transfers between devices, group_sum(): lax.ppermute(x, axis, [(i, i ^ step * k) for i in range(n)])  82.5 us
    ppermute x39, waiting for transfers between devices, group_sum(): lax.ppermute(x, axis, [(i, i ^ step * k) for i in range(n)])  78.1 us
    ppermute x10, waiting for transfers between devices, to_columns(): return lax.ppermute(x, GRID, pairs)  63.9 us
    ppermute x11, starting transfers between devices, column_total(): lax.ppermute(give_half, 'col', [(i, i ^ 1) for i in range(n)])  20.7 us
    ppermute x10, waiting for transfers between devices, join_halves(): other = lax.ppermute(mine, 'col', [(i, i ^ 1) for i in range(n)])  11 us
    ppermute x11, waiting for transfers between devices, column_total(): lax.ppermute(give_half, 'col', [(i, i ^ 1) for i in range(n)])  8.53 us
    unnamed x75, local copies, waits for them, and re-layouts  7.92 us
  transfers between devices with their start and end apart: 70, of which 57 were waited for; matrix products, arithmetic and copies ran while one was open for 6% of the time, Pallas kernels for 0%

profile of v2, /device:TPU:96, one launch (start us, length us, event | category | flops | bytes accessed | tf_op | source)
XLA Modules:
  0.0 319.3 jit_solution(9921507327360707074)
XLA Ops:
  6.0 4.4 %collective-permute-start.1 = (bf16[256,256]{0,1:T(8,128)(2,1)S(1)}, bf16[256,256]{0,1:T(8,128)(2,1)S(1)}, u32[]{:S(2)}, u32[]{:S(2)}) collective-permute-start(bf16[256,256]{0,1:T(8,128)(2,1)S(1)} %pad_maximum_fusion.1), channel_id=1, source_target_pairs={{0,32},{1,24},{2,40},{6,16},{3,48},{7,8},{4,56},{5,0},{9,41},{8,33... | collective-permute-start | bytes 393224 | tf_op jit(solution)/shard_map/ppermute | solution.py:24
  12.2 6.2 %collective-permute-done.1 = bf16[256,256]{0,1:T(8,128)(2,1)S(1)} collective-permute-done((bf16[256,256]{0,1:T(8,128)(2,1)S(1)}, bf16[256,256]{0,1:T(8,128)(2,1)S(1)}, u32[]{:S(2)}, u32[]{:S(2)}) %collective-permute-start.1) | collective-permute-done | bytes 131104 | tf_op jit(solution)/shard_map/ppermute | solution.py:24
  20.1 7.5 %collective-permute-start.4 = (f32[256,128]{1,0:T(8,128)S(1)}, f32[256,128]{1,0:T(8,128)S(1)}, u32[]{:S(2)}, u32[]{:S(2)}) collective-permute-start(f32[256,128]{1,0:T(8,128)S(1)} %dynamic-slice_add_fusion.10), channel_id=1, source_target_pairs={{0,4},{1,5},{2,6},{3,7},{4,0},{5,1},{6,2},{7,3},{8,12},{9,13},{10,... | collective-permute-start | bytes 393224 | tf_op jit(solution)/shard_map/ppermute | solution.py:34
  28.5 5.6 %collective-permute-done.4 = f32[256,128]{1,0:T(8,128)S(1)} collective-permute-done((f32[256,128]{1,0:T(8,128)S(1)}, f32[256,128]{1,0:T(8,128)S(1)}, u32[]{:S(2)}, u32[]{:S(2)}) %collective-permute-start.4) | collective-permute-done | bytes 131104 | tf_op jit(solution)/shard_map/ppermute | solution.py:34
  34.1 2.2 collective-permute-done.5
  39.9 6.3 %collective-permute-done.7 = bf16[256,256]{0,1:T(8,128)(2,1)S(1)} collective-permute-done((bf16[256,256]{0,1:T(8,128)(2,1)S(1)}, bf16[256,256]{0,1:T(8,128)(2,1)S(1)}, u32[]{:S(2)}, u32[]{:S(2)}) %collective-permute-start.7) | collective-permute-done | bytes 131104 | tf_op jit(solution)/shard_map/ppermute | solution.py:24
  49.6 4.0 %collective-permute-start.11 = (f32[256,128]{1,0:T(8,128)S(1)}, f32[256,128]{1,0:T(8,128)S(1)}, u32[]{:S(2)}, u32[]{:S(2)}) collective-permute-start(f32[256,128]{1,0:T(8,128)S(1)} %dynamic-slice_add_fusion.9), channel_id=1, source_target_pairs={{0,6},{1,7},{2,4},{3,5},{4,2},{5,3},{6,0},{7,1},{8,14},{9,15},{10,... | collective-permute-start | bytes 393224 | tf_op jit(solution)/shard_map/ppermute | solution.py:34
  56.6 2.9 collective-permute-done.11
  64.2 6.9 %collective-permute-done.13 = bf16[256,256]{0,1:T(8,128)(2,1)S(1)} collective-permute-done((bf16[256,256]{0,1:T(8,128)(2,1)S(1)}, bf16[256,256]{0,1:T(8,128)(2,1)S(1)}, u32[]{:S(2)}, u32[]{:S(2)}) %collective-permute-start.13) | collective-permute-done | bytes 131104 | tf_op jit(solution)/shard_map/ppermute | solution.py:24
  72.7 3.4 %collective-permute-start.14 = (f32[256,128]{1,0:T(8,128)S(1)}, f32[256,128]{1,0:T(8,128)S(1)}, u32[]{:S(2)}, u32[]{:S(2)}) collective-permute-start(f32[256,128]{1,0:T(8,128)S(1)} %constant_dynamic-slice_fusion.9), channel_id=1, source_target_pairs={{0,1},{1,0},{2,3},{3,2},{4,5},{5,4},{6,7},{7,6},{8,9},{9,8},{10,11... | collective-permute-start | bytes 393224 | tf_op jit(solution)/shard_map/ppermute | solution.py:43
  77.2 5.6 %collective-permute-start.16 = (f32[256,128]{1,0:T(8,128)S(1)}, f32[256,128]{1,0:T(8,128)}, u32[]{:S(2)}, u32[]{:S(2)}) collective-permute-start(f32[256,128]{1,0:T(8,128)S(1)} %dynamic-slice_add_fusion.8), channel_id=1, source_target_pairs={{0,4},{1,5},{2,6},{3,7},{4,0},{5,1},{6,2},{7,3},{8,12},{9,13},{10,... | collective-permute-start | bytes 393224 | tf_op jit(solution)/shard_map/ppermute | solution.py:34
  85.2 4.0 %collective-permute-done.16 = f32[256,128]{1,0:T(8,128)} collective-permute-done((f32[256,128]{1,0:T(8,128)S(1)}, f32[256,128]{1,0:T(8,128)}, u32[]{:S(2)}, u32[]{:S(2)}) %collective-permute-start.16) | collective-permute-done | bytes 131104 | tf_op jit(solution)/shard_map/ppermute | solution.py:34
  89.2 2.4 collective-permute-done.17
  95.2 6.7 %collective-permute-done.19 = bf16[256,256]{0,1:T(8,128)(2,1)S(1)} collective-permute-done((bf16[256,256]{0,1:T(8,128)(2,1)S(1)}, bf16[256,256]{0,1:T(8,128)(2,1)S(1)}, u32[]{:S(2)}, u32[]{:S(2)}) %collective-permute-start.19) | collective-permute-done | bytes 131104 | tf_op jit(solution)/shard_map/ppermute | solution.py:24
  107.5 4.6 %collective-permute-start.22 = (f32[256,128]{1,0:T(8,128)S(1)}, f32[256,128]{1,0:T(8,128)S(1)}, u32[]{:S(2)}, u32[]{:S(2)}) collective-permute-start(f32[256,128]{1,0:T(8,128)S(1)} %dynamic-slice_add_fusion.7), channel_id=1, source_target_pairs={{0,4},{1,5},{2,6},{3,7},{4,0},{5,1},{6,2},{7,3},{8,12},{9,13},{10,... | collective-permute-start | bytes 393224 | tf_op jit(solution)/shard_map/ppermute | solution.py:34
  113.8 4.6 %collective-permute-done.22 = f32[256,128]{1,0:T(8,128)S(1)} collective-permute-done((f32[256,128]{1,0:T(8,128)S(1)}, f32[256,128]{1,0:T(8,128)S(1)}, u32[]{:S(2)}, u32[]{:S(2)}) %collective-permute-start.22) | collective-permute-done | bytes 131104 | tf_op jit(solution)/shard_map/ppermute | solution.py:34
  118.5 2.2 collective-permute-done.23
  123.0 2.9 collective-permute-start.25
  139.7 2.6 collective-permute-start.30
  142.3 2.5 collective-permute-done.35
  145.1 3.0 collective-permute-start.36
  150.6 8.7 %collective-permute-start.31 = (f32[256,128]{1,0:T(8,128)}, f32[256,128]{1,0:T(8,128)}, u32[]{:S(2)}, u32[]{:S(2)}) collective-permute-start(f32[256,128]{1,0:T(8,128)} %add_add_fusion), channel_id=1, source_target_pairs={{0,64},{64,0},{128,192},{192,128},{1,65},{65,1},{129,193},{193,129... | collective-permute-start | bytes 393224 | tf_op jit(solution)/shard_map/ppermute | solution.py:34
  161.3 2.6 collective-permute-start.33
  166.2 2.7 collective-permute-start.38
  171.0 3.3 %collective-permute-done.38 = f32[256,128]{1,0:T(8,128)} collective-permute-done((f32[256,128]{1,0:T(8,128)}, f32[256,128]{1,0:T(8,128)}, u32[]{:S(2)}, u32[]{:S(2)}) %collective-permute-start.38) | collective-permute-done | bytes 131104 | tf_op jit(solution)/shard_map/ppermute | solution.py:34
  175.9 2.4 bitcast_convert_fusion.4
  180.7 7.0 %collective-permute-done.41 = bf16[256,256]{0,1:T(8,128)(2,1)S(1)} collective-permute-done((bf16[256,256]{0,1:T(8,128)(2,1)S(1)}, bf16[256,256]{0,1:T(8,128)(2,1)S(1)}, u32[]{:S(2)}, u32[]{:S(2)}) %collective-permute-start.41) | collective-permute-done | bytes 131104 | tf_op jit(solution)/shard_map/ppermute | solution.py:24
  192.4 6.5 %collective-permute-start.44 = (f32[256,128]{0,1:T(8,128)}, f32[256,128]{0,1:T(8,128)}, u32[]{:S(2)}, u32[]{:S(2)}) collective-permute-start(f32[256,128]{0,1:T(8,128)} %dynamic-slice_add_fusion.4), channel_id=1, source_target_pairs={{0,4},{1,5},{2,6},{3,7},{4,0},{5,1},{6,2},{7,3},{8,12},{9,13},{10,... | collective-permute-start | bytes 393224 | tf_op jit(solution)/shard_map/ppermute | solution.py:34
  201.5 4.1 %collective-permute-done.44 = f32[256,128]{0,1:T(8,128)} collective-permute-done((f32[256,128]{0,1:T(8,128)}, f32[256,128]{0,1:T(8,128)}, u32[]{:S(2)}, u32[]{:S(2)}) %collective-permute-start.44) | collective-permute-done | bytes 131104 | tf_op jit(solution)/shard_map/ppermute | solution.py:34
  205.7 2.2 collective-permute-done.45
  211.4 7.1 %collective-permute-done.47 = bf16[256,256]{0,1:T(8,128)(2,1)S(1)} collective-permute-done((bf16[256,256]{0,1:T(8,128)(2,1)S(1)}, bf16[256,256]{0,1:T(8,128)(2,1)S(1)}, u32[]{:S(2)}, u32[]{:S(2)}) %collective-permute-start.47) | collective-permute-done | bytes 131104 | tf_op jit(solution)/shard_map/ppermute | solution.py:24
  218.9 2.7 collective-permute-start.48
  222.6 4.7 %collective-permute-start.50 = (f32[256,128]{0,1:T(8,128)S(1)}, f32[256,128]{0,1:T(8,128)S(1)}, u32[]{:S(2)}, u32[]{:S(2)}) collective-permute-start(f32[256,128]{0,1:T(8,128)S(1)} %dynamic-slice_add_fusion.3), channel_id=1, source_target_pairs={{0,4},{1,5},{2,6},{3,7},{4,0},{5,1},{6,2},{7,3},{8,12},{9,13},{10,... | collective-permute-start | bytes 393224 | tf_op jit(solution)/shard_map/ppermute | solution.py:34
  229.0 4.8 %collective-permute-done.50 = f32[256,128]{0,1:T(8,128)S(1)} collective-permute-done((f32[256,128]{0,1:T(8,128)S(1)}, f32[256,128]{0,1:T(8,128)S(1)}, u32[]{:S(2)}, u32[]{:S(2)}) %collective-permute-start.50) | collective-permute-done | bytes 131104 | tf_op jit(solution)/shard_map/ppermute | solution.py:34
  233.7 2.2 collective-permute-done.51
  238.4 6.2 %collective-permute-done.53 = bf16[256,256]{0,1:T(8,128)(2,1)S(1)} collective-permute-done((bf16[256,256]{0,1:T(8,128)(2,1)S(1)}, bf16[256,256]{0,1:T(8,128)(2,1)S(1)}, u32[]{:S(2)}, u32[]{:S(2)}) %collective-permute-start.53) | collective-permute-done | bytes 131104 | tf_op jit(solution)/shard_map/ppermute | solution.py:24
  249.1 6.5 %collective-permute-start.56 = (f32[256,128]{0,1:T(8,128)S(1)}, f32[256,128]{0,1:T(8,128)S(1)}, u32[]{:S(2)}, u32[]{:S(2)}) collective-permute-start(f32[256,128]{0,1:T(8,128)S(1)} %dynamic-slice_add_fusion.2), channel_id=1, source_target_pairs={{0,4},{1,5},{2,6},{3,7},{4,0},{5,1},{6,2},{7,3},{8,12},{9,13},{10,... | collective-permute-start | bytes 393224 | tf_op jit(solution)/shard_map/ppermute | solution.py:34
  255.6 6.4 %collective-permute-done.56 = f32[256,128]{0,1:T(8,128)S(1)} collective-permute-done((f32[256,128]{0,1:T(8,128)S(1)}, f32[256,128]{0,1:T(8,128)S(1)}, u32[]{:S(2)}, u32[]{:S(2)}) %collective-permute-start.56) | collective-permute-done | bytes 131104 | tf_op jit(solution)/shard_map/ppermute | solution.py:34
  262.0 2.2 collective-permute-done.57
  266.5 7.5 %collective-permute-done.59 = bf16[256,256]{0,1:T(8,128)(2,1)S(1)} collective-permute-done((bf16[256,256]{0,1:T(8,128)(2,1)S(1)}, bf16[256,256]{0,1:T(8,128)(2,1)S(1)}, u32[]{:S(2)}, u32[]{:S(2)}) %collective-permute-start.59) | collective-permute-done | bytes 131104 | tf_op jit(solution)/shard_map/ppermute | solution.py:24
  274.4 2.3 collective-permute-start.60
  277.8 4.1 %collective-permute-start.62 = (f32[256,128]{0,1:T(8,128)S(1)}, f32[256,128]{0,1:T(8,128)S(1)}, u32[]{:S(2)}, u32[]{:S(2)}) collective-permute-start(f32[256,128]{0,1:T(8,128)S(1)} %dynamic-slice_add_fusion.1), channel_id=1, source_target_pairs={{0,4},{1,5},{2,6},{3,7},{4,0},{5,1},{6,2},{7,3},{8,12},{9,13},{10,... | collective-permute-start | bytes 393224 | tf_op jit(solution)/shard_map/ppermute | solution.py:34
  284.2 4.2 %collective-permute-done.62 = f32[256,128]{0,1:T(8,128)S(1)} collective-permute-done((f32[256,128]{0,1:T(8,128)S(1)}, f32[256,128]{0,1:T(8,128)S(1)}, u32[]{:S(2)}, u32[]{:S(2)}) %collective-permute-start.62) | collective-permute-done | bytes 131104 | tf_op jit(solution)/shard_map/ppermute | solution.py:34
  288.4 2.2 collective-permute-done.63
  292.4 7.5 %collective-permute-done.65 = bf16[256,256]{0,1:T(8,128)(2,1)S(1)} collective-permute-done((bf16[256,256]{0,1:T(8,128)(2,1)S(1)}, bf16[256,256]{0,1:T(8,128)(2,1)S(1)}, u32[]{:S(2)}, u32[]{:S(2)}) %collective-permute-start.65) | collective-permute-done | bytes 131104 | tf_op jit(solution)/shard_map/ppermute | solution.py:24
  303.7 5.8 %collective-permute-start.68 = (f32[256,128]{0,1:T(8,128)S(1)}, f32[256,128]{0,1:T(8,128)S(1)}, u32[]{:S(2)}, u32[]{:S(2)}) collective-permute-start(f32[256,128]{0,1:T(8,128)S(1)} %dynamic-slice_add_fusion), channel_id=1, source_target_pairs={{0,4},{1,5},{2,6},{3,7},{4,0},{5,1},{6,2},{7,3},{8,12},{9,13},{10,... | collective-permute-start | bytes 393224 | tf_op jit(solution)/shard_map/ppermute | solution.py:34
  310.1 5.8 %collective-permute-done.68 = f32[256,128]{0,1:T(8,128)S(1)} collective-permute-done((f32[256,128]{0,1:T(8,128)S(1)}, f32[256,128]{0,1:T(8,128)S(1)}, u32[]{:S(2)}, u32[]{:S(2)}) %collective-permute-start.68) | collective-permute-done | bytes 131104 | tf_op jit(solution)/shard_map/ppermute | solution.py:34
  315.9 2.2 collective-permute-done.69
  (257 shorter events, 102.8 us)
Async XLA Ops:
  6.0 12.3 %collective-permute-start.1 = (bf16[256,256]{0,1:T(8,128)(2,1)S(1)}, bf16[256,256]{0,1:T(8,128)(2,1)S(1)}, u32[]{:S(2)}, u32[]{:S(2)}) collective-permute-start(bf16[256,256]{0,1:T(8,128)(2,1)S(1)} %pad_maximum_fusion.1), channel_id=1, source_target_pairs={{0,32},{1,24},{2,40},{6,16},{3,48},{7,8},{4,56},{5,0},{9,41},{8,33... | collective-permute-start | bytes 393224 | tf_op jit(solution)/shard_map/ppermute | solution.py:24
  20.0 8.4 %collective-permute-start.3 = (f32[256,128]{1,0:T(8,128)S(1)}, f32[256,128]{1,0:T(8,128)S(1)}, u32[]{:S(2)}, u32[]{:S(2)}) collective-permute-start(f32[256,128]{1,0:T(8,128)S(1)} %dynamic-slice_add_fusion.10), channel_id=1, source_target_pairs={{0,2},{1,3},{2,0},{3,1},{4,6},{5,7},{6,4},{7,5},{8,10},{9,11},{10,... | collective-permute-start | bytes 393224 | tf_op jit(solution)/shard_map/ppermute | solution.py:34
  20.1 14.0 %collective-permute-start.4 = (f32[256,128]{1,0:T(8,128)S(1)}, f32[256,128]{1,0:T(8,128)S(1)}, u32[]{:S(2)}, u32[]{:S(2)}) collective-permute-start(f32[256,128]{1,0:T(8,128)S(1)} %dynamic-slice_add_fusion.10), channel_id=1, source_target_pairs={{0,4},{1,5},{2,6},{3,7},{4,0},{5,1},{6,2},{7,3},{8,12},{9,13},{10,... | collective-permute-start | bytes 393224 | tf_op jit(solution)/shard_map/ppermute | solution.py:34
  27.7 8.7 %collective-permute-start.5 = (f32[256,128]{1,0:T(8,128)S(1)}, f32[256,128]{1,0:T(8,128)S(1)}, u32[]{:S(2)}, u32[]{:S(2)}) collective-permute-start(f32[256,128]{1,0:T(8,128)S(1)} %dynamic-slice_add_fusion.10), channel_id=1, source_target_pairs={{0,6},{1,7},{2,4},{3,5},{4,2},{5,3},{6,0},{7,1},{8,14},{9,15},{10,... | collective-permute-start | bytes 393224 | tf_op jit(solution)/shard_map/ppermute | solution.py:34
  38.8 7.3 %collective-permute-start.7 = (bf16[256,256]{0,1:T(8,128)(2,1)S(1)}, bf16[256,256]{0,1:T(8,128)(2,1)S(1)}, u32[]{:S(2)}, u32[]{:S(2)}) collective-permute-start(bf16[256,256]{0,1:T(8,128)(2,1)S(1)} %pad_maximum_fusion.2), channel_id=1, source_target_pairs={{0,32},{1,24},{2,40},{6,16},{3,48},{7,8},{4,56},{5,0},{9,41},{8,33... | collective-permute-start | bytes 393224 | tf_op jit(solution)/shard_map/ppermute | solution.py:24
  49.1 7.5 %collective-permute-start.10 = (f32[256,128]{1,0:T(8,128)S(1)}, f32[256,128]{1,0:T(8,128)S(1)}, u32[]{:S(2)}, u32[]{:S(2)}) collective-permute-start(f32[256,128]{1,0:T(8,128)S(1)} %dynamic-slice_add_fusion.9), channel_id=1, source_target_pairs={{0,4},{1,5},{2,6},{3,7},{4,0},{5,1},{6,2},{7,3},{8,12},{9,13},{10,... | collective-permute-start | bytes 393224 | tf_op jit(solution)/shard_map/ppermute | solution.py:34
  49.6 9.9 %collective-permute-start.11 = (f32[256,128]{1,0:T(8,128)S(1)}, f32[256,128]{1,0:T(8,128)S(1)}, u32[]{:S(2)}, u32[]{:S(2)}) collective-permute-start(f32[256,128]{1,0:T(8,128)S(1)} %dynamic-slice_add_fusion.9), channel_id=1, source_target_pairs={{0,6},{1,7},{2,4},{3,5},{4,2},{5,3},{6,0},{7,1},{8,14},{9,15},{10,... | collective-permute-start | bytes 393224 | tf_op jit(solution)/shard_map/ppermute | solution.py:34
  53.6 7.1 %collective-permute-start.9 = (f32[256,128]{1,0:T(8,128)S(1)}, f32[256,128]{1,0:T(8,128)S(1)}, u32[]{:S(2)}, u32[]{:S(2)}) collective-permute-start(f32[256,128]{1,0:T(8,128)S(1)} %dynamic-slice_add_fusion.9), channel_id=1, source_target_pairs={{0,2},{1,3},{2,0},{3,1},{4,6},{5,7},{6,4},{7,5},{8,10},{9,11},{10,... | collective-permute-start | bytes 393224 | tf_op jit(solution)/shard_map/ppermute | solution.py:34
  63.3 7.9 %collective-permute-start.13 = (bf16[256,256]{0,1:T(8,128)(2,1)S(1)}, bf16[256,256]{0,1:T(8,128)(2,1)S(1)}, u32[]{:S(2)}, u32[]{:S(2)}) collective-permute-start(bf16[256,256]{0,1:T(8,128)(2,1)S(1)} %pad_maximum_fusion.3), channel_id=1, source_target_pairs={{0,32},{1,24},{2,40},{6,16},{3,48},{7,8},{4,56},{5,0},{9,41},{8,33... | collective-permute-start | bytes 393224 | tf_op jit(solution)/shard_map/ppermute | solution.py:24
  77.1 8.1 %collective-permute-start.15 = (f32[256,128]{1,0:T(8,128)S(1)}, f32[256,128]{1,0:T(8,128)}, u32[]{:S(2)}, u32[]{:S(2)}) collective-permute-start(f32[256,128]{1,0:T(8,128)S(1)} %dynamic-slice_add_fusion.8), channel_id=1, source_target_pairs={{0,2},{1,3},{2,0},{3,1},{4,6},{5,7},{6,4},{7,5},{8,10},{9,11},{10,... | collective-permute-start | bytes 393224 | tf_op jit(solution)/shard_map/ppermute | solution.py:34
  77.2 11.9 %collective-permute-start.16 = (f32[256,128]{1,0:T(8,128)S(1)}, f32[256,128]{1,0:T(8,128)}, u32[]{:S(2)}, u32[]{:S(2)}) collective-permute-start(f32[256,128]{1,0:T(8,128)S(1)} %dynamic-slice_add_fusion.8), channel_id=1, source_target_pairs={{0,4},{1,5},{2,6},{3,7},{4,0},{5,1},{6,2},{7,3},{8,12},{9,13},{10,... | collective-permute-start | bytes 393224 | tf_op jit(solution)/shard_map/ppermute | solution.py:34
  82.9 8.7 %collective-permute-start.17 = (f32[256,128]{1,0:T(8,128)S(1)}, f32[256,128]{1,0:T(8,128)}, u32[]{:S(2)}, u32[]{:S(2)}) collective-permute-start(f32[256,128]{1,0:T(8,128)S(1)} %dynamic-slice_add_fusion.8), channel_id=1, source_target_pairs={{0,6},{1,7},{2,4},{3,5},{4,2},{5,3},{6,0},{7,1},{8,14},{9,15},{10,... | collective-permute-start | bytes 393224 | tf_op jit(solution)/shard_map/ppermute | solution.py:34
  94.3 7.6 %collective-permute-start.19 = (bf16[256,256]{0,1:T(8,128)(2,1)S(1)}, bf16[256,256]{0,1:T(8,128)(2,1)S(1)}, u32[]{:S(2)}, u32[]{:S(2)}) collective-permute-start(bf16[256,256]{0,1:T(8,128)(2,1)S(1)} %pad_maximum_fusion.4), channel_id=1, source_target_pairs={{0,32},{1,24},{2,40},{6,16},{3,48},{7,8},{4,56},{5,0},{9,41},{8,33... | collective-permute-start | bytes 393224 | tf_op jit(solution)/shard_map/ppermute | solution.py:24
  107.4 6.5 %collective-permute-start.21 = (f32[256,128]{1,0:T(8,128)S(1)}, f32[256,128]{1,0:T(8,128)S(1)}, u32[]{:S(2)}, u32[]{:S(2)}) collective-permute-start(f32[256,128]{1,0:T(8,128)S(1)} %dynamic-slice_add_fusion.7), channel_id=1, source_target_pairs={{0,2},{1,3},{2,0},{3,1},{4,6},{5,7},{6,4},{7,5},{8,10},{9,11},{10,... | collective-permute-start | bytes 393224 | tf_op jit(solution)/shard_map/ppermute | solution.py:34
  107.5 11.0 %collective-permute-start.22 = (f32[256,128]{1,0:T(8,128)S(1)}, f32[256,128]{1,0:T(8,128)S(1)}, u32[]{:S(2)}, u32[]{:S(2)}) collective-permute-start(f32[256,128]{1,0:T(8,128)S(1)} %dynamic-slice_add_fusion.7), channel_id=1, source_target_pairs={{0,4},{1,5},{2,6},{3,7},{4,0},{5,1},{6,2},{7,3},{8,12},{9,13},{10,... | collective-permute-start | bytes 393224 | tf_op jit(solution)/shard_map/ppermute | solution.py:34
  112.0 8.7 %collective-permute-start.23 = (f32[256,128]{1,0:T(8,128)S(1)}, f32[256,128]{1,0:T(8,128)S(1)}, u32[]{:S(2)}, u32[]{:S(2)}) collective-permute-start(f32[256,128]{1,0:T(8,128)S(1)} %dynamic-slice_add_fusion.7), channel_id=1, source_target_pairs={{0,6},{1,7},{2,4},{3,5},{4,2},{5,3},{6,0},{7,1},{8,14},{9,15},{10,... | collective-permute-start | bytes 393224 | tf_op jit(solution)/shard_map/ppermute | solution.py:34
  121.4 8.8 %collective-permute-start.24 = (f32[256,128]{1,0:T(8,128)}, f32[256,128]{1,0:T(8,128)}, u32[]{:S(2)}, u32[]{:S(2)}) collective-permute-start(f32[256,128]{1,0:T(8,128)} %add_add_fusion.1), channel_id=1, source_target_pairs={{0,64},{64,0},{128,192},{192,128},{1,65},{65,1},{129,193},{193,129... | collective-permute-start | bytes 393224 | tf_op jit(solution)/shard_map/ppermute | solution.py:34
  123.0 9.0 %collective-permute-start.25 = (f32[256,128]{1,0:T(8,128)}, f32[256,128]{1,0:T(8,128)}, u32[]{:S(2)}, u32[]{:S(2)}) collective-permute-start(f32[256,128]{1,0:T(8,128)} %add_add_fusion.1), channel_id=1, source_target_pairs={{0,128},{64,192},{128,0},{192,64},{1,129},{65,193},{129,1},{193,65... | collective-permute-start | bytes 393224 | tf_op jit(solution)/shard_map/ppermute | solution.py:34
  125.9 8.1 %collective-permute-start.26 = (f32[256,128]{1,0:T(8,128)}, f32[256,128]{1,0:T(8,128)}, u32[]{:S(2)}, u32[]{:S(2)}) collective-permute-start(f32[256,128]{1,0:T(8,128)} %add_add_fusion.1), channel_id=1, source_target_pairs={{0,192},{64,128},{128,64},{192,0},{1,193},{65,129},{129,65},{193,1... | collective-permute-start | bytes 393224 | tf_op jit(solution)/shard_map/ppermute | solution.py:34
  137.2 7.6 %collective-permute-start.35 = (bf16[256,256]{0,1:T(8,128)(2,1)S(1)}, bf16[256,256]{0,1:T(8,128)(2,1)S(1)}, u32[]{:S(2)}, u32[]{:S(2)}) collective-permute-start(bf16[256,256]{0,1:T(8,128)(2,1)S(1)} %pad_maximum_fusion.5), channel_id=1, source_target_pairs={{0,32},{1,24},{2,40},{6,16},{3,48},{7,8},{4,56},{5,0},{9,41},{8,33... | collective-permute-start | bytes 393224 | tf_op jit(solution)/shard_map/ppermute | solution.py:24
  137.5 10.6 %collective-permute-start.28 = (f32[256,128]{1,0:T(8,128)S(1)}, f32[256,128]{1,0:T(8,128)S(1)}, u32[]{:S(2)}, u32[]{:S(2)}) collective-permute-start(f32[256,128]{1,0:T(8,128)S(1)} %dynamic-slice_add_fusion.6), channel_id=1, source_target_pairs={{0,2},{1,3},{2,0},{3,1},{4,6},{5,7},{6,4},{7,5},{8,10},{9,11},{10,... | collective-permute-start | bytes 393224 | tf_op jit(solution)/shard_map/ppermute | solution.py:34
  137.6 10.5 %collective-permute-start.29 = (f32[256,128]{1,0:T(8,128)S(1)}, f32[256,128]{1,0:T(8,128)S(1)}, u32[]{:S(2)}, u32[]{:S(2)}) collective-permute-start(f32[256,128]{1,0:T(8,128)S(1)} %dynamic-slice_add_fusion.6), channel_id=1, source_target_pairs={{0,4},{1,5},{2,6},{3,7},{4,0},{5,1},{6,2},{7,3},{8,12},{9,13},{10,... | collective-permute-start | bytes 393224 | tf_op jit(solution)/shard_map/ppermute | solution.py:34
  139.7 10.2 %collective-permute-start.30 = (f32[256,128]{1,0:T(8,128)S(1)}, f32[256,128]{1,0:T(8,128)S(1)}, u32[]{:S(2)}, u32[]{:S(2)}) collective-permute-start(f32[256,128]{1,0:T(8,128)S(1)} %dynamic-slice_add_fusion.6), channel_id=1, source_target_pairs={{0,6},{1,7},{2,4},{3,5},{4,2},{5,3},{6,0},{7,1},{8,14},{9,15},{10,... | collective-permute-start | bytes 393224 | tf_op jit(solution)/shard_map/ppermute | solution.py:34
  145.1 18.9 %collective-permute-start.36 = (f32[256,128]{1,0:T(8,128)S(1)}, f32[256,128]{1,0:T(8,128)S(1)}, u32[]{:S(2)}, u32[]{:S(2)}) collective-permute-start(f32[256,128]{1,0:T(8,128)S(1)} %constant_dynamic-slice_fusion.6), channel_id=1, source_target_pairs={{0,1},{1,0},{2,3},{3,2},{4,5},{5,4},{6,7},{7,6},{8,9},{9,8},{10,11... | collective-permute-start | bytes 393224 | tf_op jit(solution)/shard_map/ppermute | solution.py:43
  150.6 18.3 %collective-permute-start.31 = (f32[256,128]{1,0:T(8,128)}, f32[256,128]{1,0:T(8,128)}, u32[]{:S(2)}, u32[]{:S(2)}) collective-permute-start(f32[256,128]{1,0:T(8,128)} %add_add_fusion), channel_id=1, source_target_pairs={{0,64},{64,0},{128,192},{192,128},{1,65},{65,1},{129,193},{193,129... | collective-permute-start | bytes 393224 | tf_op jit(solution)/shard_map/ppermute | solution.py:34
  159.3 11.7 %collective-permute-start.32 = (f32[256,128]{1,0:T(8,128)}, f32[256,128]{1,0:T(8,128)}, u32[]{:S(2)}, u32[]{:S(2)}) collective-permute-start(f32[256,128]{1,0:T(8,128)} %add_add_fusion), channel_id=1, source_target_pairs={{0,128},{64,192},{128,0},{192,64},{1,129},{65,193},{129,1},{193,65... | collective-permute-start | bytes 393224 | tf_op jit(solution)/shard_map/ppermute | solution.py:34
  161.3 9.7 %collective-permute-start.33 = (f32[256,128]{1,0:T(8,128)}, f32[256,128]{1,0:T(8,128)}, u32[]{:S(2)}, u32[]{:S(2)}) collective-permute-start(f32[256,128]{1,0:T(8,128)} %add_add_fusion), channel_id=1, source_target_pairs={{0,192},{64,128},{128,64},{192,0},{1,193},{65,129},{129,65},{193,1... | collective-permute-start | bytes 393224 | tf_op jit(solution)/shard_map/ppermute | solution.py:34
  166.2 8.1 %collective-permute-start.38 = (f32[256,128]{1,0:T(8,128)}, f32[256,128]{1,0:T(8,128)}, u32[]{:S(2)}, u32[]{:S(2)}) collective-permute-start(f32[256,128]{1,0:T(8,128)} %dynamic-slice_add_fusion.5), channel_id=1, source_target_pairs={{0,4},{1,5},{2,6},{3,7},{4,0},{5,1},{6,2},{7,3},{8,12},{9,13},{10,... | collective-permute-start | bytes 393224 | tf_op jit(solution)/shard_map/ppermute | solution.py:34
  168.9 7.0 %collective-permute-start.39 = (f32[256,128]{1,0:T(8,128)}, f32[256,128]{1,0:T(8,128)}, u32[]{:S(2)}, u32[]{:S(2)}) collective-permute-start(f32[256,128]{1,0:T(8,128)} %dynamic-slice_add_fusion.5), channel_id=1, source_target_pairs={{0,6},{1,7},{2,4},{3,5},{4,2},{5,3},{6,0},{7,1},{8,14},{9,15},{10,... | collective-permute-start | bytes 393224 | tf_op jit(solution)/shard_map/ppermute | solution.py:34
  180.6 7.1 %collective-permute-start.41 = (bf16[256,256]{0,1:T(8,128)(2,1)S(1)}, bf16[256,256]{0,1:T(8,128)(2,1)S(1)}, u32[]{:S(2)}, u32[]{:S(2)}) collective-permute-start(bf16[256,256]{0,1:T(8,128)(2,1)S(1)} %pad_maximum_fusion.6), channel_id=1, source_target_pairs={{0,32},{1,24},{2,40},{6,16},{3,48},{7,8},{4,56},{5,0},{9,41},{8,33... | collective-permute-start | bytes 393224 | tf_op jit(solution)/shard_map/ppermute | solution.py:24
  191.3 10.3 %collective-permute-start.43 = (f32[256,128]{0,1:T(8,128)}, f32[256,128]{0,1:T(8,128)}, u32[]{:S(2)}, u32[]{:S(2)}) collective-permute-start(f32[256,128]{0,1:T(8,128)} %dynamic-slice_add_fusion.4), channel_id=1, source_target_pairs={{0,2},{1,3},{2,0},{3,1},{4,6},{5,7},{6,4},{7,5},{8,10},{9,11},{10,... | collective-permute-start | bytes 393224 | tf_op jit(solution)/shard_map/ppermute | solution.py:34
  192.4 13.3 %collective-permute-start.44 = (f32[256,128]{0,1:T(8,128)}, f32[256,128]{0,1:T(8,128)}, u32[]{:S(2)}, u32[]{:S(2)}) collective-permute-start(f32[256,128]{0,1:T(8,128)} %dynamic-slice_add_fusion.4), channel_id=1, source_target_pairs={{0,4},{1,5},{2,6},{3,7},{4,0},{5,1},{6,2},{7,3},{8,12},{9,13},{10,... | collective-permute-start | bytes 393224 | tf_op jit(solution)/shard_map/ppermute | solution.py:34
  198.9 9.0 %collective-permute-start.45 = (f32[256,128]{0,1:T(8,128)}, f32[256,128]{0,1:T(8,128)}, u32[]{:S(2)}, u32[]{:S(2)}) collective-permute-start(f32[256,128]{0,1:T(8,128)} %dynamic-slice_add_fusion.4), channel_id=1, source_target_pairs={{0,6},{1,7},{2,4},{3,5},{4,2},{5,3},{6,0},{7,1},{8,14},{9,15},{10,... | collective-permute-start | bytes 393224 | tf_op jit(solution)/shard_map/ppermute | solution.py:34
  211.3 7.3 %collective-permute-start.47 = (bf16[256,256]{0,1:T(8,128)(2,1)S(1)}, bf16[256,256]{0,1:T(8,128)(2,1)S(1)}, u32[]{:S(2)}, u32[]{:S(2)}) collective-permute-start(bf16[256,256]{0,1:T(8,128)(2,1)S(1)} %pad_maximum_fusion.7), channel_id=1, source_target_pairs={{0,32},{1,24},{2,40},{6,16},{3,48},{7,8},{4,56},{5,0},{9,41},{8,33... | collective-permute-start | bytes 393224 | tf_op jit(solution)/shard_map/ppermute | solution.py:24
  222.5 6.5 %collective-permute-start.49 = (f32[256,128]{0,1:T(8,128)S(1)}, f32[256,128]{0,1:T(8,128)S(1)}, u32[]{:S(2)}, u32[]{:S(2)}) collective-permute-start(f32[256,128]{0,1:T(8,128)S(1)} %dynamic-slice_add_fusion.3), channel_id=1, source_target_pairs={{0,2},{1,3},{2,0},{3,1},{4,6},{5,7},{6,4},{7,5},{8,10},{9,11},{10,... | collective-permute-start | bytes 393224 | tf_op jit(solution)/shard_map/ppermute | solution.py:34
  222.6 11.1 %collective-permute-start.50 = (f32[256,128]{0,1:T(8,128)S(1)}, f32[256,128]{0,1:T(8,128)S(1)}, u32[]{:S(2)}, u32[]{:S(2)}) collective-permute-start(f32[256,128]{0,1:T(8,128)S(1)} %dynamic-slice_add_fusion.3), channel_id=1, source_target_pairs={{0,4},{1,5},{2,6},{3,7},{4,0},{5,1},{6,2},{7,3},{8,12},{9,13},{10,... | collective-permute-start | bytes 393224 | tf_op jit(solution)/shard_map/ppermute | solution.py:34
  227.3 8.7 %collective-permute-start.51 = (f32[256,128]{0,1:T(8,128)S(1)}, f32[256,128]{0,1:T(8,128)S(1)}, u32[]{:S(2)}, u32[]{:S(2)}) collective-permute-start(f32[256,128]{0,1:T(8,128)S(1)} %dynamic-slice_add_fusion.3), channel_id=1, source_target_pairs={{0,6},{1,7},{2,4},{3,5},{4,2},{5,3},{6,0},{7,1},{8,14},{9,15},{10,... | collective-permute-start | bytes 393224 | tf_op jit(solution)/shard_map/ppermute | solution.py:34
  238.1 6.5 %collective-permute-start.53 = (bf16[256,256]{0,1:T(8,128)(2,1)S(1)}, bf16[256,256]{0,1:T(8,128)(2,1)S(1)}, u32[]{:S(2)}, u32[]{:S(2)}) collective-permute-start(bf16[256,256]{0,1:T(8,128)(2,1)S(1)} %pad_maximum_fusion.8), channel_id=1, source_target_pairs={{0,32},{1,24},{2,40},{6,16},{3,48},{7,8},{4,56},{5,0},{9,41},{8,33... | collective-permute-start | bytes 393224 | tf_op jit(solution)/shard_map/ppermute | solution.py:24
  247.1 8.5 %collective-permute-start.55 = (f32[256,128]{0,1:T(8,128)S(1)}, f32[256,128]{0,1:T(8,128)S(1)}, u32[]{:S(2)}, u32[]{:S(2)}) collective-permute-start(f32[256,128]{0,1:T(8,128)S(1)} %dynamic-slice_add_fusion.2), channel_id=1, source_target_pairs={{0,2},{1,3},{2,0},{3,1},{4,6},{5,7},{6,4},{7,5},{8,10},{9,11},{10,... | collective-permute-start | bytes 393224 | tf_op jit(solution)/shard_map/ppermute | solution.py:34
  249.1 12.9 %collective-permute-start.56 = (f32[256,128]{0,1:T(8,128)S(1)}, f32[256,128]{0,1:T(8,128)S(1)}, u32[]{:S(2)}, u32[]{:S(2)}) collective-permute-start(f32[256,128]{0,1:T(8,128)S(1)} %dynamic-slice_add_fusion.2), channel_id=1, source_target_pairs={{0,4},{1,5},{2,6},{3,7},{4,0},{5,1},{6,2},{7,3},{8,12},{9,13},{10,... | collective-permute-start | bytes 393224 | tf_op jit(solution)/shard_map/ppermute | solution.py:34
  255.6 8.7 %collective-permute-start.57 = (f32[256,128]{0,1:T(8,128)S(1)}, f32[256,128]{0,1:T(8,128)S(1)}, u32[]{:S(2)}, u32[]{:S(2)}) collective-permute-start(f32[256,128]{0,1:T(8,128)S(1)} %dynamic-slice_add_fusion.2), channel_id=1, source_target_pairs={{0,6},{1,7},{2,4},{3,5},{4,2},{5,3},{6,0},{7,1},{8,14},{9,15},{10,... | collective-permute-start | bytes 393224 | tf_op jit(solution)/shard_map/ppermute | solution.py:34
  266.4 7.6 %collective-permute-start.59 = (bf16[256,256]{0,1:T(8,128)(2,1)S(1)}, bf16[256,256]{0,1:T(8,128)(2,1)S(1)}, u32[]{:S(2)}, u32[]{:S(2)}) collective-permute-start(bf16[256,256]{0,1:T(8,128)(2,1)S(1)} %pad_maximum_fusion.9), channel_id=1, source_target_pairs={{0,32},{1,24},{2,40},{6,16},{3,48},{7,8},{4,56},{5,0},{9,41},{8,33... | collective-permute-start | bytes 393224 | tf_op jit(solution)/shard_map/ppermute | solution.py:24
  277.8 10.6 %collective-permute-start.62 = (f32[256,128]{0,1:T(8,128)S(1)}, f32[256,128]{0,1:T(8,128)S(1)}, u32[]{:S(2)}, u32[]{:S(2)}) collective-permute-start(f32[256,128]{0,1:T(8,128)S(1)} %dynamic-slice_add_fusion.1), channel_id=1, source_target_pairs={{0,4},{1,5},{2,6},{3,7},{4,0},{5,1},{6,2},{7,3},{8,12},{9,13},{10,... | collective-permute-start | bytes 393224 | tf_op jit(solution)/shard_map/ppermute | solution.py:34
  282.0 8.7 %collective-permute-start.63 = (f32[256,128]{0,1:T(8,128)S(1)}, f32[256,128]{0,1:T(8,128)S(1)}, u32[]{:S(2)}, u32[]{:S(2)}) collective-permute-start(f32[256,128]{0,1:T(8,128)S(1)} %dynamic-slice_add_fusion.1), channel_id=1, source_target_pairs={{0,6},{1,7},{2,4},{3,5},{4,2},{5,3},{6,0},{7,1},{8,14},{9,15},{10,... | collective-permute-start | bytes 393224 | tf_op jit(solution)/shard_map/ppermute | solution.py:34
  292.3 7.6 %collective-permute-start.65 = (bf16[256,256]{0,1:T(8,128)(2,1)S(1)}, bf16[256,256]{0,1:T(8,128)(2,1)S(1)}, u32[]{:S(2)}, u32[]{:S(2)}) collective-permute-start(bf16[256,256]{0,1:T(8,128)(2,1)S(1)} %pad_maximum_fusion.10), channel_id=1, source_target_pairs={{0,32},{1,24},{2,40},{6,16},{3,48},{7,8},{4,56},{5,0},{9,41},{8,33... | collective-permute-start | bytes 393224 | tf_op jit(solution)/shard_map/ppermute | solution.py:24
  303.6 6.6 %collective-permute-start.67 = (f32[256,128]{0,1:T(8,128)S(1)}, f32[256,128]{0,1:T(8,128)S(1)}, u32[]{:S(2)}, u32[]{:S(2)}) collective-permute-start(f32[256,128]{0,1:T(8,128)S(1)} %dynamic-slice_add_fusion), channel_id=1, source_target_pairs={{0,2},{1,3},{2,0},{3,1},{4,6},{5,7},{6,4},{7,5},{8,10},{9,11},{10,... | collective-permute-start | bytes 393224 | tf_op jit(solution)/shard_map/ppermute | solution.py:34
  303.7 12.3 %collective-permute-start.68 = (f32[256,128]{0,1:T(8,128)S(1)}, f32[256,128]{0,1:T(8,128)S(1)}, u32[]{:S(2)}, u32[]{:S(2)}) collective-permute-start(f32[256,128]{0,1:T(8,128)S(1)} %dynamic-slice_add_fusion), channel_id=1, source_target_pairs={{0,4},{1,5},{2,6},{3,7},{4,0},{5,1},{6,2},{7,3},{8,12},{9,13},{10,... | collective-permute-start | bytes 393224 | tf_op jit(solution)/shard_map/ppermute | solution.py:34
  309.5 8.7 %collective-permute-start.69 = (f32[256,128]{0,1:T(8,128)S(1)}, f32[256,128]{0,1:T(8,128)S(1)}, u32[]{:S(2)}, u32[]{:S(2)}) collective-permute-start(f32[256,128]{0,1:T(8,128)S(1)} %dynamic-slice_add_fusion), channel_id=1, source_target_pairs={{0,6},{1,7},{2,4},{3,5},{4,2},{5,3},{6,0},{7,1},{8,14},{9,15},{10,... | collective-permute-start | bytes 393224 | tf_op jit(solution)/shard_map/ppermute | solution.py:34
  (50 other events, 455.4 us)

commit v3 on v2

--- a/solution.py
+++ b/solution.py
@@ -45,6 +45,22 @@
     if leaves:
         mine = group_sum(mine, "leaf", leaves)
     return mine
+
+
+def column_chunk_total(x, n):
+    core = lax.axis_index("col") % 2
+    chip = lax.axis_index("col") // 2
+    half = x.shape[-1] // 2
+    keep_half = lax.dynamic_slice_in_dim(x, core * half, half, x.ndim - 1)
+    give_half = lax.dynamic_slice_in_dim(x, (1 - core) * half, half, x.ndim - 1)
+    mine = keep_half + lax.ppermute(give_half, "col", [(i, i ^ 1) for i in range(n)])
+    chips = n // 2
+    chunk = half // chips
+    got = [lax.dynamic_slice_in_dim(mine, chip * chunk, chunk, x.ndim - 1)]
+    for k in range(1, chips):
+        piece = lax.dynamic_slice_in_dim(mine, (chip ^ k) * chunk, chunk, x.ndim - 1)
+        got.append(lax.ppermute(piece, "col", [(i, i ^ (2 * k)) for i in range(n)]))
+    return tree_sum(got)
 
 
 def join_halves(mine, n):
@@ -150,14 +166,18 @@
     for level in reversed(range(levels)):
         blocks = [um[level, t] for t in range(tops)] + [fm[level, j] for j in range(level + 1, levels)]
         part = products(blocks, tback + back[level + 1 :])
-        resid = (ys[level] - column_total(part, ncol)).astype(bf16)
+        if level > 0:
+            resid = (ys[level] - column_total(part, ncol)).astype(bf16)
+        else:
+            mine = lax.dynamic_slice_in_dim(ys[level], (lax.axis_index("col") // 2) * share, share, 1)
+            resid = (mine - column_chunk_total(part, ncol)).astype(bf16)
         solved = keep[level] * jnp.dot(inv[1, level], resid, preferred_element_type=f32)
         zs[level] = solved
         if level > 0:
             back[level] = to_columns(join_halves(solved.astype(bf16), ncol), n)
 
     start = (lax.axis_index("col") // 2) * share
-    result = lax.dynamic_slice_in_dim(jnp.stack(zs, 0), start, share, 2)
+    result = jnp.stack([zs[0]] + [lax.dynamic_slice_in_dim(z, start, share, 1) for z in zs[1:]], 0)
     result_top = lax.dynamic_slice_in_dim(jnp.stack(zts, 0), start, share, 2)
     return (result[None, :, None], result_top[:, None])
 

time: 324 us -> 324 us (level)
  waiting for transfers between devices: 162 us -> 154 us
  local copies, waits for them, and re-layouts: 13.6 us -> 19.1 us
    ppermute x39 -> x36, waiting for transfers between devices: 78.1 us -> 68.5 us  [group_sum(): lax.ppermute(x, axis, [(i, i ^ step * k) for i in range(n)])]
    ppermute x0 -> x4, starting transfers between devices: none -> 8.32 us  [the longest x3 4.78 us: column_chunk_total(): got.append(lax.ppermute(piece, 'col', [(i, i ^ 2 * k) for i in range(n)]))]
    ppermute x0 -> x4, waiting for transfers between devices: none -> 5.88 us  [the longest x3 4.9 us: column_chunk_total(): got.append(lax.ppermute(piece, 'col', [(i, i ^ 2 * k) for i in range(n)]))]
    ppermute x11 -> x10, starting transfers between devices: 20.7 us -> 15 us  [column_total(): lax.ppermute(give_half, 'col', [(i, i ^ 1) for i in range(n)])]
    unnamed x75, local copies, waits for them, and re-layouts: 7.92 us -> 12.6 us
    ppermute x39 -> x36, starting transfers between devices: 82.5 us -> 79.3 us  [group_sum(): lax.ppermute(x, axis, [(i, i ^ step * k) for i in range(n)])]
    ppermute x11 -> x10, waiting for transfers between devices: 8.53 us -> 7.31 us  [column_total(): lax.ppermute(give_half, 'col', [(i, i ^ 1) for i in range(n)])]
  transfers between devices with their start and end apart: 70 -> 70, of which waited for: 57 -> 54; matrix products, arithmetic and copies ran while one was open for 6% -> 8% of each run, Pallas kernels for 0% -> 0%
where the time goes in v3:
time: 324 us; the launch traced here: 319 us
  waiting for transfers between devices  154 us (48%)
  starting transfers between devices  109 us (34%)
  matrix products  21.7 us (7%)
  local copies, waits for them, and re-layouts  19.1 us (6%)
  other arithmetic  12.3 us (4%)
    ppermute x36, starting transfers between devices, group_sum(): lax.ppermute(x, axis, [(i, i ^ step * k) for i in range(n)])  79.3 us
    ppermute x36, waiting for transfers between devices, group_sum(): lax.ppermute(x, axis, [(i, i ^ step * k) for i in range(n)])  68.5 us
    ppermute x10, waiting for transfers between devices, to_columns(): return lax.ppermute(x, GRID, pairs)  63.2 us
    ppermute x10, starting transfers between devices, column_total(): lax.ppermute(give_half, 'col', [(i, i ^ 1) for i in range(n)])  15 us
    unnamed x75, local copies, waits for them, and re-layouts  12.6 us
    ppermute x10, waiting for transfers between devices, join_halves(): other = lax.ppermute(mine, 'col', [(i, i ^ 1) for i in range(n)])  9.39 us
    dot_general x11, matrix products, products(): jnp.einsum('jbk,jkr->br', jnp.stack(blocks, 0), jnp.stack(segments, 0), p...  7.62 us
    ppermute x10, waiting for transfers between devices, column_total(): lax.ppermute(give_half, 'col', [(i, i ^ 1) for i in range(n)])  7.31 us
  transfers between devices with their start and end apart: 70, of which 54 were waited for; matrix products, arithmetic and copies ran while one was open for 8% of the time, Pallas kernels for 0%

profile of v3, /device:TPU:96, one launch (start us, length us, event | category | flops | bytes accessed | tf_op | source)
XLA Modules:
  0.0 318.6 jit_solution(12890344374136087646)
XLA Ops:
  5.4 4.4 %collective-permute-start.1 = (bf16[256,256]{0,1:T(8,128)(2,1)S(1)}, bf16[256,256]{0,1:T(8,128)(2,1)S(1)}, u32[]{:S(2)}, u32[]{:S(2)}) collective-permute-start(bf16[256,256]{0,1:T(8,128)(2,1)S(1)} %pad_maximum_fusion.1), channel_id=1, source_target_pairs={{0,32},{1,24},{2,40},{6,16},{3,48},{7,8},{4,56},{5,0},{9,41},{8,33... | collective-permute-start | bytes 393224 | tf_op jit(solution)/shard_map/ppermute | solution.py:24
  11.6 6.2 %collective-permute-done.1 = bf16[256,256]{0,1:T(8,128)(2,1)S(1)} collective-permute-done((bf16[256,256]{0,1:T(8,128)(2,1)S(1)}, bf16[256,256]{0,1:T(8,128)(2,1)S(1)}, u32[]{:S(2)}, u32[]{:S(2)}) %collective-permute-start.1) | collective-permute-done | bytes 131104 | tf_op jit(solution)/shard_map/ppermute | solution.py:24
  19.6 7.5 %collective-permute-start.4 = (f32[256,128]{1,0:T(8,128)S(1)}, f32[256,128]{1,0:T(8,128)S(1)}, u32[]{:S(2)}, u32[]{:S(2)}) collective-permute-start(f32[256,128]{1,0:T(8,128)S(1)} %dynamic-slice_add_fusion.10), channel_id=1, source_target_pairs={{0,4},{1,5},{2,6},{3,7},{4,0},{5,1},{6,2},{7,3},{8,12},{9,13},{10,... | collective-permute-start | bytes 393224 | tf_op jit(solution)/shard_map/ppermute | solution.py:34
  27.9 5.6 %collective-permute-done.4 = f32[256,128]{1,0:T(8,128)S(1)} collective-permute-done((f32[256,128]{1,0:T(8,128)S(1)}, f32[256,128]{1,0:T(8,128)S(1)}, u32[]{:S(2)}, u32[]{:S(2)}) %collective-permute-start.4) | collective-permute-done | bytes 131104 | tf_op jit(solution)/shard_map/ppermute | solution.py:34
  33.6 2.2 collective-permute-done.5
  39.8 6.4 %collective-permute-done.7 = bf16[256,256]{0,1:T(8,128)(2,1)S(1)} collective-permute-done((bf16[256,256]{0,1:T(8,128)(2,1)S(1)}, bf16[256,256]{0,1:T(8,128)(2,1)S(1)}, u32[]{:S(2)}, u32[]{:S(2)}) %collective-permute-start.7) | collective-permute-done | bytes 131104 | tf_op jit(solution)/shard_map/ppermute | solution.py:24
  50.5 4.0 %collective-permute-start.11 = (f32[256,128]{1,0:T(8,128)S(1)}, f32[256,128]{1,0:T(8,128)S(1)}, u32[]{:S(2)}, u32[]{:S(2)}) collective-permute-start(f32[256,128]{1,0:T(8,128)S(1)} %dynamic-slice_add_fusion.9), channel_id=1, source_target_pairs={{0,6},{1,7},{2,4},{3,5},{4,2},{5,3},{6,0},{7,1},{8,14},{9,15},{10,... | collective-permute-start | bytes 393224 | tf_op jit(solution)/shard_map/ppermute | solution.py:34
  57.5 2.9 collective-permute-done.11
  65.8 6.9 %collective-permute-done.13 = bf16[256,256]{0,1:T(8,128)(2,1)S(1)} collective-permute-done((bf16[256,256]{0,1:T(8,128)(2,1)S(1)}, bf16[256,256]{0,1:T(8,128)(2,1)S(1)}, u32[]{:S(2)}, u32[]{:S(2)}) %collective-permute-start.13) | collective-permute-done | bytes 131104 | tf_op jit(solution)/shard_map/ppermute | solution.py:24
  74.1 3.4 %collective-permute-start.14 = (f32[256,128]{1,0:T(8,128)S(1)}, f32[256,128]{1,0:T(8,128)S(1)}, u32[]{:S(2)}, u32[]{:S(2)}) collective-permute-start(f32[256,128]{1,0:T(8,128)S(1)} %constant_dynamic-slice_fusion.12), channel_id=1, source_target_pairs={{0,1},{1,0},{2,3},{3,2},{4,5},{5,4},{6,7},{7,6},{8,9},{9,8},{10,11... | collective-permute-start | bytes 393224 | tf_op jit(solution)/shard_map/ppermute | solution.py:43
  78.6 5.6 %collective-permute-start.16 = (f32[256,128]{1,0:T(8,128)S(1)}, f32[256,128]{1,0:T(8,128)}, u32[]{:S(2)}, u32[]{:S(2)}) collective-permute-start(f32[256,128]{1,0:T(8,128)S(1)} %dynamic-slice_add_fusion.8), channel_id=1, source_target_pairs={{0,4},{1,5},{2,6},{3,7},{4,0},{5,1},{6,2},{7,3},{8,12},{9,13},{10,... | collective-permute-start | bytes 393224 | tf_op jit(solution)/shard_map/ppermute | solution.py:34
  85.9 4.6 %collective-permute-done.16 = f32[256,128]{1,0:T(8,128)} collective-permute-done((f32[256,128]{1,0:T(8,128)S(1)}, f32[256,128]{1,0:T(8,128)}, u32[]{:S(2)}, u32[]{:S(2)}) %collective-permute-start.16) | collective-permute-done | bytes 131104 | tf_op jit(solution)/shard_map/ppermute | solution.py:34
  90.5 2.3 collective-permute-done.17
  97.1 6.7 %collective-permute-done.19 = bf16[256,256]{0,1:T(8,128)(2,1)S(1)} collective-permute-done((bf16[256,256]{0,1:T(8,128)(2,1)S(1)}, bf16[256,256]{0,1:T(8,128)(2,1)S(1)}, u32[]{:S(2)}, u32[]{:S(2)}) %collective-permute-start.19) | collective-permute-done | bytes 131104 | tf_op jit(solution)/shard_map/ppermute | solution.py:24
  108.8 4.5 %collective-permute-start.22 = (f32[256,128]{1,0:T(8,128)S(1)}, f32[256,128]{1,0:T(8,128)S(1)}, u32[]{:S(2)}, u32[]{:S(2)}) collective-permute-start(f32[256,128]{1,0:T(8,128)S(1)} %dynamic-slice_add_fusion.7), channel_id=1, source_target_pairs={{0,4},{1,5},{2,6},{3,7},{4,0},{5,1},{6,2},{7,3},{8,12},{9,13},{10,... | collective-permute-start | bytes 393224 | tf_op jit(solution)/shard_map/ppermute | solution.py:34
  115.2 4.6 %collective-permute-done.22 = f32[256,128]{1,0:T(8,128)S(1)} collective-permute-done((f32[256,128]{1,0:T(8,128)S(1)}, f32[256,128]{1,0:T(8,128)S(1)}, u32[]{:S(2)}, u32[]{:S(2)}) %collective-permute-start.22) | collective-permute-done | bytes 131104 | tf_op jit(solution)/shard_map/ppermute | solution.py:34
  119.8 2.2 collective-permute-done.23
  123.8 2.9 collective-permute-start.25
  130.0 2.6 collective-permute-done.25
  139.7 2.6 collective-permute-start.30
  142.3 2.5 collective-permute-done.35
  145.0 3.0 collective-permute-start.36
  149.9 9.0 %collective-permute-start.31 = (f32[256,128]{1,0:T(8,128)S(1)}, f32[256,128]{1,0:T(8,128)S(1)}, u32[]{:S(2)}, u32[]{:S(2)}) collective-permute-start(f32[256,128]{1,0:T(8,128)S(1)} %add_add_fusion), channel_id=1, source_target_pairs={{0,64},{64,0},{128,192},{192,128},{1,65},{65,1},{129,193},{193,129... | collective-permute-start | bytes 393224 | tf_op jit(solution)/shard_map/ppermute | solution.py:34
  161.0 2.7 collective-permute-start.33
  165.9 2.7 collective-permute-start.38
  171.3 2.6 collective-permute-done.38
  175.9 2.3 bitcast_convert_fusion.1
  180.6 7.0 %collective-permute-done.41 = bf16[256,256]{0,1:T(8,128)(2,1)S(1)} collective-permute-done((bf16[256,256]{0,1:T(8,128)(2,1)S(1)}, bf16[256,256]{0,1:T(8,128)(2,1)S(1)}, u32[]{:S(2)}, u32[]{:S(2)}) %collective-permute-start.41) | collective-permute-done | bytes 131104 | tf_op jit(solution)/shard_map/ppermute | solution.py:24
  192.5 6.5 %collective-permute-start.44 = (f32[256,128]{0,1:T(8,128)S(1)}, f32[256,128]{0,1:T(8,128)}, u32[]{:S(2)}, u32[]{:S(2)}) collective-permute-start(f32[256,128]{0,1:T(8,128)S(1)} %dynamic-slice_add_fusion.4), channel_id=1, source_target_pairs={{0,4},{1,5},{2,6},{3,7},{4,0},{5,1},{6,2},{7,3},{8,12},{9,13},{10,... | collective-permute-start | bytes 393224 | tf_op jit(solution)/shard_map/ppermute | solution.py:34
  201.5 3.9 %collective-permute-done.44 = f32[256,128]{0,1:T(8,128)} collective-permute-done((f32[256,128]{0,1:T(8,128)S(1)}, f32[256,128]{0,1:T(8,128)}, u32[]{:S(2)}, u32[]{:S(2)}) %collective-permute-start.44) | collective-permute-done | bytes 131104 | tf_op jit(solution)/shard_map/ppermute | solution.py:34
  205.5 2.2 collective-permute-done.45
  211.1 7.1 %collective-permute-done.47 = bf16[256,256]{0,1:T(8,128)(2,1)S(1)} collective-permute-done((bf16[256,256]{0,1:T(8,128)(2,1)S(1)}, bf16[256,256]{0,1:T(8,128)(2,1)S(1)}, u32[]{:S(2)}, u32[]{:S(2)}) %collective-permute-start.47) | collective-permute-done | bytes 131104 | tf_op jit(solution)/shard_map/ppermute | solution.py:24
  221.7 5.4 %collective-permute-start.50 = (f32[256,128]{0,1:T(8,128)S(1)}, f32[256,128]{0,1:T(8,128)S(1)}, u32[]{:S(2)}, u32[]{:S(2)}) collective-permute-start(f32[256,128]{0,1:T(8,128)S(1)} %dynamic-slice_add_fusion.3), channel_id=1, source_target_pairs={{0,4},{1,5},{2,6},{3,7},{4,0},{5,1},{6,2},{7,3},{8,12},{9,13},{10,... | collective-permute-start | bytes 393224 | tf_op jit(solution)/shard_map/ppermute | solution.py:34
  227.1 6.4 %collective-permute-done.50 = f32[256,128]{0,1:T(8,128)S(1)} collective-permute-done((f32[256,128]{0,1:T(8,128)S(1)}, f32[256,128]{0,1:T(8,128)S(1)}, u32[]{:S(2)}, u32[]{:S(2)}) %collective-permute-start.50) | collective-permute-done | bytes 131104 | tf_op jit(solution)/shard_map/ppermute | solution.py:34
  233.5 2.2 collective-permute-done.51
  237.7 6.9 %collective-permute-done.53 = bf16[256,256]{0,1:T(8,128)(2,1)S(1)} collective-permute-done((bf16[256,256]{0,1:T(8,128)(2,1)S(1)}, bf16[256,256]{0,1:T(8,128)(2,1)S(1)}, u32[]{:S(2)}, u32[]{:S(2)}) %collective-permute-start.53) | collective-permute-done | bytes 131104 | tf_op jit(solution)/shard_map/ppermute | solution.py:24
  248.4 6.4 %collective-permute-start.56 = (f32[256,128]{0,1:T(8,128)S(1)}, f32[256,128]{0,1:T(8,128)S(1)}, u32[]{:S(2)}, u32[]{:S(2)}) collective-permute-start(f32[256,128]{0,1:T(8,128)S(1)} %dynamic-slice_add_fusion.2), channel_id=1, source_target_pairs={{0,4},{1,5},{2,6},{3,7},{4,0},{5,1},{6,2},{7,3},{8,12},{9,13},{10,... | collective-permute-start | bytes 393224 | tf_op jit(solution)/shard_map/ppermute | solution.py:34
  255.5 5.8 %collective-permute-done.56 = f32[256,128]{0,1:T(8,128)S(1)} collective-permute-done((f32[256,128]{0,1:T(8,128)S(1)}, f32[256,128]{0,1:T(8,128)S(1)}, u32[]{:S(2)}, u32[]{:S(2)}) %collective-permute-start.56) | collective-permute-done | bytes 131104 | tf_op jit(solution)/shard_map/ppermute | solution.py:34
  261.2 2.2 collective-permute-done.57
  265.8 6.9 %collective-permute-done.59 = bf16[256,256]{0,1:T(8,128)(2,1)S(1)} collective-permute-done((bf16[256,256]{0,1:T(8,128)(2,1)S(1)}, bf16[256,256]{0,1:T(8,128)(2,1)S(1)}, u32[]{:S(2)}, u32[]{:S(2)}) %collective-permute-start.59) | collective-permute-done | bytes 131104 | tf_op jit(solution)/shard_map/ppermute | solution.py:24
  273.4 2.2 collective-permute-start.60
  277.3 4.1 %collective-permute-start.62 = (f32[256,128]{0,1:T(8,128)}, f32[256,128]{0,1:T(8,128)}, u32[]{:S(2)}, u32[]{:S(2)}) collective-permute-start(f32[256,128]{0,1:T(8,128)} %dynamic-slice_add_fusion.1), channel_id=1, source_target_pairs={{0,4},{1,5},{2,6},{3,7},{4,0},{5,1},{6,2},{7,3},{8,12},{9,13},{10,... | collective-permute-start | bytes 393224 | tf_op jit(solution)/shard_map/ppermute | solution.py:34
  284.1 4.0 %collective-permute-done.62 = f32[256,128]{0,1:T(8,128)} collective-permute-done((f32[256,128]{0,1:T(8,128)}, f32[256,128]{0,1:T(8,128)}, u32[]{:S(2)}, u32[]{:S(2)}) %collective-permute-start.62) | collective-permute-done | bytes 131104 | tf_op jit(solution)/shard_map/ppermute | solution.py:34
  288.1 2.2 collective-permute-done.63
  294.1 6.6 %collective-permute-done.65 = bf16[256,256]{0,1:T(8,128)(2,1)S(1)} collective-permute-done((bf16[256,256]{0,1:T(8,128)(2,1)S(1)}, bf16[256,256]{0,1:T(8,128)(2,1)S(1)}, u32[]{:S(2)}, u32[]{:S(2)}) %collective-permute-start.65) | collective-permute-done | bytes 131104 | tf_op jit(solution)/shard_map/ppermute | solution.py:24
  303.2 3.5 %collective-permute-start.66 = (f32[256,128]{0,1:T(8,128)S(1)}, f32[256,128]{0,1:T(8,128)S(1)}, u32[]{:S(2)}, u32[]{:S(2)}) collective-permute-start(f32[256,128]{0,1:T(8,128)S(1)} %constant_dynamic-slice_fusion.4), channel_id=1, source_target_pairs={{0,1},{1,0},{2,3},{3,2},{4,5},{5,4},{6,7},{7,6},{8,9},{9,8},{10,11... | collective-permute-start | bytes 393224 | tf_op jit(solution)/shard_map/ppermute | solution.py:56
  307.9 4.5 %collective-permute-start.68 = (f32[256,32]{0,1:T(8,128)S(1)}, f32[256,32]{0,1:T(8,128)S(1)}, u32[]{:S(2)}, u32[]{:S(2)}) collective-permute-start(f32[256,32]{0,1:T(8,128)S(1)} %get-tuple-element.35), channel_id=1, source_target_pairs={{0,4},{1,5},{2,6},{3,7},{4,0},{5,1},{6,2},{7,3},{8,12},{9,13},{10,... | collective-permute-start | bytes 98312 | tf_op jit(solution)/shard_map/ppermute | solution.py:62
  314.6 2.9 collective-permute-done.69
  (265 shorter events, 104.3 us)
Async XLA Ops:
  5.4 12.3 %collective-permute-start.1 = (bf16[256,256]{0,1:T(8,128)(2,1)S(1)}, bf16[256,256]{0,1:T(8,128)(2,1)S(1)}, u32[]{:S(2)}, u32[]{:S(2)}) collective-permute-start(bf16[256,256]{0,1:T(8,128)(2,1)S(1)} %pad_maximum_fusion.1), channel_id=1, source_target_pairs={{0,32},{1,24},{2,40},{6,16},{3,48},{7,8},{4,56},{5,0},{9,41},{8,33... | collective-permute-start | bytes 393224 | tf_op jit(solution)/shard_map/ppermute | solution.py:24
  19.5 8.4 %collective-permute-start.3 = (f32[256,128]{1,0:T(8,128)S(1)}, f32[256,128]{1,0:T(8,128)S(1)}, u32[]{:S(2)}, u32[]{:S(2)}) collective-permute-start(f32[256,128]{1,0:T(8,128)S(1)} %dynamic-slice_add_fusion.10), channel_id=1, source_target_pairs={{0,2},{1,3},{2,0},{3,1},{4,6},{5,7},{6,4},{7,5},{8,10},{9,11},{10,... | collective-permute-start | bytes 393224 | tf_op jit(solution)/shard_map/ppermute | solution.py:34
  19.6 14.0 %collective-permute-start.4 = (f32[256,128]{1,0:T(8,128)S(1)}, f32[256,128]{1,0:T(8,128)S(1)}, u32[]{:S(2)}, u32[]{:S(2)}) collective-permute-start(f32[256,128]{1,0:T(8,128)S(1)} %dynamic-slice_add_fusion.10), channel_id=1, source_target_pairs={{0,4},{1,5},{2,6},{3,7},{4,0},{5,1},{6,2},{7,3},{8,12},{9,13},{10,... | collective-permute-start | bytes 393224 | tf_op jit(solution)/shard_map/ppermute | solution.py:34
  27.1 8.7 %collective-permute-start.5 = (f32[256,128]{1,0:T(8,128)S(1)}, f32[256,128]{1,0:T(8,128)S(1)}, u32[]{:S(2)}, u32[]{:S(2)}) collective-permute-start(f32[256,128]{1,0:T(8,128)S(1)} %dynamic-slice_add_fusion.10), channel_id=1, source_target_pairs={{0,6},{1,7},{2,4},{3,5},{4,2},{5,3},{6,0},{7,1},{8,14},{9,15},{10,... | collective-permute-start | bytes 393224 | tf_op jit(solution)/shard_map/ppermute | solution.py:34
  38.9 7.3 %collective-permute-start.7 = (bf16[256,256]{0,1:T(8,128)(2,1)S(1)}, bf16[256,256]{0,1:T(8,128)(2,1)S(1)}, u32[]{:S(2)}, u32[]{:S(2)}) collective-permute-start(bf16[256,256]{0,1:T(8,128)(2,1)S(1)} %pad_maximum_fusion.2), channel_id=1, source_target_pairs={{0,32},{1,24},{2,40},{6,16},{3,48},{7,8},{4,56},{5,0},{9,41},{8,33... | collective-permute-start | bytes 393224 | tf_op jit(solution)/shard_map/ppermute | solution.py:24
  50.1 7.5 %collective-permute-start.10 = (f32[256,128]{1,0:T(8,128)S(1)}, f32[256,128]{1,0:T(8,128)S(1)}, u32[]{:S(2)}, u32[]{:S(2)}) collective-permute-start(f32[256,128]{1,0:T(8,128)S(1)} %dynamic-slice_add_fusion.9), channel_id=1, source_target_pairs={{0,4},{1,5},{2,6},{3,7},{4,0},{5,1},{6,2},{7,3},{8,12},{9,13},{10,... | collective-permute-start | bytes 393224 | tf_op jit(solution)/shard_map/ppermute | solution.py:34
  50.5 9.9 %collective-permute-start.11 = (f32[256,128]{1,0:T(8,128)S(1)}, f32[256,128]{1,0:T(8,128)S(1)}, u32[]{:S(2)}, u32[]{:S(2)}) collective-permute-start(f32[256,128]{1,0:T(8,128)S(1)} %dynamic-slice_add_fusion.9), channel_id=1, source_target_pairs={{0,6},{1,7},{2,4},{3,5},{4,2},{5,3},{6,0},{7,1},{8,14},{9,15},{10,... | collective-permute-start | bytes 393224 | tf_op jit(solution)/shard_map/ppermute | solution.py:34
  54.6 7.1 %collective-permute-start.9 = (f32[256,128]{1,0:T(8,128)S(1)}, f32[256,128]{1,0:T(8,128)S(1)}, u32[]{:S(2)}, u32[]{:S(2)}) collective-permute-start(f32[256,128]{1,0:T(8,128)S(1)} %dynamic-slice_add_fusion.9), channel_id=1, source_target_pairs={{0,2},{1,3},{2,0},{3,1},{4,6},{5,7},{6,4},{7,5},{8,10},{9,11},{10,... | collective-permute-start | bytes 393224 | tf_op jit(solution)/shard_map/ppermute | solution.py:34
  64.8 7.8 %collective-permute-start.13 = (bf16[256,256]{0,1:T(8,128)(2,1)S(1)}, bf16[256,256]{0,1:T(8,128)(2,1)S(1)}, u32[]{:S(2)}, u32[]{:S(2)}) collective-permute-start(bf16[256,256]{0,1:T(8,128)(2,1)S(1)} %pad_maximum_fusion.3), channel_id=1, source_target_pairs={{0,32},{1,24},{2,40},{6,16},{3,48},{7,8},{4,56},{5,0},{9,41},{8,33... | collective-permute-start | bytes 393224 | tf_op jit(solution)/shard_map/ppermute | solution.py:24
  78.5 7.4 %collective-permute-start.15 = (f32[256,128]{1,0:T(8,128)S(1)}, f32[256,128]{1,0:T(8,128)}, u32[]{:S(2)}, u32[]{:S(2)}) collective-permute-start(f32[256,128]{1,0:T(8,128)S(1)} %dynamic-slice_add_fusion.8), channel_id=1, source_target_pairs={{0,2},{1,3},{2,0},{3,1},{4,6},{5,7},{6,4},{7,5},{8,10},{9,11},{10,... | collective-permute-start | bytes 393224 | tf_op jit(solution)/shard_map/ppermute | solution.py:34
  78.6 11.9 %collective-permute-start.16 = (f32[256,128]{1,0:T(8,128)S(1)}, f32[256,128]{1,0:T(8,128)}, u32[]{:S(2)}, u32[]{:S(2)}) collective-permute-start(f32[256,128]{1,0:T(8,128)S(1)} %dynamic-slice_add_fusion.8), channel_id=1, source_target_pairs={{0,4},{1,5},{2,6},{3,7},{4,0},{5,1},{6,2},{7,3},{8,12},{9,13},{10,... | collective-permute-start | bytes 393224 | tf_op jit(solution)/shard_map/ppermute | solution.py:34
  84.2 8.7 %collective-permute-start.17 = (f32[256,128]{1,0:T(8,128)S(1)}, f32[256,128]{1,0:T(8,128)}, u32[]{:S(2)}, u32[]{:S(2)}) collective-permute-start(f32[256,128]{1,0:T(8,128)S(1)} %dynamic-slice_add_fusion.8), channel_id=1, source_target_pairs={{0,6},{1,7},{2,4},{3,5},{4,2},{5,3},{6,0},{7,1},{8,14},{9,15},{10,... | collective-permute-start | bytes 393224 | tf_op jit(solution)/shard_map/ppermute | solution.py:34
  96.2 7.6 %collective-permute-start.19 = (bf16[256,256]{0,1:T(8,128)(2,1)S(1)}, bf16[256,256]{0,1:T(8,128)(2,1)S(1)}, u32[]{:S(2)}, u32[]{:S(2)}) collective-permute-start(bf16[256,256]{0,1:T(8,128)(2,1)S(1)} %pad_maximum_fusion.4), channel_id=1, source_target_pairs={{0,32},{1,24},{2,40},{6,16},{3,48},{7,8},{4,56},{5,0},{9,41},{8,33... | collective-permute-start | bytes 393224 | tf_op jit(solution)/shard_map/ppermute | solution.py:24
  108.7 6.5 %collective-permute-start.21 = (f32[256,128]{1,0:T(8,128)S(1)}, f32[256,128]{1,0:T(8,128)S(1)}, u32[]{:S(2)}, u32[]{:S(2)}) collective-permute-start(f32[256,128]{1,0:T(8,128)S(1)} %dynamic-slice_add_fusion.7), channel_id=1, source_target_pairs={{0,2},{1,3},{2,0},{3,1},{4,6},{5,7},{6,4},{7,5},{8,10},{9,11},{10,... | collective-permute-start | bytes 393224 | tf_op jit(solution)/shard_map/ppermute | solution.py:34
  108.8 11.0 %collective-permute-start.22 = (f32[256,128]{1,0:T(8,128)S(1)}, f32[256,128]{1,0:T(8,128)S(1)}, u32[]{:S(2)}, u32[]{:S(2)}) collective-permute-start(f32[256,128]{1,0:T(8,128)S(1)} %dynamic-slice_add_fusion.7), channel_id=1, source_target_pairs={{0,4},{1,5},{2,6},{3,7},{4,0},{5,1},{6,2},{7,3},{8,12},{9,13},{10,... | collective-permute-start | bytes 393224 | tf_op jit(solution)/shard_map/ppermute | solution.py:34
  113.4 8.7 %collective-permute-start.23 = (f32[256,128]{1,0:T(8,128)S(1)}, f32[256,128]{1,0:T(8,128)S(1)}, u32[]{:S(2)}, u32[]{:S(2)}) collective-permute-start(f32[256,128]{1,0:T(8,128)S(1)} %dynamic-slice_add_fusion.7), channel_id=1, source_target_pairs={{0,6},{1,7},{2,4},{3,5},{4,2},{5,3},{6,0},{7,1},{8,14},{9,15},{10,... | collective-permute-start | bytes 393224 | tf_op jit(solution)/shard_map/ppermute | solution.py:34
  122.1 7.9 %collective-permute-start.24 = (f32[256,128]{1,0:T(8,128)S(1)}, f32[256,128]{1,0:T(8,128)}, u32[]{:S(2)}, u32[]{:S(2)}) collective-permute-start(f32[256,128]{1,0:T(8,128)S(1)} %add_add_fusion.1), channel_id=1, source_target_pairs={{0,64},{64,0},{128,192},{192,128},{1,65},{65,1},{129,193},{193,129... | collective-permute-start | bytes 393224 | tf_op jit(solution)/shard_map/ppermute | solution.py:34
  123.8 8.8 %collective-permute-start.25 = (f32[256,128]{1,0:T(8,128)S(1)}, f32[256,128]{1,0:T(8,128)}, u32[]{:S(2)}, u32[]{:S(2)}) collective-permute-start(f32[256,128]{1,0:T(8,128)S(1)} %add_add_fusion.1), channel_id=1, source_target_pairs={{0,128},{64,192},{128,0},{192,64},{1,129},{65,193},{129,1},{193,65... | collective-permute-start | bytes 393224 | tf_op jit(solution)/shard_map/ppermute | solution.py:34
  126.7 7.9 %collective-permute-start.26 = (f32[256,128]{1,0:T(8,128)S(1)}, f32[256,128]{1,0:T(8,128)}, u32[]{:S(2)}, u32[]{:S(2)}) collective-permute-start(f32[256,128]{1,0:T(8,128)S(1)} %add_add_fusion.1), channel_id=1, source_target_pairs={{0,192},{64,128},{128,64},{192,0},{1,193},{65,129},{129,65},{193,1... | collective-permute-start | bytes 393224 | tf_op jit(solution)/shard_map/ppermute | solution.py:34
  137.2 7.6 %collective-permute-start.35 = (bf16[256,256]{0,1:T(8,128)(2,1)S(1)}, bf16[256,256]{0,1:T(8,128)(2,1)S(1)}, u32[]{:S(2)}, u32[]{:S(2)}) collective-permute-start(bf16[256,256]{0,1:T(8,128)(2,1)S(1)} %pad_maximum_fusion.5), channel_id=1, source_target_pairs={{0,32},{1,24},{2,40},{6,16},{3,48},{7,8},{4,56},{5,0},{9,41},{8,33... | collective-permute-start | bytes 393224 | tf_op jit(solution)/shard_map/ppermute | solution.py:24
  137.5 10.6 %collective-permute-start.28 = (f32[256,128]{1,0:T(8,128)S(1)}, f32[256,128]{1,0:T(8,128)S(1)}, u32[]{:S(2)}, u32[]{:S(2)}) collective-permute-start(f32[256,128]{1,0:T(8,128)S(1)} %dynamic-slice_add_fusion.6), channel_id=1, source_target_pairs={{0,2},{1,3},{2,0},{3,1},{4,6},{5,7},{6,4},{7,5},{8,10},{9,11},{10,... | collective-permute-start | bytes 393224 | tf_op jit(solution)/shard_map/ppermute | solution.py:34
  137.6 10.5 %collective-permute-start.29 = (f32[256,128]{1,0:T(8,128)S(1)}, f32[256,128]{1,0:T(8,128)S(1)}, u32[]{:S(2)}, u32[]{:S(2)}) collective-permute-start(f32[256,128]{1,0:T(8,128)S(1)} %dynamic-slice_add_fusion.6), channel_id=1, source_target_pairs={{0,4},{1,5},{2,6},{3,7},{4,0},{5,1},{6,2},{7,3},{8,12},{9,13},{10,... | collective-permute-start | bytes 393224 | tf_op jit(solution)/shard_map/ppermute | solution.py:34
  139.7 10.2 %collective-permute-start.30 = (f32[256,128]{1,0:T(8,128)S(1)}, f32[256,128]{1,0:T(8,128)S(1)}, u32[]{:S(2)}, u32[]{:S(2)}) collective-permute-start(f32[256,128]{1,0:T(8,128)S(1)} %dynamic-slice_add_fusion.6), channel_id=1, source_target_pairs={{0,6},{1,7},{2,4},{3,5},{4,2},{5,3},{6,0},{7,1},{8,14},{9,15},{10,... | collective-permute-start | bytes 393224 | tf_op jit(solution)/shard_map/ppermute | solution.py:34
  145.0 18.6 %collective-permute-start.36 = (f32[256,128]{1,0:T(8,128)S(1)}, f32[256,128]{1,0:T(8,128)S(1)}, u32[]{:S(2)}, u32[]{:S(2)}) collective-permute-start(f32[256,128]{1,0:T(8,128)S(1)} %constant_dynamic-slice_fusion.9), channel_id=1, source_target_pairs={{0,1},{1,0},{2,3},{3,2},{4,5},{5,4},{6,7},{7,6},{8,9},{9,8},{10,11... | collective-permute-start | bytes 393224 | tf_op jit(solution)/shard_map/ppermute | solution.py:43
  149.9 18.7 %collective-permute-start.31 = (f32[256,128]{1,0:T(8,128)S(1)}, f32[256,128]{1,0:T(8,128)S(1)}, u32[]{:S(2)}, u32[]{:S(2)}) collective-permute-start(f32[256,128]{1,0:T(8,128)S(1)} %add_add_fusion), channel_id=1, source_target_pairs={{0,64},{64,0},{128,192},{192,128},{1,65},{65,1},{129,193},{193,129... | collective-permute-start | bytes 393224 | tf_op jit(solution)/shard_map/ppermute | solution.py:34
  158.9 12.4 %collective-permute-start.32 = (f32[256,128]{1,0:T(8,128)S(1)}, f32[256,128]{1,0:T(8,128)}, u32[]{:S(2)}, u32[]{:S(2)}) collective-permute-start(f32[256,128]{1,0:T(8,128)S(1)} %add_add_fusion), channel_id=1, source_target_pairs={{0,128},{64,192},{128,0},{192,64},{1,129},{65,193},{129,1},{193,65... | collective-permute-start | bytes 393224 | tf_op jit(solution)/shard_map/ppermute | solution.py:34
  161.0 10.4 %collective-permute-start.33 = (f32[256,128]{1,0:T(8,128)S(1)}, f32[256,128]{1,0:T(8,128)}, u32[]{:S(2)}, u32[]{:S(2)}) collective-permute-start(f32[256,128]{1,0:T(8,128)S(1)} %add_add_fusion), channel_id=1, source_target_pairs={{0,192},{64,128},{128,64},{192,0},{1,193},{65,129},{129,65},{193,1... | collective-permute-start | bytes 393224 | tf_op jit(solution)/shard_map/ppermute | solution.py:34
  164.3 7.0 %collective-permute-start.37 = (f32[256,128]{1,0:T(8,128)}, f32[256,128]{1,0:T(8,128)}, u32[]{:S(2)}, u32[]{:S(2)}) collective-permute-start(f32[256,128]{1,0:T(8,128)} %dynamic-slice_add_fusion.5), channel_id=1, source_target_pairs={{0,2},{1,3},{2,0},{3,1},{4,6},{5,7},{6,4},{7,5},{8,10},{9,11},{10,... | collective-permute-start | bytes 393224 | tf_op jit(solution)/shard_map/ppermute | solution.py:34
  165.9 8.1 %collective-permute-start.38 = (f32[256,128]{1,0:T(8,128)}, f32[256,128]{1,0:T(8,128)}, u32[]{:S(2)}, u32[]{:S(2)}) collective-permute-start(f32[256,128]{1,0:T(8,128)} %dynamic-slice_add_fusion.5), channel_id=1, source_target_pairs={{0,4},{1,5},{2,6},{3,7},{4,0},{5,1},{6,2},{7,3},{8,12},{9,13},{10,... | collective-permute-start | bytes 393224 | tf_op jit(solution)/shard_map/ppermute | solution.py:34
  169.2 6.7 %collective-permute-start.39 = (f32[256,128]{1,0:T(8,128)}, f32[256,128]{1,0:T(8,128)}, u32[]{:S(2)}, u32[]{:S(2)}) collective-permute-start(f32[256,128]{1,0:T(8,128)} %dynamic-slice_add_fusion.5), channel_id=1, source_target_pairs={{0,6},{1,7},{2,4},{3,5},{4,2},{5,3},{6,0},{7,1},{8,14},{9,15},{10,... | collective-permute-start | bytes 393224 | tf_op jit(solution)/shard_map/ppermute | solution.py:34
  180.5 7.1 %collective-permute-start.41 = (bf16[256,256]{0,1:T(8,128)(2,1)S(1)}, bf16[256,256]{0,1:T(8,128)(2,1)S(1)}, u32[]{:S(2)}, u32[]{:S(2)}) collective-permute-start(bf16[256,256]{0,1:T(8,128)(2,1)S(1)} %pad_maximum_fusion.6), channel_id=1, source_target_pairs={{0,32},{1,24},{2,40},{6,16},{3,48},{7,8},{4,56},{5,0},{9,41},{8,33... | collective-permute-start | bytes 393224 | tf_op jit(solution)/shard_map/ppermute | solution.py:24
  191.1 10.5 %collective-permute-start.43 = (f32[256,128]{0,1:T(8,128)S(1)}, f32[256,128]{0,1:T(8,128)}, u32[]{:S(2)}, u32[]{:S(2)}) collective-permute-start(f32[256,128]{0,1:T(8,128)S(1)} %dynamic-slice_add_fusion.4), channel_id=1, source_target_pairs={{0,2},{1,3},{2,0},{3,1},{4,6},{5,7},{6,4},{7,5},{8,10},{9,11},{10,... | collective-permute-start | bytes 393224 | tf_op jit(solution)/shard_map/ppermute | solution.py:34
  192.5 13.0 %collective-permute-start.44 = (f32[256,128]{0,1:T(8,128)S(1)}, f32[256,128]{0,1:T(8,128)}, u32[]{:S(2)}, u32[]{:S(2)}) collective-permute-start(f32[256,128]{0,1:T(8,128)S(1)} %dynamic-slice_add_fusion.4), channel_id=1, source_target_pairs={{0,4},{1,5},{2,6},{3,7},{4,0},{5,1},{6,2},{7,3},{8,12},{9,13},{10,... | collective-permute-start | bytes 393224 | tf_op jit(solution)/shard_map/ppermute | solution.py:34
  198.9 8.8 %collective-permute-start.45 = (f32[256,128]{0,1:T(8,128)S(1)}, f32[256,128]{0,1:T(8,128)}, u32[]{:S(2)}, u32[]{:S(2)}) collective-permute-start(f32[256,128]{0,1:T(8,128)S(1)} %dynamic-slice_add_fusion.4), channel_id=1, source_target_pairs={{0,6},{1,7},{2,4},{3,5},{4,2},{5,3},{6,0},{7,1},{8,14},{9,15},{10,... | collective-permute-start | bytes 393224 | tf_op jit(solution)/shard_map/ppermute | solution.py:34
  211.0 7.3 %collective-permute-start.47 = (bf16[256,256]{0,1:T(8,128)(2,1)S(1)}, bf16[256,256]{0,1:T(8,128)(2,1)S(1)}, u32[]{:S(2)}, u32[]{:S(2)}) collective-permute-start(bf16[256,256]{0,1:T(8,128)(2,1)S(1)} %pad_maximum_fusion.7), channel_id=1, source_target_pairs={{0,32},{1,24},{2,40},{6,16},{3,48},{7,8},{4,56},{5,0},{9,41},{8,33... | collective-permute-start | bytes 393224 | tf_op jit(solution)/shard_map/ppermute | solution.py:24
  220.0 7.1 %collective-permute-start.49 = (f32[256,128]{0,1:T(8,128)S(1)}, f32[256,128]{0,1:T(8,128)S(1)}, u32[]{:S(2)}, u32[]{:S(2)}) collective-permute-start(f32[256,128]{0,1:T(8,128)S(1)} %dynamic-slice_add_fusion.3), channel_id=1, source_target_pairs={{0,2},{1,3},{2,0},{3,1},{4,6},{5,7},{6,4},{7,5},{8,10},{9,11},{10,... | collective-permute-start | bytes 393224 | tf_op jit(solution)/shard_map/ppermute | solution.py:34
  221.7 11.8 %collective-permute-start.50 = (f32[256,128]{0,1:T(8,128)S(1)}, f32[256,128]{0,1:T(8,128)S(1)}, u32[]{:S(2)}, u32[]{:S(2)}) collective-permute-start(f32[256,128]{0,1:T(8,128)S(1)} %dynamic-slice_add_fusion.3), channel_id=1, source_target_pairs={{0,4},{1,5},{2,6},{3,7},{4,0},{5,1},{6,2},{7,3},{8,12},{9,13},{10,... | collective-permute-start | bytes 393224 | tf_op jit(solution)/shard_map/ppermute | solution.py:34
  227.1 8.7 %collective-permute-start.51 = (f32[256,128]{0,1:T(8,128)S(1)}, f32[256,128]{0,1:T(8,128)S(1)}, u32[]{:S(2)}, u32[]{:S(2)}) collective-permute-start(f32[256,128]{0,1:T(8,128)S(1)} %dynamic-slice_add_fusion.3), channel_id=1, source_target_pairs={{0,6},{1,7},{2,4},{3,5},{4,2},{5,3},{6,0},{7,1},{8,14},{9,15},{10,... | collective-permute-start | bytes 393224 | tf_op jit(solution)/shard_map/ppermute | solution.py:34
  237.4 7.3 %collective-permute-start.53 = (bf16[256,256]{0,1:T(8,128)(2,1)S(1)}, bf16[256,256]{0,1:T(8,128)(2,1)S(1)}, u32[]{:S(2)}, u32[]{:S(2)}) collective-permute-start(bf16[256,256]{0,1:T(8,128)(2,1)S(1)} %pad_maximum_fusion.8), channel_id=1, source_target_pairs={{0,32},{1,24},{2,40},{6,16},{3,48},{7,8},{4,56},{5,0},{9,41},{8,33... | collective-permute-start | bytes 393224 | tf_op jit(solution)/shard_map/ppermute | solution.py:24
  246.5 9.0 %collective-permute-start.55 = (f32[256,128]{0,1:T(8,128)S(1)}, f32[256,128]{0,1:T(8,128)S(1)}, u32[]{:S(2)}, u32[]{:S(2)}) collective-permute-start(f32[256,128]{0,1:T(8,128)S(1)} %dynamic-slice_add_fusion.2), channel_id=1, source_target_pairs={{0,2},{1,3},{2,0},{3,1},{4,6},{5,7},{6,4},{7,5},{8,10},{9,11},{10,... | collective-permute-start | bytes 393224 | tf_op jit(solution)/shard_map/ppermute | solution.py:34
  248.4 12.8 %collective-permute-start.56 = (f32[256,128]{0,1:T(8,128)S(1)}, f32[256,128]{0,1:T(8,128)S(1)}, u32[]{:S(2)}, u32[]{:S(2)}) collective-permute-start(f32[256,128]{0,1:T(8,128)S(1)} %dynamic-slice_add_fusion.2), channel_id=1, source_target_pairs={{0,4},{1,5},{2,6},{3,7},{4,0},{5,1},{6,2},{7,3},{8,12},{9,13},{10,... | collective-permute-start | bytes 393224 | tf_op jit(solution)/shard_map/ppermute | solution.py:34
  254.8 8.7 %collective-permute-start.57 = (f32[256,128]{0,1:T(8,128)S(1)}, f32[256,128]{0,1:T(8,128)S(1)}, u32[]{:S(2)}, u32[]{:S(2)}) collective-permute-start(f32[256,128]{0,1:T(8,128)S(1)} %dynamic-slice_add_fusion.2), channel_id=1, source_target_pairs={{0,6},{1,7},{2,4},{3,5},{4,2},{5,3},{6,0},{7,1},{8,14},{9,15},{10,... | collective-permute-start | bytes 393224 | tf_op jit(solution)/shard_map/ppermute | solution.py:34
  265.1 7.6 %collective-permute-start.59 = (bf16[256,256]{0,1:T(8,128)(2,1)S(1)}, bf16[256,256]{0,1:T(8,128)(2,1)S(1)}, u32[]{:S(2)}, u32[]{:S(2)}) collective-permute-start(bf16[256,256]{0,1:T(8,128)(2,1)S(1)} %pad_maximum_fusion.9), channel_id=1, source_target_pairs={{0,32},{1,24},{2,40},{6,16},{3,48},{7,8},{4,56},{5,0},{9,41},{8,33... | collective-permute-start | bytes 393224 | tf_op jit(solution)/shard_map/ppermute | solution.py:24
  277.3 6.8 %collective-permute-start.61 = (f32[256,128]{0,1:T(8,128)}, f32[256,128]{0,1:T(8,128)}, u32[]{:S(2)}, u32[]{:S(2)}) collective-permute-start(f32[256,128]{0,1:T(8,128)} %dynamic-slice_add_fusion.1), channel_id=1, source_target_pairs={{0,2},{1,3},{2,0},{3,1},{4,6},{5,7},{6,4},{7,5},{8,10},{9,11},{10,... | collective-permute-start | bytes 393224 | tf_op jit(solution)/shard_map/ppermute | solution.py:34
  277.3 10.9 %collective-permute-start.62 = (f32[256,128]{0,1:T(8,128)}, f32[256,128]{0,1:T(8,128)}, u32[]{:S(2)}, u32[]{:S(2)}) collective-permute-start(f32[256,128]{0,1:T(8,128)} %dynamic-slice_add_fusion.1), channel_id=1, source_target_pairs={{0,4},{1,5},{2,6},{3,7},{4,0},{5,1},{6,2},{7,3},{8,12},{9,13},{10,... | collective-permute-start | bytes 393224 | tf_op jit(solution)/shard_map/ppermute | solution.py:34
  281.4 9.0 %collective-permute-start.63 = (f32[256,128]{0,1:T(8,128)}, f32[256,128]{0,1:T(8,128)}, u32[]{:S(2)}, u32[]{:S(2)}) collective-permute-start(f32[256,128]{0,1:T(8,128)} %dynamic-slice_add_fusion.1), channel_id=1, source_target_pairs={{0,6},{1,7},{2,4},{3,5},{4,2},{5,3},{6,0},{7,1},{8,14},{9,15},{10,... | collective-permute-start | bytes 393224 | tf_op jit(solution)/shard_map/ppermute | solution.py:34
  293.1 7.6 %collective-permute-start.65 = (bf16[256,256]{0,1:T(8,128)(2,1)S(1)}, bf16[256,256]{0,1:T(8,128)(2,1)S(1)}, u32[]{:S(2)}, u32[]{:S(2)}) collective-permute-start(bf16[256,256]{0,1:T(8,128)(2,1)S(1)} %pad_maximum_fusion.10), channel_id=1, source_target_pairs={{0,32},{1,24},{2,40},{6,16},{3,48},{7,8},{4,56},{5,0},{9,41},{8,33... | collective-permute-start | bytes 393224 | tf_op jit(solution)/shard_map/ppermute | solution.py:24
  307.9 6.7 %collective-permute-start.68 = (f32[256,32]{0,1:T(8,128)S(1)}, f32[256,32]{0,1:T(8,128)S(1)}, u32[]{:S(2)}, u32[]{:S(2)}) collective-permute-start(f32[256,32]{0,1:T(8,128)S(1)} %get-tuple-element.35), channel_id=1, source_target_pairs={{0,4},{1,5},{2,6},{3,7},{4,0},{5,1},{6,2},{7,3},{8,12},{9,13},{10,... | collective-permute-start | bytes 98312 | tf_op jit(solution)/shard_map/ppermute | solution.py:62
  (50 other events, 450.8 us)
